TPU v7x, 32 devices: a whole 2x2x4 slice. The times are simulated.
32 devices in a mesh: dp: 4 (over z), tensor: 8 (over y, x, core).
Axes of the slice: x: 2, y: 2, z: 4, core: 2. Of those that a mesh axis runs over, the one named last changes fastest.
Arguments:
- inputs: bfloat16 [4, 32, 4096], P(None, 'tensor', 'dp'), may hold values from -6 to 6
- norm_gain: float32 [4096], P('dp'), may hold values from 0.1 to 1.9
- w_gate: bfloat16 [4096, 28672], P('dp', 'tensor'), may hold values from -0.09375 to 0.09375
- w_up: bfloat16 [4096, 28672], P('dp', 'tensor'), may hold values from -0.09375 to 0.09375
- w_down: bfloat16 [28672, 4096], P('tensor', 'dp'), may hold values from -0.03125 to 0.03125
- d_output: bfloat16 [4, 32, 4096], P(None, 'tensor', 'dp'), may hold values from -0.75 to 0.75
- level_of_batch: int32 [4], replicated, may hold values from 0 to 3, each once
Outputs:
- outputs: bfloat16 [4, 32, 4096], P(None, 'tensor', 'dp')
- d_inputs: bfloat16 [4, 32, 4096], P(None, 'tensor', 'dp')
- d_gain: float32 [4096], P('dp')
- d_gate: bfloat16 [4096, 28672], P('dp', 'tensor')
- d_up: bfloat16 [4096, 28672], P('dp', 'tensor')
- d_down: bfloat16 [28672, 4096], P('tensor', 'dp')
- row_product: float32 [4, 32], P(None, 'tensor')
Inputs may be any that keep to these rules, and one draw needn't show every extreme that they name: `level_of_batch`: every level from 0 to 3 belongs to exactly one micro-batch.
All inputs are finite; a program needn't handle non-finite values.
Results may differ from a plain program's by a relative error of at most 0.02.
Values may be sent and summed in bfloat16 or wider, within the bound.
No kernel may reach another device: no remote copies, remote signals or barrier semaphores. Data moves between devices by JAX's collectives and lax.ppermute only.
A program may use at most 384 MiB of HBM per device.

v0:
```python
import jax
import jax.numpy as jnp
from jax import lax
from jax.sharding import PartitionSpec as P

epsilon = 1e-05
contract_cols = (((1,), (1,)), ((), ()))
contract_rows = (((0,), (0,)), ((), ()))


def local_terms(gate_sum, up_sum, back_sum, active_mask):
    sigmoid_gate = jax.nn.sigmoid(gate_sum)
    silu_gate = gate_sum * sigmoid_gate
    slope = sigmoid_gate * (1.0 + gate_sum * (1.0 - sigmoid_gate))
    hidden = (silu_gate * up_sum * active_mask).astype(jnp.bfloat16)
    gate_grad = (back_sum * up_sum * slope * active_mask).astype(jnp.bfloat16)
    up_grad = (back_sum * silu_gate * active_mask).astype(jnp.bfloat16)
    return (hidden, gate_grad, up_grad)


def per_device(inputs, norm_gain, w_gate, w_up, w_down, d_output, level_of_batch):
    groups = lax.axis_size("tensor")
    tensor_index = lax.axis_index("tensor")
    local_feat = w_gate.shape[0]
    local_cols = w_gate.shape[1]
    full_width = local_feat * lax.axis_size("dp")
    batches, local_rows, _ = inputs.shape
    both = jnp.concatenate([inputs, d_output], axis=0)
    both_all = lax.all_gather(both, "tensor", axis=1, tiled=True)
    inputs_all = both_all[:batches].astype(jnp.float32)
    grad_all = both_all[batches:]
    rows = inputs_all.shape[1]
    square_sum = lax.psum(jnp.sum(inputs_all * inputs_all, axis=2), "dp")
    row_scale_all = lax.rsqrt(square_sum / full_width + epsilon)
    normed_all = (inputs_all * row_scale_all[:, :, None] * norm_gain).astype(jnp.bfloat16)
    start = tensor_index * local_rows
    row_scale = lax.dynamic_slice_in_dim(row_scale_all, start, local_rows, axis=1)
    wide_inputs = inputs.astype(jnp.float32)

    flat_normed = normed_all.reshape(batches * rows, local_feat)
    flat_grad = grad_all.reshape(batches * rows, local_feat)
    gate_part = jnp.dot(flat_normed, w_gate, preferred_element_type=jnp.float32)
    up_part = jnp.dot(flat_normed, w_up, preferred_element_type=jnp.float32)
    back_part = lax.dot_general(
        flat_grad, w_down, contract_cols, preferred_element_type=jnp.float32
    )
    gate_sum, up_sum, back_sum = (
        lax.psum(gate_part.astype(jnp.bfloat16), "dp").astype(jnp.float32),
        lax.psum(up_part.astype(jnp.bfloat16), "dp").astype(jnp.float32),
        lax.psum(back_part.astype(jnp.bfloat16), "dp").astype(jnp.float32),
    )
    halvings = 3 - level_of_batch
    active = (tensor_index < jnp.right_shift(groups, halvings)).astype(jnp.float32)
    active_mask = jnp.repeat(active, rows)[:, None]
    hidden, gate_grad, up_grad = local_terms(gate_sum, up_sum, back_sum, active_mask)

    down_part = jnp.dot(hidden, w_down, preferred_element_type=jnp.float32)
    normed_part = lax.dot_general(
        gate_grad, w_gate, contract_cols, preferred_element_type=jnp.float32
    ) + lax.dot_general(up_grad, w_up, contract_cols, preferred_element_type=jnp.float32)
    stacked = jnp.stack([down_part, normed_part]).astype(jnp.bfloat16)
    stacked = stacked.reshape(2, batches, rows, local_feat)
    shares = lax.psum_scatter(stacked, "tensor", scatter_dimension=2, tiled=True).astype(
        jnp.float32
    )
    down_output = shares[0]
    normed_grad = shares[1]

    down_out = lax.dot_general(
        hidden, flat_grad, contract_rows, preferred_element_type=jnp.float32
    ).astype(jnp.bfloat16)
    gate_out = lax.dot_general(
        flat_normed, gate_grad, contract_rows, preferred_element_type=jnp.float32
    ).astype(jnp.bfloat16)
    up_out = lax.dot_general(
        flat_normed, up_grad, contract_rows, preferred_element_type=jnp.float32
    ).astype(jnp.bfloat16)

    wide_grad = d_output.astype(jnp.float32)
    weighted = norm_gain * normed_grad
    row_part = jnp.sum(weighted * wide_inputs, axis=2)
    gain_part = jnp.sum(normed_grad * wide_inputs * row_scale[:, :, None], axis=(0, 1))
    row_product = lax.psum(row_part, "dp")
    d_gain = lax.psum(gain_part, "tensor")
    outputs = (wide_inputs + down_output).astype(jnp.bfloat16)
    scale_cube = row_scale * row_scale * row_scale
    d_inputs = (
        wide_grad
        + row_scale[:, :, None] * weighted
        - wide_inputs * (scale_cube * row_product / full_width)[:, :, None]
    ).astype(jnp.bfloat16)
    return (outputs, d_inputs, d_gain, gate_out, up_out, down_out, row_product)


def solution(mesh):
    in_specs = (
        P(None, "tensor", "dp"),
        P("dp"),
        P("dp", "tensor"),
        P("dp", "tensor"),
        P("tensor", "dp"),
        P(None, "tensor", "dp"),
        P(),
    )
    out_specs = (
        P(None, "tensor", "dp"),
        P(None, "tensor", "dp"),
        P("dp"),
        P("dp", "tensor"),
        P("dp", "tensor"),
        P("tensor", "dp"),
        P(None, "tensor"),
    )
    return jax.shard_map(
        per_device, mesh=mesh, in_specs=in_specs, out_specs=out_specs, check_vma=False
    )
```

profile of v0, /device:TPU:0, one launch (start us, length us, event | category | flops | bytes accessed | tf_op | source)
XLA Modules:
  0.0 258.6 jit_solution(6873629607457570932)
XLA Ops:
  7.2 0.8 copy.18
  8.0 0.8 copy.17
  8.8 11.3 %all_gather.3 = bf16[8,32,1024]{2,0,1:T(8,128)(2,1)S(1)} all-gather(bf16[8,4,1024]{2,0,1:T(8,128)(2,1)S(1)} %pad_maximum_fusion.1), channel_id=1, replica_groups=mesh['dp'=4,'tensor'=8] {'tensor'}, dimensions={1}, use_global_device_ids=true | all-gather | bytes 589824 | tf_op jit(solution)/shard_map/all_gather | solution.py:29
  20.6 12.0 %psum.42 = f32[4,32]{1,0:T(4,128)S(1)} all-reduce(f32[4,32]{1,0:T(4,128)S(1)} %fusion.13), channel_id=1, replica_groups=mesh['dp'=4,'tensor'=8] {'dp'}, use_global_device_ids=true, to_apply=%region_1.0 | all-reduce | flops 128 | bytes 1024 | tf_op jit(solution)/shard_map/psum | solution.py:33
  32.7 5.3 %convolution_convert_fusion.4 = bf16[128,3584]{1,0:T(8,128)(2,1)} fusion(bf16[128,1024]{1,0:T(8,128)(2,1)S(1)} %bitcast.41, bf16[1024,3584]{1,0:T(8,128)(2,1)} %param.10), kind=kOutput, calls=%fused_computation.4 | convolution fusion | flops 939982848 | bytes 8519680 | tf_op jit(solution)/shard_map/dot_general | solution.py:43
  38.0 2.1 convolution_convert_fusion.5
  40.1 0.4 slice-done.7
  40.5 3.5 %convolution_convert_fusion.3 = bf16[128,3584]{1,0:T(8,128)(2,1)} fusion(bf16[128,1024]{1,0:T(8,128)(2,1)S(1)} %bitcast.45, bf16[3584,1024]{1,0:T(8,128)(2,1)S(1)} %bitcast.40), kind=kOutput, calls=%fused_computation.3 | convolution fusion | flops 939982848 | bytes 8519680 | tf_op jit(solution)/shard_map/dot_general | solution.py:44
  44.0 0.2 all-reduce.5.cloned.1.call-start
  44.2 0.4 copy-done.7
  44.8 0.6 dynamic-slice
  46.1 103.7 %all-reduce.7.cloned.1.call-done = (bf16[128,3584]{1,0:T(8,128)(2,1)}, bf16[128,3584]{1,0:T(8,128)(2,1)}, bf16[128,3584]{1,0:T(8,128)(2,1)}) async-done(((bf16[128,3584]{1,0:T(8,128)(2,1)}, bf16[128,3584]{1,0:T(8,128)(2,1)}, bf16[128,3584]{1,0:T(8,128)(2,1)}), (bf16[128,3584]{1,0:T(8,128)(2,1)}, bf16[128,3584]{1,0:T(8,128)(2,1)}, bf16[128,3584]{1,0:T(8,128)(2,1)})) %all-reduce.7.cloned.1.call-update) | async-done | bytes 2752528 | tf_op jit(solution)/shard_map/psum | solution.py:49
  149.8 5.2 %convolution_convert_fusion.6 = bf16[128,1024]{1,0:T(8,128)(2,1)S(1)} fusion(bf16[3584,1024]{1,0:T(8,128)(2,1)} %param.11, bf16[128,3584]{1,0:T(8,128)(2,1)} %get-tuple-element.9, f32[128]{0:T(128)S(1)} %mul.117, bf16[128,3584]{1,0:T(8,128)(2,1)} %get-tuple-element.11), kind=kOutput, calls=%fused_computation.26 | convolution fusion | flops 943783936 | bytes 9437696 | tf_op jit(solution)/shard_map/dot_general | solution.py:57
  155.0 5.4 %convolution_convert_fusion = bf16[3584,1024]{1,0:T(8,128)(2,1)} fusion(bf16[128,1024]{1,0:T(8,128)(2,1)S(1)} %bitcast.46, bf16[128,3584]{1,0:T(8,128)(2,1)S(1)} %copy-done.6, f32[128]{0:T(128)S(1)} %mul.117, bf16[128,3584]{1,0:T(8,128)(2,1)S(1)} %copy-done.5), kind=kOutput, calls=%fused_computation | convolution fusion | flops 947322880 | bytes 9437696 | tf_op jit(solution)/shard_map/dot_general | solution.py:69
  160.5 2.6 fusion.30
  163.1 5.4 %convolution_convert_fusion.2 = bf16[1024,3584]{1,0:T(8,128)(2,1)} fusion(bf16[128,1024]{1,0:T(8,128)(2,1)S(1)} %bitcast.43, bf16[128,3584]{1,0:T(8,128)(2,1)S(1)} %copy-done.6, bf16[128,3584]{1,0:T(8,128)(2,1)S(1)} %copy-done.4, bf16[128,3584]{1,0:T(8,128)(2,1)S(1)} %copy-done.5, f32[128]{0:T(128)S(1)} %mul.117), kind=kOutput, calls=%fused_computation.2 | convolution fusion | flops 949616640 | bytes 10355200 | tf_op jit(solution)/shard_map/dot_general | solution.py:72
  168.5 2.5 fusion.12
  171.0 0.8 pad_maximum_fusion
  171.9 5.4 %convolution_convert_fusion.1 = bf16[1024,3584]{1,0:T(8,128)(2,1)} fusion(bf16[128,1024]{1,0:T(8,128)(2,1)S(1)} %bitcast.44, bf16[128,3584]{1,0:T(8,128)(2,1)S(1)} %copy-done.4, f32[128]{0:T(128)S(1)} %mul.117, bf16[128,3584]{1,0:T(8,128)(2,1)S(1)} %copy-done.5), kind=kOutput, calls=%fused_computation.1 | convolution fusion | flops 947322880 | bytes 9437696 | tf_op jit(solution)/shard_map/dot_general | solution.py:75
  177.3 48.6 %all-reduce.5.cloned.1.call-done = bf16[2,4,32,1024]{3,2,1,0:T(8,128)(2,1)} async-done(((bf16[2,4,32,1024]{3,2,1,0:T(8,128)(2,1)}), bf16[2,4,32,1024]{3,2,1,0:T(8,128)(2,1)}) %all-reduce.5.cloned.1.call-update) | async-done | bytes 524304
  225.9 0.9 dynamic-slice_convert_fusion
  227.0 12.4 %psum.47 = f32[1024]{0:T(1024)} all-reduce(f32[1024]{0:T(1024)S(1)} %get-tuple-element.7), channel_id=1, replica_groups=mesh['dp'=4,'tensor'=8] {'tensor'}, use_global_device_ids=true, to_apply=%region_9.0 | all-reduce | flops 1024 | bytes 8192 | tf_op jit(solution)/shard_map/psum | solution.py:84
  239.4 11.6 %psum.46 = f32[4,4]{1,0:T(4,128)S(1)} all-reduce(f32[4,4]{1,0:T(4,128)S(1)} %get-tuple-element.8), channel_id=1, replica_groups=mesh['dp'=4,'tensor'=8] {'dp'}, use_global_device_ids=true, to_apply=%region_7.0 | all-reduce | flops 16 | bytes 128 | tf_op jit(solution)/shard_map/psum | solution.py:83
  251.0 0.7 fusion.19
  (51 shorter events, 1.2 us)
Async XLA Ops:
  7.2 25.4 %copy-start.2 = (f32[1024]{0:T(1024)S(1)}, f32[1024]{0:T(1024)}, u32[]{:S(2)}) copy-start(f32[1024]{0:T(1024)} %param.8) | copy-start | bytes 12292
  7.2 142.6 %all-reduce.7.cloned.1.call-start = ((), (), s32[]{:S(2)}) async-start(), calls=%async_computation.1 | async-start | bytes 5505024 | tf_op jit(solution)/shard_map/psum | solution.py:49
  32.6 5.5 %slice-start = ((s8[7340032]{0:T(1024)(128)(4,1)}), s8[4194304]{0:T(1024)(128)(4,1)S(1)}, s32[]{:S(2)}) async-start(s8[7340032]{0:T(1024)(128)(4,1)} %bitcast.33), calls=%async_computation.2 | async-start | bytes 8388608
  32.7 5.3 %slice-start.1 = ((s8[7340032]{0:T(1024)(128)(4,1)}), s8[3145728]{0:T(1024)(128)(4,1)S(1)}, s32[]{:S(2)}) async-start(s8[7340032]{0:T(1024)(128)(4,1)} %bitcast.33), calls=%async_computation.3 | async-start | bytes 6291456
  32.7 7.4 %slice-start.6 = ((s8[7340032]{0:T(1024)(128)(4,1)}), s8[4194304]{0:T(1024)(128)(4,1)S(1)}, s32[]{:S(2)}) async-start(s8[7340032]{0:T(1024)(128)(4,1)} %bitcast.39), calls=%async_computation.8 | async-start | bytes 8388608
  38.0 2.4 slice-start.7
  43.9 0.7 copy-start.7
  43.9 0.8 copy-start.8
  44.0 181.9 %all-reduce.5.cloned.1.call-start = ((), (), s32[]{:S(2)}) async-start(), calls=%async_computation | async-start | bytes 1048576
  149.7 5.2 %copy-start.5 = (bf16[128,3584]{1,0:T(8,128)(2,1)S(1)}, bf16[128,3584]{1,0:T(8,128)(2,1)}, u32[]{:S(2)}) copy-start(bf16[128,3584]{1,0:T(8,128)(2,1)} %get-tuple-element.11) | copy-start | bytes 2752516
  149.7 5.2 %copy-start.6 = (bf16[128,3584]{1,0:T(8,128)(2,1)S(1)}, bf16[128,3584]{1,0:T(8,128)(2,1)}, u32[]{:S(2)}) copy-start(bf16[128,3584]{1,0:T(8,128)(2,1)} %get-tuple-element.9) | copy-start | bytes 2752516
  149.8 10.7 %slice-start.2 = ((s8[7340032]{0:T(1024)(128)(4,1)}), s8[4194304]{0:T(1024)(128)(4,1)S(1)}, s32[]{:S(2)}) async-start(s8[7340032]{0:T(1024)(128)(4,1)} %bitcast.35), calls=%async_computation.4 | async-start | bytes 8388608
  155.0 5.5 %slice-start.3 = ((s8[7340032]{0:T(1024)(128)(4,1)}), s8[3145728]{0:T(1024)(128)(4,1)S(1)}, s32[]{:S(2)}) async-start(s8[7340032]{0:T(1024)(128)(4,1)} %bitcast.35), calls=%async_computation.5 | async-start | bytes 6291456
  155.0 5.5 %copy-start.4 = (bf16[128,3584]{1,0:T(8,128)(2,1)S(1)}, bf16[128,3584]{1,0:T(8,128)(2,1)}, u32[]{:S(2)}) copy-start(bf16[128,3584]{1,0:T(8,128)(2,1)} %get-tuple-element.10) | copy-start | bytes 2752516
  155.0 13.4 %slice-start.4 = ((s8[7340032]{0:T(1024)(128)(4,1)}), s8[4194304]{0:T(1024)(128)(4,1)S(1)}, s32[]{:S(2)}) async-start(s8[7340032]{0:T(1024)(128)(4,1)} %bitcast.37), calls=%async_computation.6 | async-start | bytes 8388608
  160.5 8.0 %slice-start.5 = ((s8[7340032]{0:T(1024)(128)(4,1)}), s8[3145728]{0:T(1024)(128)(4,1)S(1)}, s32[]{:S(2)}) async-start(s8[7340032]{0:T(1024)(128)(4,1)} %bitcast.37), calls=%async_computation.7 | async-start | bytes 6291456
  171.9 55.0 %copy-start = (bf16[4,4,1024]{2,1,0:T(4,128)(2,1)S(1)}, bf16[4,4,1024]{2,1,0:T(4,128)(2,1)}, u32[]{:S(2)}) copy-start(bf16[4,4,1024]{2,1,0:T(4,128)(2,1)} %param.7) | copy-start | bytes 98308
  171.9 79.1 %copy-start.1 = (bf16[4,4,1024]{2,1,0:T(4,128)(2,1)S(1)}, bf16[4,4,1024]{2,1,0:T(4,128)(2,1)}, u32[]{:S(2)}) copy-start(bf16[4,4,1024]{2,1,0:T(4,128)(2,1)} %param.12) | copy-start | bytes 98308
  250.9 0.8 copy-start.3
Sparse Core Ops, SparseCore 0:
  44.1 105.6 all-reduce.6
  172.0 53.8 all-reduce.4
where the time goes:
time: 259 us
  waiting for transfers between devices  152 us (59%)
  blocking collectives  47.3 us (18%)
  matrix products  37.3 us (14%)
  between operations  14.9 us (6%)
  local copies, waits for them, and re-layouts  3.46 us (1%)
  other arithmetic  3.02 us (1%)
    psum x1, waiting for transfers between devices, per_device(): lax.psum(up_part.astype(jnp.bfloat16), 'dp').astype(jnp.float32)  104 us
    unnamed x3, waiting for transfers between devices  48.7 us
    psum x1, blocking collectives, per_device(): d_gain = lax.psum(gain_part, 'tensor')  12.4 us
    psum x1, blocking collectives, per_device(): square_sum = lax.psum(jnp.sum(inputs_all * inputs_all, axis=2), 'dp')  12 us
    psum x1, blocking collectives, per_device(): row_product = lax.psum(row_part, 'dp')  11.6 us
    all_gather x1, blocking collectives, per_device(): both_all = lax.all_gather(both, 'tensor', axis=1, tiled=True)  11.3 us
    dot_general x1, matrix products, per_device(): lax.dot_general(flat_normed, gate_grad, contract_rows, preferred_element_...  5.42 us
    dot_general x1, matrix products, per_device(): lax.dot_general(hidden, flat_grad, contract_rows, preferred_element_type=...  5.42 us
  transfers between devices with their start and end apart: 2, of which 2 were waited for; matrix products, arithmetic and copies ran while one was open for 2% of the time, Pallas kernels for 0%

commit v1 on v0

--- a/solution.py
+++ b/solution.py
@@ -25,20 +25,20 @@
     local_cols = w_gate.shape[1]
     full_width = local_feat * lax.axis_size("dp")
     batches, local_rows, _ = inputs.shape
-    both = jnp.concatenate([inputs, d_output], axis=0)
-    both_all = lax.all_gather(both, "tensor", axis=1, tiled=True)
-    inputs_all = both_all[:batches].astype(jnp.float32)
-    grad_all = both_all[batches:]
-    rows = inputs_all.shape[1]
+    both = jnp.concatenate([inputs, d_output], axis=0).transpose(1, 0, 2)
+    both_all = lax.all_gather(both, "tensor", axis=0, tiled=True)
+    inputs_all = both_all[:, :batches].astype(jnp.float32)
+    grad_all = both_all[:, batches:]
+    rows = inputs_all.shape[0]
     square_sum = lax.psum(jnp.sum(inputs_all * inputs_all, axis=2), "dp")
     row_scale_all = lax.rsqrt(square_sum / full_width + epsilon)
     normed_all = (inputs_all * row_scale_all[:, :, None] * norm_gain).astype(jnp.bfloat16)
     start = tensor_index * local_rows
-    row_scale = lax.dynamic_slice_in_dim(row_scale_all, start, local_rows, axis=1)
+    row_scale = lax.dynamic_slice_in_dim(row_scale_all, start, local_rows, axis=0).T
     wide_inputs = inputs.astype(jnp.float32)
 
-    flat_normed = normed_all.reshape(batches * rows, local_feat)
-    flat_grad = grad_all.reshape(batches * rows, local_feat)
+    flat_normed = normed_all.reshape(rows * batches, local_feat)
+    flat_grad = grad_all.reshape(rows * batches, local_feat)
     gate_part = jnp.dot(flat_normed, w_gate, preferred_element_type=jnp.float32)
     up_part = jnp.dot(flat_normed, w_up, preferred_element_type=jnp.float32)
     back_part = lax.dot_general(
@@ -51,20 +51,27 @@
     )
     halvings = 3 - level_of_batch
     active = (tensor_index < jnp.right_shift(groups, halvings)).astype(jnp.float32)
-    active_mask = jnp.repeat(active, rows)[:, None]
+    active_mask = jnp.tile(active, rows)[:, None]
     hidden, gate_grad, up_grad = local_terms(gate_sum, up_sum, back_sum, active_mask)
 
     down_part = jnp.dot(hidden, w_down, preferred_element_type=jnp.float32)
     normed_part = lax.dot_general(
         gate_grad, w_gate, contract_cols, preferred_element_type=jnp.float32
     ) + lax.dot_general(up_grad, w_up, contract_cols, preferred_element_type=jnp.float32)
-    stacked = jnp.stack([down_part, normed_part]).astype(jnp.bfloat16)
-    stacked = stacked.reshape(2, batches, rows, local_feat)
-    shares = lax.psum_scatter(stacked, "tensor", scatter_dimension=2, tiled=True).astype(
+    stacked = jnp.stack(
+        [
+            down_part.reshape(rows, batches, local_feat),
+            normed_part.reshape(rows, batches, local_feat),
+        ],
+        axis=1,
+    ).astype(jnp.bfloat16)
+    stacked = stacked.reshape(rows, 2 * batches, local_feat)
+    shares = lax.psum_scatter(stacked, "tensor", scatter_dimension=0, tiled=True).astype(
         jnp.float32
     )
-    down_output = shares[0]
-    normed_grad = shares[1]
+    shares = shares.reshape(local_rows, 2, batches, local_feat)
+    down_output = shares[:, 0].transpose(1, 0, 2)
+    normed_grad = shares[:, 1].transpose(1, 0, 2)
 
     down_out = lax.dot_general(
         hidden, flat_grad, contract_rows, preferred_element_type=jnp.float32
@@ -80,8 +87,14 @@
     weighted = norm_gain * normed_grad
     row_part = jnp.sum(weighted * wide_inputs, axis=2)
     gain_part = jnp.sum(normed_grad * wide_inputs * row_scale[:, :, None], axis=(0, 1))
-    row_product = lax.psum(row_part, "dp")
-    d_gain = lax.psum(gain_part, "tensor")
+    dp_index = lax.axis_index("dp")
+    row_slots = jnp.zeros((groups,) + row_part.shape, jnp.float32)
+    row_slots = lax.dynamic_update_index_in_dim(row_slots, row_part, tensor_index, 0)
+    gain_slots = jnp.zeros((lax.axis_size("dp"), local_feat), jnp.float32)
+    gain_slots = lax.dynamic_update_index_in_dim(gain_slots, gain_part, dp_index, 0)
+    row_slots, gain_slots = lax.psum((row_slots, gain_slots), ("dp", "tensor"))
+    row_product = lax.dynamic_index_in_dim(row_slots, tensor_index, 0, keepdims=False)
+    d_gain = lax.dynamic_index_in_dim(gain_slots, dp_index, 0, keepdims=False)
     outputs = (wide_inputs + down_output).astype(jnp.bfloat16)
     scale_cube = row_scale * row_scale * row_scale
     d_inputs = (

time: 259 us -> 271 us (1.046)
  waiting for transfers between devices: 152 us -> 127 us
  blocking collectives: 47.3 us -> 69.8 us
  local copies, waits for them, and re-layouts: 3.46 us -> 12.8 us
  matrix products: 37.3 us -> 42.8 us
    unnamed x3 -> x2, waiting for transfers between devices: 48.7 us -> 0.03 us
    reduce_scatter x0 -> x1, waiting for transfers between devices: none -> 22.4 us  [per_device(): lax.psum_scatter(stacked, 'tensor', scatter_dimension=0, tiled=True)]
    psum x2 -> x1, blocking collectives: 24 us -> 39.5 us  [per_device(): row_slots, gain_slots = lax.psum((row_slots, gain_slots), ('dp', 'tensor'))]
    psum x1, blocking collectives: 12 us -> 19 us  [per_device(): square_sum = lax.psum(jnp.sum(inputs_all * inputs_all, axis=2), 'dp')]
    another operation x0 -> x5, local copies, waits for them, and re-layouts: none -> 4.92 us  [the longest x4 4.92 us: per_device(): jnp.stack([down_part.reshape(rows, batches, local_feat), normed_part.resh...]
    dot_general x1, matrix products: 2.55 us -> 6.6 us  [per_device(): lax.dot_general(gate_grad, w_gate, contract_cols, preferred_element_type=...]
    reshape x0 -> x3, local copies, waits for them, and re-layouts: none -> 2.83 us  [the longest x1 1.88 us: per_device(): flat_grad = grad_all.reshape(rows * batches, local_feat)]
  transfers between devices with their start and end apart: 2 -> 2, of which waited for: 2 -> 2; matrix products, arithmetic and copies ran while one was open for 2% -> 4% of each run, Pallas kernels for 0% -> 0%
where the time goes in v1:
time: 271 us; the launch traced here: 270 us
  waiting for transfers between devices  127 us (47%)
  blocking collectives  69.8 us (26%)
  matrix products  42.8 us (16%)
  between operations  14.3 us (5%)
  local copies, waits for them, and re-layouts  12.8 us (5%)
  other arithmetic  3 us (1%)
    psum x1, waiting for transfers between devices, per_device(): lax.psum(up_part.astype(jnp.bfloat16), 'dp').astype(jnp.float32)  105 us
    psum x1, blocking collectives, per_device(): row_slots, gain_slots = lax.psum((row_slots, gain_slots), ('dp', 'tensor'))  39.5 us
    reduce_scatter x1, waiting for transfers between devices, per_device(): lax.psum_scatter(stacked, 'tensor', scatter_dimension=0, tiled=True)  22.4 us
    psum x1, blocking collectives, per_device(): square_sum = lax.psum(jnp.sum(inputs_all * inputs_all, axis=2), 'dp')  19 us
    all_gather x1, blocking collectives, per_device(): both_all = lax.all_gather(both, 'tensor', axis=0, tiled=True)  11.3 us
    dot_general x1, matrix products, per_device(): lax.dot_general(gate_grad, w_gate, contract_cols, preferred_element_type=...  6.6 us
    dot_general x1, matrix products, per_device(): down_part = jnp.dot(hidden, w_down, preferred_element_type=jnp.float32)  5.93 us
    dot_general x1, matrix products, per_device(): lax.dot_general(flat_normed, gate_grad, contract_rows, preferred_element_...  5.43 us
  transfers between devices with their start and end apart: 2, of which 2 were waited for; matrix products, arithmetic and copies ran while one was open for 4% of the time, Pallas kernels for 0%

profile of v1, /device:TPU:0, one launch (start us, length us, event | category | flops | bytes accessed | tf_op | source)
XLA Modules:
  0.0 270.4 jit_solution(21029129249374350)
XLA Ops:
  7.2 0.8 copy.27
  8.8 11.3 %all_gather.3 = bf16[32,8,1024]{2,1,0:T(8,128)(2,1)S(1)} all-gather(bf16[4,8,1024]{2,1,0:T(8,128)(2,1)S(1)} %maximum_bitcast_fusion), channel_id=1, replica_groups=mesh['dp'=4,'tensor'=8] {'tensor'}, dimensions={0}, use_global_device_ids=true | all-gather | bytes 589824 | tf_op jit(solution)/shard_map/all_gather | solution.py:29
  20.4 0.8 slice.17
  21.2 19.0 %psum.42 = f32[32,4]{1,0:T(8,128)S(1)} all-reduce(f32[32,4]{1,0:T(8,128)S(1)} %fusion.13), channel_id=1, replica_groups=mesh['dp'=4,'tensor'=8] {'dp'}, use_global_device_ids=true, to_apply=%region_1.0 | all-reduce | flops 128 | bytes 1024 | tf_op jit(solution)/shard_map/psum | solution.py:33
  40.2 0.9 fusion.15
  41.2 1.9 reshape.36
  43.1 5.3 %convolution_convert_fusion.4 = bf16[128,3584]{1,0:T(8,128)(2,1)} fusion(bf16[128,1024]{1,0:T(8,128)(2,1)S(1)} %reshape.35, bf16[1024,3584]{1,0:T(8,128)(2,1)} %param.10), kind=kOutput, calls=%fused_computation.4 | convolution fusion | flops 939982848 | bytes 8519680 | tf_op jit(solution)/shard_map/dot_general | solution.py:43
  48.4 2.1 convolution_convert_fusion.5
  50.5 3.5 %convolution_convert_fusion.3 = bf16[128,3584]{1,0:T(8,128)(2,1)} fusion(bf16[128,1024]{1,0:T(8,128)(2,1)S(1)} %copy-done, bf16[3584,1024]{1,0:T(8,128)(2,1)S(1)} %bitcast.49), kind=kOutput, calls=%fused_computation.3 | convolution fusion | flops 939982848 | bytes 8519680 | tf_op jit(solution)/shard_map/dot_general | solution.py:44
  54.8 104.9 %all-reduce.4.cloned.1.call-done = (bf16[128,3584]{1,0:T(8,128)(2,1)}, bf16[128,3584]{1,0:T(8,128)(2,1)}, bf16[128,3584]{1,0:T(8,128)(2,1)}) async-done(((bf16[128,3584]{1,0:T(8,128)(2,1)}, bf16[128,3584]{1,0:T(8,128)(2,1)}, bf16[128,3584]{1,0:T(8,128)(2,1)}), (bf16[128,3584]{1,0:T(8,128)(2,1)}, bf16[128,3584]{1,0:T(8,128)(2,1)}, bf16[128,3584]{1,0:T(8,128)(2,1)})) %all-reduce.4.cloned.1.call-update) | async-done | bytes 2752528 | tf_op jit(solution)/shard_map/psum | solution.py:49
  159.7 5.9 %convolution_convert_fusion.6 = bf16[128,1024]{1,0:T(8,128)(2,1)} fusion(bf16[3584,1024]{1,0:T(8,128)(2,1)} %param.11, bf16[128,3584]{1,0:T(8,128)(2,1)} %get-tuple-element.11, f32[128]{0:T(128)S(1)} %mul.117, bf16[128,3584]{1,0:T(8,128)(2,1)} %get-tuple-element.13), kind=kOutput, calls=%fused_computation.26 | convolution fusion | flops 943783936 | bytes 9437696 | tf_op jit(solution)/shard_map/dot_general | solution.py:57
  165.7 5.4 %convolution_convert_fusion = bf16[3584,1024]{1,0:T(8,128)(2,1)} fusion(bf16[128,1024]{1,0:T(8,128)(2,1)S(1)} %copy-done.1, bf16[128,3584]{1,0:T(8,128)(2,1)S(1)} %copy-done.6, f32[128]{0:T(128)S(1)} %mul.117, bf16[128,3584]{1,0:T(8,128)(2,1)S(1)} %copy-done.10), kind=kOutput, calls=%fused_computation | convolution fusion | flops 947322880 | bytes 9437696 | tf_op jit(solution)/shard_map/dot_general | solution.py:76
  171.1 1.9 stack_reshape.8
  173.0 1.7 copy.28
  174.7 6.6 %fusion.30 = f32[128,1024]{1,0:T(8,128)S(1)} fusion(bf16[1024,3584]{1,0:T(8,128)(2,1)} %param.9, bf16[128,3584]{1,0:T(8,128)(2,1)} %get-tuple-element.11, bf16[128,3584]{1,0:T(8,128)(2,1)} %get-tuple-element.12, bf16[128,3584]{1,0:T(8,128)(2,1)} %get-tuple-element.13, f32[128]{0:T(128)S(1)} %mul.117), kind=kOutput, calls=%fused_computation.56 | convolution fusion | flops 945946624 | bytes 10617344 | tf_op jit(solution)/shard_map/dot_general | solution.py:58
  181.4 3.3 %fusion.12 = bf16[128,1024]{1,0:T(8,128)(2,1)} fusion(f32[128,1024]{1,0:T(8,128)S(1)} %fusion.30, bf16[1024,3584]{1,0:T(8,128)(2,1)S(1)} %bitcast.47, bf16[128,3584]{1,0:T(8,128)(2,1)S(1)} %copy-done.8, f32[128]{0:T(128)S(1)} %mul.117, bf16[128,3584]{1,0:T(8,128)(2,1)S(1)} %copy-done.11), kind=kOutput, calls=%fused_computation.25 | convolution fusion | flops 943915008 | bytes 9961984 | tf_op jit(solution)/shard_map/dot_general | solution.py:60
  184.7 1.2 stack_reshape.9
  186.0 1.0 pad_maximum_fusion
  187.0 1.1 copy.30
  188.1 5.4 %convolution_convert_fusion.1 = bf16[1024,3584]{1,0:T(8,128)(2,1)} fusion(bf16[128,1024]{1,0:T(8,128)(2,1)S(1)} %reshape.35, bf16[128,3584]{1,0:T(8,128)(2,1)S(1)} %copy-done.9, f32[128]{0:T(128)S(1)} %mul.117, bf16[128,3584]{1,0:T(8,128)(2,1)S(1)} %copy-done.12), kind=kOutput, calls=%fused_computation.1 | convolution fusion | flops 947322880 | bytes 9437696 | tf_op jit(solution)/shard_map/dot_general | solution.py:82
  193.5 5.4 %convolution_convert_fusion.2 = bf16[1024,3584]{1,0:T(8,128)(2,1)} fusion(bf16[128,1024]{1,0:T(8,128)(2,1)S(1)} %reshape.35, bf16[128,3584]{1,0:T(8,128)(2,1)S(1)} %copy-done.7, bf16[128,3584]{1,0:T(8,128)(2,1)S(1)} %copy-done.9, bf16[128,3584]{1,0:T(8,128)(2,1)S(1)} %copy-done.12, f32[128]{0:T(128)S(1)} %mul.117), kind=kOutput, calls=%fused_computation.2 | convolution fusion | flops 949616640 | bytes 10355200 | tf_op jit(solution)/shard_map/dot_general | solution.py:79
  198.9 22.4 %reduce-scatter.2.cloned.1.call-done = bf16[4,8,1024]{2,1,0:T(8,128)(2,1)} async-done(((bf16[32,8,1024]{2,1,0:T(8,128)(2,1)}), bf16[4,8,1024]{2,1,0:T(8,128)(2,1)}) %reduce-scatter.2.cloned.1.call-update) | async-done | bytes 65552 | tf_op jit(solution)/shard_map/reduce_scatter | solution.py:69
  221.4 0.9 copy.36
  222.5 39.5 %all-reduce = (f32[8,4,4]{2,1,0:T(4,128)S(1)}, f32[4,1024]{1,0:T(4,128)S(1)}) all-reduce(f32[8,4,4]{2,1,0:T(4,128)S(1)} %bitcast_dynamic-update-slice_fusion, f32[4,1024]{1,0:T(4,128)S(1)} %dynamic_update_slice.9), channel_id=1, replica_groups=mesh['dp'=4,'tensor'=8] {'dp','tensor'}, use_global_device_ids=true, to_apply=%region_7.0 | all-reduce | flops 4224 | bytes 33792 | tf_op jit(solution)/shard_map/psum | solution.py:95
  (69 shorter events, 3.9 us)
Async XLA Ops:
  7.2 152.6 %all-reduce.4.cloned.1.call-start = ((), (), s32[]{:S(2)}) async-start(), calls=%async_computation.2 | async-start | bytes 5505024 | tf_op jit(solution)/shard_map/psum | solution.py:49
  41.2 7.2 %slice-start = ((s8[7340032]{0:T(1024)(128)(4,1)}), s8[3145728]{0:T(1024)(128)(4,1)S(1)}, s32[]{:S(2)}) async-start(s8[7340032]{0:T(1024)(128)(4,1)} %bitcast.44), calls=%async_computation.3 | async-start | bytes 6291456
  43.1 5.3 %slice-start.1 = ((s8[7340032]{0:T(1024)(128)(4,1)}), s8[4194304]{0:T(1024)(128)(4,1)S(1)}, s32[]{:S(2)}) async-start(s8[7340032]{0:T(1024)(128)(4,1)} %bitcast.44), calls=%async_computation.4 | async-start | bytes 8388608
  43.1 7.4 %slice-start.4 = ((s8[7340032]{0:T(1024)(128)(4,1)}), s8[4194304]{0:T(1024)(128)(4,1)S(1)}, s32[]{:S(2)}) async-start(s8[7340032]{0:T(1024)(128)(4,1)} %bitcast.48), calls=%async_computation.7 | async-start | bytes 8388608
  48.4 2.1 slice-start.5
  48.4 2.1 copy-start
  53.9 0.7 copy-start.13
  53.9 167.4 %reduce-scatter.2.cloned.1.call-start = ((), (), s32[]{:S(2)}) async-start(), calls=%async_computation.1 | async-start | bytes 589824 | tf_op jit(solution)/shard_map/reduce_scatter | solution.py:69
  159.7 5.9 %copy-start.1 = (bf16[128,1024]{1,0:T(8,128)(2,1)S(1)}, bf16[128,1024]{1,0:T(8,128)(2,1)}, u32[]{:S(2)}) copy-start(bf16[128,1024]{1,0:T(8,128)(2,1)} %reshape.36) | copy-start | bytes 786436
  159.7 5.9 %copy-start.6 = (bf16[128,3584]{1,0:T(8,128)(2,1)S(1)}, bf16[128,3584]{1,0:T(8,128)(2,1)}, u32[]{:S(2)}) copy-start(bf16[128,3584]{1,0:T(8,128)(2,1)} %get-tuple-element.11) | copy-start | bytes 2752516
  159.7 5.9 %copy-start.10 = (bf16[128,3584]{1,0:T(8,128)(2,1)S(1)}, bf16[128,3584]{1,0:T(8,128)(2,1)}, u32[]{:S(2)}) copy-start(bf16[128,3584]{1,0:T(8,128)(2,1)} %get-tuple-element.13) | copy-start | bytes 2752516
  171.1 10.3 %slice-start.2 = ((s8[7340032]{0:T(1024)(128)(4,1)}), s8[3145728]{0:T(1024)(128)(4,1)S(1)}, s32[]{:S(2)}) async-start(s8[7340032]{0:T(1024)(128)(4,1)} %bitcast.46), calls=%async_computation.5 | async-start | bytes 6291456
  174.7 6.6 %slice-start.3 = ((s8[7340032]{0:T(1024)(128)(4,1)}), s8[4194304]{0:T(1024)(128)(4,1)S(1)}, s32[]{:S(2)}) async-start(s8[7340032]{0:T(1024)(128)(4,1)} %bitcast.46), calls=%async_computation.6 | async-start | bytes 8388608
  174.7 6.6 %copy-start.8 = (bf16[128,3584]{1,0:T(8,128)(2,1)S(1)}, bf16[128,3584]{1,0:T(8,128)(2,1)}, u32[]{:S(2)}) copy-start(bf16[128,3584]{1,0:T(8,128)(2,1)} %get-tuple-element.12) | copy-start | bytes 2752516
  174.7 6.6 %copy-start.11 = (bf16[128,3584]{1,0:T(8,128)(2,1)S(1)}, bf16[128,3584]{1,0:T(8,128)(2,1)}, u32[]{:S(2)}) copy-start(bf16[128,3584]{1,0:T(8,128)(2,1)} %get-tuple-element.13) | copy-start | bytes 2752516
  184.7 3.4 %copy-start.9 = (bf16[128,3584]{1,0:T(8,128)(2,1)S(1)}, bf16[128,3584]{1,0:T(8,128)(2,1)}, u32[]{:S(2)}) copy-start(bf16[128,3584]{1,0:T(8,128)(2,1)} %get-tuple-element.12) | copy-start | bytes 2752516
  184.7 3.4 %copy-start.12 = (bf16[128,3584]{1,0:T(8,128)(2,1)S(1)}, bf16[128,3584]{1,0:T(8,128)(2,1)}, u32[]{:S(2)}) copy-start(bf16[128,3584]{1,0:T(8,128)(2,1)} %get-tuple-element.13) | copy-start | bytes 2752516
  188.1 5.4 %copy-start.7 = (bf16[128,3584]{1,0:T(8,128)(2,1)S(1)}, bf16[128,3584]{1,0:T(8,128)(2,1)}, u32[]{:S(2)}) copy-start(bf16[128,3584]{1,0:T(8,128)(2,1)} %get-tuple-element.11) | copy-start | bytes 2752516
  193.5 28.8 %copy-start.2 = (bf16[4,4,1024]{2,1,0:T(4,128)(2,1)S(1)}, bf16[4,4,1024]{2,1,0:T(4,128)(2,1)}, u32[]{:S(2)}) copy-start(bf16[4,4,1024]{2,1,0:T(4,128)(2,1)} %param.7) | copy-start | bytes 98308
  193.5 28.8 %copy-start.4 = (f32[1024]{0:T(1024)S(1)}, f32[1024]{0:T(1024)}, u32[]{:S(2)}) copy-start(f32[1024]{0:T(1024)} %param.8) | copy-start | bytes 12292
  193.5 68.8 %copy-start.3 = (bf16[4,4,1024]{2,1,0:T(4,128)(2,1)S(1)}, bf16[4,4,1024]{2,1,0:T(4,128)(2,1)}, u32[]{:S(2)}) copy-start(bf16[4,4,1024]{2,1,0:T(4,128)(2,1)} %param.12) | copy-start | bytes 98308
  262.1 1.5 copy-start.5
Sparse Core Ops, SparseCore 0:
  54.1 105.6 all-reduce.3
  188.2 33.1 reduce-scatter.1

commit v2 on v1

--- a/solution.py
+++ b/solution.py
@@ -30,7 +30,7 @@
     inputs_all = both_all[:, :batches].astype(jnp.float32)
     grad_all = both_all[:, batches:]
     rows = inputs_all.shape[0]
-    square_sum = lax.psum(jnp.sum(inputs_all * inputs_all, axis=2), "dp")
+    square_sum = lax.psum(jnp.sum(inputs_all * inputs_all, axis=2).T, "dp").T
     row_scale_all = lax.rsqrt(square_sum / full_width + epsilon)
     normed_all = (inputs_all * row_scale_all[:, :, None] * norm_gain).astype(jnp.bfloat16)
     start = tensor_index * local_rows
@@ -39,25 +39,53 @@
 
     flat_normed = normed_all.reshape(rows * batches, local_feat)
     flat_grad = grad_all.reshape(rows * batches, local_feat)
-    gate_part = jnp.dot(flat_normed, w_gate, preferred_element_type=jnp.float32)
-    up_part = jnp.dot(flat_normed, w_up, preferred_element_type=jnp.float32)
-    back_part = lax.dot_general(
-        flat_grad, w_down, contract_cols, preferred_element_type=jnp.float32
-    )
-    gate_sum, up_sum, back_sum = (
-        lax.psum(gate_part.astype(jnp.bfloat16), "dp").astype(jnp.float32),
-        lax.psum(up_part.astype(jnp.bfloat16), "dp").astype(jnp.float32),
-        lax.psum(back_part.astype(jnp.bfloat16), "dp").astype(jnp.float32),
-    )
     halvings = 3 - level_of_batch
     active = (tensor_index < jnp.right_shift(groups, halvings)).astype(jnp.float32)
     active_mask = jnp.tile(active, rows)[:, None]
-    hidden, gate_grad, up_grad = local_terms(gate_sum, up_sum, back_sum, active_mask)
+    chunks = 2
+    width = local_cols // chunks
+    down_part = None
+    normed_part = None
+    hiddens, gate_grads, up_grads = [], [], []
+    previous = None
+    for chunk in range(chunks):
+        cols = slice(chunk * width, (chunk + 1) * width)
+        gate_w = w_gate[:, cols]
+        up_w = w_up[:, cols]
+        down_w = w_down[cols, :]
+        gate_part = jnp.dot(flat_normed, gate_w, preferred_element_type=jnp.float32)
+        up_part = jnp.dot(flat_normed, up_w, preferred_element_type=jnp.float32)
+        back_part = lax.dot_general(
+            flat_grad, down_w, contract_cols, preferred_element_type=jnp.float32
+        )
+        parts = (
+            gate_part.astype(jnp.bfloat16),
+            up_part.astype(jnp.bfloat16),
+            back_part.astype(jnp.bfloat16),
+        )
+        if previous is not None:
+            parts, _ = lax.optimization_barrier((parts, previous))
+        gate_sum, up_sum, back_sum = lax.psum(parts, "dp")
+        previous = (gate_sum, up_sum, back_sum)
+        hidden, gate_grad, up_grad = local_terms(
+            gate_sum.astype(jnp.float32),
+            up_sum.astype(jnp.float32),
+            back_sum.astype(jnp.float32),
+            active_mask,
+        )
+        hiddens.append(hidden)
+        gate_grads.append(gate_grad)
+        up_grads.append(up_grad)
+        down_term = jnp.dot(hidden, down_w, preferred_element_type=jnp.float32)
+        normed_term = lax.dot_general(
+            gate_grad, gate_w, contract_cols, preferred_element_type=jnp.float32
+        ) + lax.dot_general(up_grad, up_w, contract_cols, preferred_element_type=jnp.float32)
+        down_part = down_term if down_part is None else down_part + down_term
+        normed_part = normed_term if normed_part is None else normed_part + normed_term
+    hidden = jnp.concatenate(hiddens, axis=1)
+    gate_grad = jnp.concatenate(gate_grads, axis=1)
+    up_grad = jnp.concatenate(up_grads, axis=1)
 
-    down_part = jnp.dot(hidden, w_down, preferred_element_type=jnp.float32)
-    normed_part = lax.dot_general(
-        gate_grad, w_gate, contract_cols, preferred_element_type=jnp.float32
-    ) + lax.dot_general(up_grad, w_up, contract_cols, preferred_element_type=jnp.float32)
     stacked = jnp.stack(
         [
             down_part.reshape(rows, batches, local_feat),
@@ -87,14 +115,8 @@
     weighted = norm_gain * normed_grad
     row_part = jnp.sum(weighted * wide_inputs, axis=2)
     gain_part = jnp.sum(normed_grad * wide_inputs * row_scale[:, :, None], axis=(0, 1))
-    dp_index = lax.axis_index("dp")
-    row_slots = jnp.zeros((groups,) + row_part.shape, jnp.float32)
-    row_slots = lax.dynamic_update_index_in_dim(row_slots, row_part, tensor_index, 0)
-    gain_slots = jnp.zeros((lax.axis_size("dp"), local_feat), jnp.float32)
-    gain_slots = lax.dynamic_update_index_in_dim(gain_slots, gain_part, dp_index, 0)
-    row_slots, gain_slots = lax.psum((row_slots, gain_slots), ("dp", "tensor"))
-    row_product = lax.dynamic_index_in_dim(row_slots, tensor_index, 0, keepdims=False)
-    d_gain = lax.dynamic_index_in_dim(gain_slots, dp_index, 0, keepdims=False)
+    row_product = lax.psum(row_part, "dp")
+    d_gain = lax.psum(gain_part, "tensor")
     outputs = (wide_inputs + down_output).astype(jnp.bfloat16)
     scale_cube = row_scale * row_scale * row_scale
     d_inputs = (

time: 271 us -> 267 us (0.985)
  blocking collectives: 69.8 us -> 54.4 us
  waiting for transfers between devices: 127 us -> 135 us
  matrix products: 42.8 us -> 49.4 us
  local copies, waits for them, and re-layouts: 12.8 us -> 7.51 us
    psum x2 -> x3, blocking collectives: 58.5 us -> 43 us  [the longest x1 19 us: per_device(): square_sum = lax.psum(jnp.sum(inputs_all * inputs_all, axis=2).T, 'dp').T]
    dot_general x6 -> x12, matrix products: 26.6 us -> 34 us  [the longest x2 7.08 us: per_device(): up_part = jnp.dot(flat_normed, up_w, preferred_element_type=jnp.float32)]
    psum x1 -> x2, waiting for transfers between devices: 105 us -> 112 us  [per_device(): gate_sum, up_sum, back_sum = lax.psum(parts, 'dp')]
    convert_element_type x0 -> x1, other arithmetic: none -> 3.18 us  [local_terms(): hidden = (silu_gate * up_sum * active_mask).astype(jnp.bfloat16)]
    another operation x4, local copies, waits for them, and re-layouts: 4.92 us -> 2.03 us  [per_device(): jnp.stack([down_part.reshape(rows, batches, local_feat), normed_part.resh...]
  transfers between devices with their start and end apart: 2 -> 3, of which waited for: 2 -> 3; matrix products, arithmetic and copies ran while one was open for 4% -> 8% of each run, Pallas kernels for 0% -> 0%
where the time goes in v2:
time: 267 us; the launch traced here: 266 us
  waiting for transfers between devices  135 us (51%)
  blocking collectives  54.4 us (20%)
  matrix products  49.4 us (19%)
  between operations  14 us (5%)
  local copies, waits for them, and re-layouts  7.51 us (3%)
  other arithmetic  5.23 us (2%)
    psum x2, waiting for transfers between devices, per_device(): gate_sum, up_sum, back_sum = lax.psum(parts, 'dp')  112 us
    reduce_scatter x1, waiting for transfers between devices, per_device(): lax.psum_scatter(stacked, 'tensor', scatter_dimension=0, tiled=True)  23.2 us
    psum x1, blocking collectives, per_device(): square_sum = lax.psum(jnp.sum(inputs_all * inputs_all, axis=2).T, 'dp').T  19 us
    psum x1, blocking collectives, per_device(): d_gain = lax.psum(gain_part, 'tensor')  12.4 us
    psum x1, blocking collectives, per_device(): row_product = lax.psum(row_part, 'dp')  11.7 us
    all_gather x1, blocking collectives, per_device(): both_all = lax.all_gather(both, 'tensor', axis=0, tiled=True)  11.3 us
    dot_general x2, matrix products, per_device(): up_part = jnp.dot(flat_normed, up_w, preferred_element_type=jnp.float32)  7.08 us
    dot_general x2, matrix products, per_device(): gate_part = jnp.dot(flat_normed, gate_w, preferred_element_type=jnp.float32)  6.94 us
  transfers between devices with their start and end apart: 3, of which 3 were waited for; matrix products, arithmetic and copies ran while one was open for 8% of the time, Pallas kernels for 0%

profile of v2, /device:TPU:0, one launch (start us, length us, event | category | flops | bytes accessed | tf_op | source)
XLA Modules:
  0.0 266.2 jit_solution(6082502554845740097)
XLA Ops:
  8.8 11.3 %all_gather.3 = bf16[32,8,1024]{2,1,0:T(8,128)(2,1)S(1)} all-gather(bf16[4,8,1024]{2,1,0:T(8,128)(2,1)S(1)} %maximum_bitcast_fusion), channel_id=1, replica_groups=mesh['dp'=4,'tensor'=8] {'tensor'}, dimensions={0}, use_global_device_ids=true | all-gather | bytes 589824 | tf_op jit(solution)/shard_map/all_gather | solution.py:29
  20.5 19.0 %psum.63 = f32[4,32]{0,1:T(8,128)S(1)} all-reduce(f32[4,32]{0,1:T(8,128)S(1)} %bitcast.43), channel_id=1, replica_groups=mesh['dp'=4,'tensor'=8] {'dp'}, use_global_device_ids=true, to_apply=%region_1.0 | all-reduce | flops 128 | bytes 1024 | tf_op jit(solution)/shard_map/psum | solution.py:33
  40.6 3.6 %fusion.27 = bf16[128,1792]{1,0:T(8,128)(2,1)} fusion(bf16[128,1024]{1,0:T(8,128)(2,1)S(1)} %reshape.35, bf16[1024,3584]{1,0:T(8,128)(2,1)} %param.10), kind=kOutput, calls=%fused_computation.28 | convolution fusion | flops 469991424 | bytes 4390912 | tf_op jit(solution)/shard_map/dot_general | solution.py:57
  44.2 3.5 %fusion.24 = bf16[128,1792]{1,0:T(8,128)(2,1)} fusion(bf16[128,1024]{1,0:T(8,128)(2,1)S(1)} %reshape.35, bf16[1024,3584]{1,0:T(8,128)(2,1)} %param.9), kind=kOutput, calls=%fused_computation.27 | convolution fusion | flops 469991424 | bytes 4390912 | tf_op jit(solution)/shard_map/dot_general | solution.py:56
  47.6 2.1 fusion.30
  49.8 4.2 %fusion.39 = bf16[128,1792]{1,0:T(8,128)(2,1)} fusion(bf16[128,1024]{1,0:T(8,128)(2,1)S(1)} %reshape.36, bf16[3584,1024]{1,0:T(8,128)(2,1)} %param.11), kind=kOutput, calls=%fused_computation.32 | convolution fusion | flops 469991424 | bytes 4390912 | tf_op jit(solution)/shard_map/dot_general | solution.py:58
  54.0 3.5 %fusion.36 = bf16[128,1792]{1,0:T(8,128)(2,1)} fusion(bf16[128,1024]{1,0:T(8,128)(2,1)S(1)} %reshape.35, bf16[1024,3584]{1,0:T(8,128)(2,1)} %param.10), kind=kOutput, calls=%fused_computation.31 | convolution fusion | flops 469991424 | bytes 4390912 | tf_op jit(solution)/shard_map/dot_general | solution.py:57
  57.5 3.5 %fusion.33 = bf16[128,1792]{1,0:T(8,128)(2,1)} fusion(bf16[128,1024]{1,0:T(8,128)(2,1)S(1)} %reshape.35, bf16[1024,3584]{1,0:T(8,128)(2,1)} %param.9), kind=kOutput, calls=%fused_computation.30 | convolution fusion | flops 469991424 | bytes 4390912 | tf_op jit(solution)/shard_map/dot_general | solution.py:56
  61.0 48.8 %all-reduce.7.cloned.1.call-done = (bf16[128,1792]{1,0:T(8,128)(2,1)}, bf16[128,1792]{1,0:T(8,128)(2,1)}, bf16[128,1792]{1,0:T(8,128)(2,1)}) async-done(((bf16[128,1792]{1,0:T(8,128)(2,1)}, bf16[128,1792]{1,0:T(8,128)(2,1)}, bf16[128,1792]{1,0:T(8,128)(2,1)}), (bf16[128,1792]{1,0:T(8,128)(2,1)}, bf16[128,1792]{1,0:T(8,128)(2,1)}, bf16[128,1792]{1,0:T(8,128)(2,1)})) %all-reduce.7.cloned.1.call-update) | async-done | bytes 1376272 | tf_op jit(solution)/shard_map/psum | solution.py:68
  110.8 63.3 %all-reduce.5.cloned.1.call-done = (bf16[128,1792]{1,0:T(8,128)(2,1)}, bf16[128,1792]{1,0:T(8,128)(2,1)}, bf16[128,1792]{1,0:T(8,128)(2,1)}) async-done(((bf16[128,1792]{1,0:T(8,128)(2,1)}, bf16[128,1792]{1,0:T(8,128)(2,1)}, bf16[128,1792]{1,0:T(8,128)(2,1)}), (bf16[128,1792]{1,0:T(8,128)(2,1)}, bf16[128,1792]{1,0:T(8,128)(2,1)}, bf16[128,1792]{1,0:T(8,128)(2,1)})) %all-reduce.5.cloned.1.call-update) | async-done | bytes 1376272 | tf_op jit(solution)/shard_map/psum | solution.py:68
  174.2 3.2 %fusion.61 = (bf16[128,1792]{1,0:T(8,128)(2,1)S(1)}, bf16[128,1792]{1,0:T(8,128)(2,1)S(1)}, bf16[128,1792]{1,0:T(8,128)(2,1)S(1)}, bf16[128,1792]{1,0:T(8,128)(2...) fusion(bf16[128,1792]{1,0:T(8,128)(2,1)} %get-tuple-element.33, f32[128]{0:T(128)S(1)} %mul.156, ...), kind=kLoop, calls=%fused_computation.52 | loop fusion | flops 9633792 | bytes 5505536 | tf_op jit(solution)/shard_map/convert_element_type | solution.py:15
  177.4 3.5 %fusion.16 = f32[128,1024]{1,0:T(8,128)S(1)} fusion(bf16[128,1792]{1,0:T(8,128)(2,1)S(1)} %get-tuple-element.37, bf16[1024,3584]{1,0:T(8,128)(2,1)} %param.10), kind=kOutput, calls=%fused_computation.19 | convolution fusion | flops 469762048 | bytes 4653056 | tf_op jit(solution)/shard_map/dot_general | solution.py:82
  180.9 3.3 %fusion.4 = f32[128,1024]{1,0:T(8,128)S(1)} fusion(bf16[128,1792]{1,0:T(8,128)(2,1)S(1)} %get-tuple-element.45, bf16[1024,3584]{1,0:T(8,128)(2,1)} %param.10), kind=kOutput, calls=%fused_computation.7 | convolution fusion | flops 469762048 | bytes 4653056 | tf_op jit(solution)/shard_map/dot_general | solution.py:82
  184.2 1.3 fusion.51
  185.5 2.0 fusion.57
  187.6 1.1 stack_reshape.9
  189.4 2.8 %fusion = f32[128,1024]{1,0:T(8,128)S(1)} fusion(bf16[128,1792]{1,0:T(8,128)(2,1)S(1)} %get-tuple-element.47, bf16[3584,1024]{1,0:T(8,128)(2,1)} %param.11), kind=kOutput, calls=%fused_computation.3 | convolution fusion | flops 469762048 | bytes 4653056 | tf_op jit(solution)/shard_map/dot_general | solution.py:79
  192.3 5.1 %convolution_convert_fusion = bf16[3584,1024]{1,0:T(8,128)(2,1)} fusion(bf16[128,1024]{1,0:T(8,128)(2,1)S(1)} %reshape.36, bf16[128,1792]{1,0:T(8,128)(2,1)S(1)} %get-tuple-element.47, bf16[128,1792]{1,0:T(8,128)(2,1)S(1)} %get-tuple-element.35), kind=kOutput, calls=%fused_computation | convolution fusion | flops 945029120 | bytes 8519680 | tf_op jit(solution)/shard_map/dot_general | solution.py:104
  198.4 1.1 copy.40
  199.5 5.1 %convolution_convert_fusion.2 = bf16[1024,3584]{1,0:T(8,128)(2,1)} fusion(bf16[128,1024]{1,0:T(8,128)(2,1)S(1)} %reshape.35, bf16[128,1792]{1,0:T(8,128)(2,1)S(1)} %get-tuple-element.46, bf16[128,1792]{1,0:T(8,128)(2,1)S(1)} %get-tuple-element.36), kind=kOutput, calls=%fused_computation.2 | convolution fusion | flops 945029120 | bytes 8519680 | tf_op jit(solution)/shard_map/dot_general | solution.py:107
  204.7 5.1 %convolution_convert_fusion.1 = bf16[1024,3584]{1,0:T(8,128)(2,1)} fusion(bf16[128,1024]{1,0:T(8,128)(2,1)S(1)} %reshape.35, bf16[128,1792]{1,0:T(8,128)(2,1)S(1)} %get-tuple-element.45, bf16[128,1792]{1,0:T(8,128)(2,1)S(1)} %get-tuple-element.37), kind=kOutput, calls=%fused_computation.1 | convolution fusion | flops 945029120 | bytes 8519680 | tf_op jit(solution)/shard_map/dot_general | solution.py:110
  209.8 23.2 %reduce-scatter.2.cloned.1.call-done = bf16[4,8,1024]{2,1,0:T(8,128)(2,1)} async-done(((bf16[32,8,1024]{2,1,0:T(8,128)(2,1)}), bf16[4,8,1024]{2,1,0:T(8,128)(2,1)}) %reduce-scatter.2.cloned.1.call-update) | async-done | bytes 65552 | tf_op jit(solution)/shard_map/reduce_scatter | solution.py:97
  234.2 11.7 %psum.70 = f32[4,4]{0,1:T(4,128)S(1)} all-reduce(f32[4,4]{0,1:T(4,128)S(1)} %copy.44), channel_id=1, replica_groups=mesh['dp'=4,'tensor'=8] {'dp'}, use_global_device_ids=true, to_apply=%region_10.0 | all-reduce | flops 16 | bytes 128 | tf_op jit(solution)/shard_map/psum | solution.py:118
  246.5 12.4 %psum.71 = f32[1024]{0:T(1024)} all-reduce(f32[1024]{0:T(1024)S(1)} %get-tuple-element.27), channel_id=1, replica_groups=mesh['dp'=4,'tensor'=8] {'tensor'}, use_global_device_ids=true, to_apply=%region_12.0 | all-reduce | flops 1024 | bytes 8192 | tf_op jit(solution)/shard_map/psum | solution.py:119
  (56 shorter events, 8.5 us)
Async XLA Ops:
  7.2 102.6 %all-reduce.7.cloned.1.call-start = ((), (), s32[]{:S(2)}) async-start(), calls=%async_computation.3 | async-start | bytes 2752512 | tf_op jit(solution)/shard_map/psum | solution.py:68
  40.6 7.1 %copy-start.5 = (bf16[3584,1024]{1,0:T(8,128)(2,1)S(1)}, bf16[3584,1024]{1,0:T(8,128)(2,1)}, u32[]{:S(2)}) copy-start(bf16[3584,1024]{1,0:T(8,128)(2,1)} %param.11) | copy-start | bytes 22020100
  49.8 60.2 %copy-start.6 = (s32[4]{0:T(128)S(1)}, s32[4]{0:T(128)}, u32[]{:S(2)}) copy-start(s32[4]{0:T(128)} %param.13) | copy-start | bytes 52
  49.8 124.4 %all-reduce.5.cloned.1.call-start = ((), (), s32[]{:S(2)}) async-start(), calls=%async_computation.2 | async-start | bytes 2752512 | tf_op jit(solution)/shard_map/psum | solution.py:68
  109.8 123.2 %reduce-scatter.2.cloned.1.call-start = ((), (), s32[]{:S(2)}) async-start(), calls=%async_computation.1 | async-start | bytes 589824 | tf_op jit(solution)/shard_map/reduce_scatter | solution.py:97
  174.2 10.0 %slice-start = ((s8[7340032]{0:T(1024)(128)(4,1)}), s8[4194304]{0:T(1024)(128)(4,1)S(1)}, s32[]{:S(2)}) async-start(s8[7340032]{0:T(1024)(128)(4,1)} %bitcast.44), calls=%async_computation.4 | async-start | bytes 8388608
  177.4 6.8 %slice-start.1 = ((s8[7340032]{0:T(1024)(128)(4,1)}), s8[3145728]{0:T(1024)(128)(4,1)S(1)}, s32[]{:S(2)}) async-start(s8[7340032]{0:T(1024)(128)(4,1)} %bitcast.44), calls=%async_computation.5 | async-start | bytes 6291456
  189.4 8.0 %slice-start.2 = ((s8[7340032]{0:T(1024)(128)(4,1)}), s8[4194304]{0:T(1024)(128)(4,1)S(1)}, s32[]{:S(2)}) async-start(s8[7340032]{0:T(1024)(128)(4,1)} %bitcast.46), calls=%async_computation.6 | async-start | bytes 8388608
  192.2 5.2 %slice-start.3 = ((s8[7340032]{0:T(1024)(128)(4,1)}), s8[3145728]{0:T(1024)(128)(4,1)S(1)}, s32[]{:S(2)}) async-start(s8[7340032]{0:T(1024)(128)(4,1)} %bitcast.46), calls=%async_computation.7 | async-start | bytes 6291456
  192.3 6.1 %copy-start = (bf16[32,1,4,1024]{3,0,2,1:T(8,128)(2,1)S(1)}, bf16[32,1,4,1024]{3,0,2,1:T(8,128)(2,1)}, u32[]{:S(2)}) copy-start(bf16[32,1,4,1024]{3,0,2,1:T(8,128)(2,1)} %copy.39) | copy-start | bytes 786436
  204.7 29.3 %copy-start.1 = (bf16[4,4,1024]{2,1,0:T(4,128)(2,1)S(1)}, bf16[4,4,1024]{2,1,0:T(4,128)(2,1)}, u32[]{:S(2)}) copy-start(bf16[4,4,1024]{2,1,0:T(4,128)(2,1)} %param.7) | copy-start | bytes 98308
  204.7 29.3 %copy-start.3 = (f32[1024]{0:T(1024)S(1)}, f32[1024]{0:T(1024)}, u32[]{:S(2)}) copy-start(f32[1024]{0:T(1024)} %param.8) | copy-start | bytes 12292
  204.7 29.3 %copy-start.4 = (f32[4,4]{1,0:T(4,128)S(1)}, f32[4,4]{1,0:T(4,128)}, u32[]{:S(2)}) copy-start(f32[4,4]{1,0:T(4,128)} %copy.42) | copy-start | bytes 196
  204.7 54.3 %copy-start.2 = (bf16[4,4,1024]{2,1,0:T(4,128)(2,1)S(1)}, bf16[4,4,1024]{2,1,0:T(4,128)(2,1)}, u32[]{:S(2)}) copy-start(bf16[4,4,1024]{2,1,0:T(4,128)(2,1)} %param.12) | copy-start | bytes 98308
Sparse Core Ops, SparseCore 0:
  49.9 59.8 all-reduce.6
  112.3 61.7 all-reduce.4
  199.6 33.3 reduce-scatter.1

commit v3 on v2

--- a/solution.py
+++ b/solution.py
@@ -25,24 +25,22 @@
     local_cols = w_gate.shape[1]
     full_width = local_feat * lax.axis_size("dp")
     batches, local_rows, _ = inputs.shape
-    both = jnp.concatenate([inputs, d_output], axis=0).transpose(1, 0, 2)
+    wide_inputs = inputs.astype(jnp.float32)
+    square_sum = lax.psum(jnp.sum(wide_inputs * wide_inputs, axis=2), "dp")
+    row_scale = lax.rsqrt(square_sum / full_width + epsilon)
+    normed = (wide_inputs * row_scale[:, :, None] * norm_gain).astype(jnp.bfloat16)
+    both = jnp.concatenate([normed, d_output], axis=0).transpose(1, 0, 2)
     both_all = lax.all_gather(both, "tensor", axis=0, tiled=True)
-    inputs_all = both_all[:, :batches].astype(jnp.float32)
+    normed_all = both_all[:, :batches]
     grad_all = both_all[:, batches:]
-    rows = inputs_all.shape[0]
-    square_sum = lax.psum(jnp.sum(inputs_all * inputs_all, axis=2).T, "dp").T
-    row_scale_all = lax.rsqrt(square_sum / full_width + epsilon)
-    normed_all = (inputs_all * row_scale_all[:, :, None] * norm_gain).astype(jnp.bfloat16)
-    start = tensor_index * local_rows
-    row_scale = lax.dynamic_slice_in_dim(row_scale_all, start, local_rows, axis=0).T
-    wide_inputs = inputs.astype(jnp.float32)
+    rows = normed_all.shape[0]
 
     flat_normed = normed_all.reshape(rows * batches, local_feat)
     flat_grad = grad_all.reshape(rows * batches, local_feat)
     halvings = 3 - level_of_batch
     active = (tensor_index < jnp.right_shift(groups, halvings)).astype(jnp.float32)
     active_mask = jnp.tile(active, rows)[:, None]
-    chunks = 2
+    chunks = 1
     width = local_cols // chunks
     down_part = None
     normed_part = None

time: 267 us -> 248 us (0.929)
  waiting for transfers between devices: 135 us -> 128 us
  blocking collectives: 54.4 us -> 47.7 us
  matrix products: 49.4 us -> 42.9 us
  local copies, waits for them, and re-layouts: 7.51 us -> 10.3 us
    psum x2 -> x1, waiting for transfers between devices: 112 us -> 105 us  [per_device(): gate_sum, up_sum, back_sum = lax.psum(parts, 'dp')]
    psum x1, blocking collectives: 19 us -> 13.5 us  [per_device(): square_sum = lax.psum(jnp.sum(wide_inputs * wide_inputs, axis=2), 'dp')]
    dot_general x2 -> x1, matrix products: 6.94 us -> 2.06 us  [per_device(): gate_part = jnp.dot(flat_normed, gate_w, preferred_element_type=jnp.float32)]
    dot_general x2 -> x1, matrix products: 6.8 us -> 3.28 us  [per_device(): lax.dot_general(up_grad, up_w, contract_cols, preferred_element_type=jnp....]
    dot_general x2 -> x1, matrix products: 3.33 us -> 6.6 us  [per_device(): lax.dot_general(gate_grad, gate_w, contract_cols, preferred_element_type=...]
    convert_element_type x2 -> x1, other arithmetic: 4.07 us -> 0.85 us  [per_device(): (wide_inputs * row_scale[:, :, None] * norm_gain).astype(jnp.bfloat16)]
    another operation x4, local copies, waits for them, and re-layouts: 2.03 us -> 4.91 us  [per_device(): jnp.stack([down_part.reshape(rows, batches, local_feat), normed_part.resh...]
    dot_general x2 -> x1, matrix products: 6.27 us -> 3.46 us  [per_device(): lax.dot_general(flat_grad, down_w, contract_cols, preferred_element_type=...]
  transfers between devices with their start and end apart: 3 -> 2, of which waited for: 3 -> 2; matrix products, arithmetic and copies ran while one was open for 8% -> 4% of each run, Pallas kernels for 0% -> 0%
where the time goes in v3:
time: 248 us; the launch traced here: 247 us
  waiting for transfers between devices  128 us (52%)
  blocking collectives  47.7 us (19%)
  matrix products  42.9 us (17%)
  between operations  14.2 us (6%)
  local copies, waits for them, and re-layouts  10.3 us (4%)
  other arithmetic  4.38 us (2%)
    psum x1, waiting for transfers between devices, per_device(): gate_sum, up_sum, back_sum = lax.psum(parts, 'dp')  105 us
    reduce_scatter x1, waiting for transfers between devices, per_device(): lax.psum_scatter(stacked, 'tensor', scatter_dimension=0, tiled=True)  22.5 us
    psum x1, blocking collectives, per_device(): square_sum = lax.psum(jnp.sum(wide_inputs * wide_inputs, axis=2), 'dp')  13.5 us
    psum x1, blocking collectives, per_device(): d_gain = lax.psum(gain_part, 'tensor')  12.7 us
    psum x1, blocking collectives, per_device(): row_product = lax.psum(row_part, 'dp')  11.7 us
    all_gather x1, blocking collectives, per_device(): both_all = lax.all_gather(both, 'tensor', axis=0, tiled=True)  9.86 us
    dot_general x1, matrix products, per_device(): lax.dot_general(gate_grad, gate_w, contract_cols, preferred_element_type=...  6.6 us
    dot_general x1, matrix products, per_device(): down_term = jnp.dot(hidden, down_w, preferred_element_type=jnp.float32)  5.93 us
  transfers between devices with their start and end apart: 2, of which 2 were waited for; matrix products, arithmetic and copies ran while one was open for 4% of the time, Pallas kernels for 0%

profile of v3, /device:TPU:0, one launch (start us, length us, event | category | flops | bytes accessed | tf_op | source)
XLA Modules:
  0.0 247.2 jit_solution(4491726993086342741)
XLA Ops:
  7.2 0.9 fusion.13
  8.1 13.5 %psum.42 = f32[4,4]{1,0:T(4,128)S(1)} all-reduce(f32[4,4]{1,0:T(4,128)S(1)} %fusion.13), channel_id=1, replica_groups=mesh['dp'=4,'tensor'=8] {'dp'}, use_global_device_ids=true, to_apply=%region_1.0 | all-reduce | flops 16 | bytes 128 | tf_op jit(solution)/shard_map/psum | solution.py:29
  23.2 9.9 %all_gather.3 = bf16[32,8,1024]{2,1,0:T(8,128)(2,1)S(1)} all-gather(bf16[4,8,1024]{2,1,0:T(8,128)(2,1)S(1)} %copy.28), channel_id=1, replica_groups=mesh['dp'=4,'tensor'=8] {'tensor'}, dimensions={0}, use_global_device_ids=true | all-gather | bytes 589824 | tf_op jit(solution)/shard_map/all_gather | solution.py:33
  33.1 0.9 fusion.32
  34.7 1.2 reshape.34
  35.9 5.3 %convolution_convert_fusion.4 = bf16[128,3584]{1,0:T(8,128)(2,1)} fusion(bf16[128,1024]{1,0:T(8,128)(2,1)S(1)} %reshape.34, bf16[1024,3584]{1,0:T(8,128)(2,1)} %param.10), kind=kOutput, calls=%fused_computation.4 | convolution fusion | flops 939982848 | bytes 8519680 | tf_op jit(solution)/shard_map/dot_general | solution.py:55
  41.3 2.1 convolution_convert_fusion.5
  43.3 3.5 %convolution_convert_fusion.3 = bf16[128,3584]{1,0:T(8,128)(2,1)} fusion(bf16[128,1024]{1,0:T(8,128)(2,1)S(1)} %copy-done, bf16[3584,1024]{1,0:T(8,128)(2,1)S(1)} %bitcast.39), kind=kOutput, calls=%fused_computation.3 | convolution fusion | flops 939982848 | bytes 8519680 | tf_op jit(solution)/shard_map/dot_general | solution.py:56
  47.6 105.0 %all-reduce.3.cloned.1.call-done = (bf16[128,3584]{1,0:T(8,128)(2,1)}, bf16[128,3584]{1,0:T(8,128)(2,1)}, bf16[128,3584]{1,0:T(8,128)(2,1)}) async-done(((bf16[128,3584]{1,0:T(8,128)(2,1)}, bf16[128,3584]{1,0:T(8,128)(2,1)}, bf16[128,3584]{1,0:T(8,128)(2,1)}), (bf16[128,3584]{1,0:T(8,128)(2,1)}, bf16[128,3584]{1,0:T(8,128)(2,1)}, bf16[128,3584]{1,0:T(8,128)(2,1)})) %all-reduce.3.cloned.1.call-update) | async-done | bytes 2752528 | tf_op jit(solution)/shard_map/psum | solution.py:66
  152.6 5.9 %convolution_convert_fusion.6 = bf16[128,1024]{1,0:T(8,128)(2,1)} fusion(bf16[3584,1024]{1,0:T(8,128)(2,1)} %param.11, bf16[128,3584]{1,0:T(8,128)(2,1)} %get-tuple-element.16, f32[128]{0:T(128)S(1)} %mul.110, bf16[128,3584]{1,0:T(8,128)(2,1)} %get-tuple-element.18), kind=kOutput, calls=%fused_computation.26 | convolution fusion | flops 943783936 | bytes 9437696 | tf_op jit(solution)/shard_map/dot_general | solution.py:77
  158.5 5.4 %convolution_convert_fusion = bf16[3584,1024]{1,0:T(8,128)(2,1)} fusion(bf16[128,1024]{1,0:T(8,128)(2,1)S(1)} %copy-done.1, bf16[128,3584]{1,0:T(8,128)(2,1)S(1)} %copy-done.6, f32[128]{0:T(128)S(1)} %mul.110, bf16[128,3584]{1,0:T(8,128)(2,1)S(1)} %copy-done.10), kind=kOutput, calls=%fused_computation | convolution fusion | flops 947322880 | bytes 9437696 | tf_op jit(solution)/shard_map/dot_general | solution.py:102
  164.0 1.9 stack_reshape.8
  165.9 1.7 copy.29
  167.6 6.6 %fusion.30 = f32[128,1024]{1,0:T(8,128)S(1)} fusion(bf16[1024,3584]{1,0:T(8,128)(2,1)} %param.9, bf16[128,3584]{1,0:T(8,128)(2,1)} %get-tuple-element.16, bf16[128,3584]{1,0:T(8,128)(2,1)} %get-tuple-element.17, bf16[128,3584]{1,0:T(8,128)(2,1)} %get-tuple-element.18, f32[128]{0:T(128)S(1)} %mul.110), kind=kOutput, calls=%fused_computation.52 | convolution fusion | flops 945946624 | bytes 10617344 | tf_op jit(solution)/shard_map/dot_general | solution.py:78
  174.3 3.3 %fusion.12 = bf16[128,1024]{1,0:T(8,128)(2,1)} fusion(f32[128,1024]{1,0:T(8,128)S(1)} %fusion.30, bf16[1024,3584]{1,0:T(8,128)(2,1)S(1)} %bitcast.37, bf16[128,3584]{1,0:T(8,128)(2,1)S(1)} %copy-done.8, f32[128]{0:T(128)S(1)} %mul.110, bf16[128,3584]{1,0:T(8,128)(2,1)S(1)} %copy-done.11), kind=kOutput, calls=%fused_computation.25 | convolution fusion | flops 943915008 | bytes 9961984 | tf_op jit(solution)/shard_map/dot_general | solution.py:80
  177.6 1.2 stack_reshape.9
  178.8 1.0 pad_maximum_fusion
  179.8 1.1 copy.31
  181.0 5.4 %convolution_convert_fusion.1 = bf16[1024,3584]{1,0:T(8,128)(2,1)} fusion(bf16[128,1024]{1,0:T(8,128)(2,1)S(1)} %reshape.34, bf16[128,3584]{1,0:T(8,128)(2,1)S(1)} %copy-done.9, f32[128]{0:T(128)S(1)} %mul.110, bf16[128,3584]{1,0:T(8,128)(2,1)S(1)} %copy-done.12), kind=kOutput, calls=%fused_computation.1 | convolution fusion | flops 947322880 | bytes 9437696 | tf_op jit(solution)/shard_map/dot_general | solution.py:108
  186.4 5.4 %convolution_convert_fusion.2 = bf16[1024,3584]{1,0:T(8,128)(2,1)} fusion(bf16[128,1024]{1,0:T(8,128)(2,1)S(1)} %reshape.34, bf16[128,3584]{1,0:T(8,128)(2,1)S(1)} %copy-done.7, bf16[128,3584]{1,0:T(8,128)(2,1)S(1)} %copy-done.9, bf16[128,3584]{1,0:T(8,128)(2,1)S(1)} %copy-done.12, f32[128]{0:T(128)S(1)} %mul.110), kind=kOutput, calls=%fused_computation.2 | convolution fusion | flops 949616640 | bytes 10355200 | tf_op jit(solution)/shard_map/dot_general | solution.py:105
  191.8 22.5 %reduce-scatter.2.cloned.1.call-done = bf16[4,8,1024]{2,1,0:T(8,128)(2,1)} async-done(((bf16[32,8,1024]{2,1,0:T(8,128)(2,1)}), bf16[4,8,1024]{2,1,0:T(8,128)(2,1)}) %reduce-scatter.2.cloned.1.call-update) | async-done | bytes 65552 | tf_op jit(solution)/shard_map/reduce_scatter | solution.py:95
  214.3 0.9 copy.32
  215.3 12.7 %psum.47 = f32[1024]{0:T(1024)} all-reduce(f32[1024]{0:T(1024)S(1)} %get-tuple-element.14), channel_id=1, replica_groups=mesh['dp'=4,'tensor'=8] {'tensor'}, use_global_device_ids=true, to_apply=%region_9.0 | all-reduce | flops 1024 | bytes 8192 | tf_op jit(solution)/shard_map/psum | solution.py:117
  228.0 11.7 %psum.46 = f32[4,4]{1,0:T(4,128)S(1)} all-reduce(f32[4,4]{1,0:T(4,128)S(1)} %get-tuple-element.15), channel_id=1, replica_groups=mesh['dp'=4,'tensor'=8] {'dp'}, use_global_device_ids=true, to_apply=%region_7.0 | all-reduce | flops 16 | bytes 128 | tf_op jit(solution)/shard_map/psum | solution.py:116
  (59 shorter events, 4.3 us)
Async XLA Ops:
  7.2 145.4 %all-reduce.3.cloned.1.call-start = ((), (), s32[]{:S(2)}) async-start(), calls=%async_computation.2 | async-start | bytes 5505024 | tf_op jit(solution)/shard_map/psum | solution.py:66
  34.7 6.5 %slice-start = ((s8[7340032]{0:T(1024)(128)(4,1)}), s8[3145728]{0:T(1024)(128)(4,1)S(1)}, s32[]{:S(2)}) async-start(s8[7340032]{0:T(1024)(128)(4,1)} %bitcast.34), calls=%async_computation.3 | async-start | bytes 6291456
  35.9 5.3 %slice-start.1 = ((s8[7340032]{0:T(1024)(128)(4,1)}), s8[4194304]{0:T(1024)(128)(4,1)S(1)}, s32[]{:S(2)}) async-start(s8[7340032]{0:T(1024)(128)(4,1)} %bitcast.34), calls=%async_computation.4 | async-start | bytes 8388608
  35.9 7.4 %slice-start.4 = ((s8[7340032]{0:T(1024)(128)(4,1)}), s8[4194304]{0:T(1024)(128)(4,1)S(1)}, s32[]{:S(2)}) async-start(s8[7340032]{0:T(1024)(128)(4,1)} %bitcast.38), calls=%async_computation.7 | async-start | bytes 8388608
  41.2 2.1 slice-start.5
  41.2 2.1 copy-start
  46.8 0.7 copy-start.13
  46.8 167.4 %reduce-scatter.2.cloned.1.call-start = ((), (), s32[]{:S(2)}) async-start(), calls=%async_computation.1 | async-start | bytes 589824 | tf_op jit(solution)/shard_map/reduce_scatter | solution.py:95
  152.6 5.9 %copy-start.1 = (bf16[128,1024]{1,0:T(8,128)(2,1)S(1)}, bf16[128,1024]{1,0:T(8,128)(2,1)}, u32[]{:S(2)}) copy-start(bf16[128,1024]{1,0:T(8,128)(2,1)} %reshape.35) | copy-start | bytes 786436
  152.6 5.9 %copy-start.6 = (bf16[128,3584]{1,0:T(8,128)(2,1)S(1)}, bf16[128,3584]{1,0:T(8,128)(2,1)}, u32[]{:S(2)}) copy-start(bf16[128,3584]{1,0:T(8,128)(2,1)} %get-tuple-element.16) | copy-start | bytes 2752516
  152.6 5.9 %copy-start.10 = (bf16[128,3584]{1,0:T(8,128)(2,1)S(1)}, bf16[128,3584]{1,0:T(8,128)(2,1)}, u32[]{:S(2)}) copy-start(bf16[128,3584]{1,0:T(8,128)(2,1)} %get-tuple-element.18) | copy-start | bytes 2752516
  164.0 10.3 %slice-start.2 = ((s8[7340032]{0:T(1024)(128)(4,1)}), s8[3145728]{0:T(1024)(128)(4,1)S(1)}, s32[]{:S(2)}) async-start(s8[7340032]{0:T(1024)(128)(4,1)} %bitcast.36), calls=%async_computation.5 | async-start | bytes 6291456
  167.6 6.6 %slice-start.3 = ((s8[7340032]{0:T(1024)(128)(4,1)}), s8[4194304]{0:T(1024)(128)(4,1)S(1)}, s32[]{:S(2)}) async-start(s8[7340032]{0:T(1024)(128)(4,1)} %bitcast.36), calls=%async_computation.6 | async-start | bytes 8388608
  167.6 6.6 %copy-start.8 = (bf16[128,3584]{1,0:T(8,128)(2,1)S(1)}, bf16[128,3584]{1,0:T(8,128)(2,1)}, u32[]{:S(2)}) copy-start(bf16[128,3584]{1,0:T(8,128)(2,1)} %get-tuple-element.17) | copy-start | bytes 2752516
  167.6 6.6 %copy-start.11 = (bf16[128,3584]{1,0:T(8,128)(2,1)S(1)}, bf16[128,3584]{1,0:T(8,128)(2,1)}, u32[]{:S(2)}) copy-start(bf16[128,3584]{1,0:T(8,128)(2,1)} %get-tuple-element.18) | copy-start | bytes 2752516
  177.5 3.4 %copy-start.9 = (bf16[128,3584]{1,0:T(8,128)(2,1)S(1)}, bf16[128,3584]{1,0:T(8,128)(2,1)}, u32[]{:S(2)}) copy-start(bf16[128,3584]{1,0:T(8,128)(2,1)} %get-tuple-element.17) | copy-start | bytes 2752516
  177.5 3.4 %copy-start.12 = (bf16[128,3584]{1,0:T(8,128)(2,1)S(1)}, bf16[128,3584]{1,0:T(8,128)(2,1)}, u32[]{:S(2)}) copy-start(bf16[128,3584]{1,0:T(8,128)(2,1)} %get-tuple-element.18) | copy-start | bytes 2752516
  181.0 5.4 %copy-start.7 = (bf16[128,3584]{1,0:T(8,128)(2,1)S(1)}, bf16[128,3584]{1,0:T(8,128)(2,1)}, u32[]{:S(2)}) copy-start(bf16[128,3584]{1,0:T(8,128)(2,1)} %get-tuple-element.16) | copy-start | bytes 2752516
  186.4 28.8 %copy-start.2 = (bf16[4,4,1024]{2,1,0:T(4,128)(2,1)S(1)}, bf16[4,4,1024]{2,1,0:T(4,128)(2,1)}, u32[]{:S(2)}) copy-start(bf16[4,4,1024]{2,1,0:T(4,128)(2,1)} %param.7) | copy-start | bytes 98308
  186.4 28.8 %copy-start.4 = (f32[1024]{0:T(1024)S(1)}, f32[1024]{0:T(1024)}, u32[]{:S(2)}) copy-start(f32[1024]{0:T(1024)} %param.8) | copy-start | bytes 12292
  186.4 53.3 %copy-start.3 = (bf16[4,4,1024]{2,1,0:T(4,128)(2,1)S(1)}, bf16[4,4,1024]{2,1,0:T(4,128)(2,1)}, u32[]{:S(2)}) copy-start(bf16[4,4,1024]{2,1,0:T(4,128)(2,1)} %param.12) | copy-start | bytes 98308
  239.7 0.7 copy-start.5
Sparse Core Ops, SparseCore 0:
  46.9 105.6 all-reduce.2
  181.1 33.1 reduce-scatter.1

commit v4 on v3

--- a/solution.py
+++ b/solution.py
@@ -29,10 +29,12 @@
     square_sum = lax.psum(jnp.sum(wide_inputs * wide_inputs, axis=2), "dp")
     row_scale = lax.rsqrt(square_sum / full_width + epsilon)
     normed = (wide_inputs * row_scale[:, :, None] * norm_gain).astype(jnp.bfloat16)
-    both = jnp.concatenate([normed, d_output], axis=0).transpose(1, 0, 2)
+    both = jnp.concatenate([normed, d_output, inputs], axis=0).transpose(1, 0, 2)
     both_all = lax.all_gather(both, "tensor", axis=0, tiled=True)
     normed_all = both_all[:, :batches]
-    grad_all = both_all[:, batches:]
+    grad_all = both_all[:, batches : 2 * batches]
+    inputs_all = both_all[:, 2 * batches :].astype(jnp.float32)
+    row_scale_all = lax.all_gather(row_scale.T, "tensor", axis=0, tiled=True)
     rows = normed_all.shape[0]
 
     flat_normed = normed_all.reshape(rows * batches, local_feat)
@@ -92,6 +94,9 @@
         axis=1,
     ).astype(jnp.bfloat16)
     stacked = stacked.reshape(rows, 2 * batches, local_feat)
+    scaled_all = (inputs_all * row_scale_all[:, :, None]).reshape(rows * batches, local_feat)
+    d_gain = lax.psum(jnp.sum(normed_part * scaled_all, axis=0), "tensor")
+    hidden, flat_grad, _ = lax.optimization_barrier((hidden, flat_grad, stacked))
     shares = lax.psum_scatter(stacked, "tensor", scatter_dimension=0, tiled=True).astype(
         jnp.float32
     )
@@ -112,9 +117,7 @@
     wide_grad = d_output.astype(jnp.float32)
     weighted = norm_gain * normed_grad
     row_part = jnp.sum(weighted * wide_inputs, axis=2)
-    gain_part = jnp.sum(normed_grad * wide_inputs * row_scale[:, :, None], axis=(0, 1))
     row_product = lax.psum(row_part, "dp")
-    d_gain = lax.psum(gain_part, "tensor")
     outputs = (wide_inputs + down_output).astype(jnp.bfloat16)
     scale_cube = row_scale * row_scale * row_scale
     d_inputs = (

time: 248 us -> 231 us (0.931)
  waiting for transfers between devices: 128 us -> 103 us
  blocking collectives: 47.7 us -> 59.6 us
  matrix products: 42.9 us -> 39.5 us
  local copies, waits for them, and re-layouts: 10.3 us -> 7.59 us
  other arithmetic: 4.38 us -> 6.88 us
    reduce_scatter x1, waiting for transfers between devices: 22.5 us -> 8.45 us  [per_device(): lax.psum_scatter(stacked, 'tensor', scatter_dimension=0, tiled=True)]
    psum x1, waiting for transfers between devices: 105 us -> 94.3 us  [per_device(): gate_sum, up_sum, back_sum = lax.psum(parts, 'dp')]
    all_gather x0 -> x1, blocking collectives: none -> 9.07 us  [per_device(): row_scale_all = lax.all_gather(row_scale.T, 'tensor', axis=0, tiled=True)]
    another operation x4, local copies, waits for them, and re-layouts: 4.91 us -> 0.37 us  [per_device(): jnp.stack([down_part.reshape(rows, batches, local_feat), normed_part.resh...]
  transfers between devices with their start and end apart: 2 -> 2, of which waited for: 2 -> 2; matrix products, arithmetic and copies ran while one was open for 4% -> 6% of each run, Pallas kernels for 0% -> 0%
where the time goes in v4:
time: 231 us
  waiting for transfers between devices  103 us (45%)
  blocking collectives  59.6 us (26%)
  matrix products  39.5 us (17%)
  between operations  14.2 us (6%)
  local copies, waits for them, and re-layouts  7.59 us (3%)
  other arithmetic  6.88 us (3%)
    psum x1, waiting for transfers between devices, per_device(): gate_sum, up_sum, back_sum = lax.psum(parts, 'dp')  94.3 us
    psum x1, blocking collectives, per_device(): d_gain = lax.psum(jnp.sum(normed_part * scaled_all, axis=0), 'tensor')  14.2 us
    psum x1, blocking collectives, per_device(): square_sum = lax.psum(jnp.sum(wide_inputs * wide_inputs, axis=2), 'dp')  13.5 us
    psum x1, blocking collectives, per_device(): row_product = lax.psum(row_part, 'dp')  11.6 us
    all_gather x1, blocking collectives, per_device(): both_all = lax.all_gather(both, 'tensor', axis=0, tiled=True)  11.2 us
    all_gather x1, blocking collectives, per_device(): row_scale_all = lax.all_gather(row_scale.T, 'tensor', axis=0, tiled=True)  9.07 us
    reduce_scatter x1, waiting for transfers between devices, per_device(): lax.psum_scatter(stacked, 'tensor', scatter_dimension=0, tiled=True)  8.45 us
    dot_general x1, matrix products, per_device(): lax.dot_general(gate_grad, gate_w, contract_cols, preferred_element_type=...  5.93 us
  transfers between devices with their start and end apart: 2, of which 2 were waited for; matrix products, arithmetic and copies ran while one was open for 6% of the time, Pallas kernels for 0%

profile of v4, /device:TPU:0, one launch (start us, length us, event | category | flops | bytes accessed | tf_op | source)
XLA Modules:
  0.0 230.7 jit_solution(6818898128641849798)
XLA Ops:
  8.1 13.5 %psum.42 = f32[4,4]{1,0:T(4,128)S(1)} all-reduce(f32[4,4]{1,0:T(4,128)S(1)} %fusion.12), channel_id=1, replica_groups=mesh['dp'=4,'tensor'=8] {'dp'}, use_global_device_ids=true, to_apply=%region_1.0 | all-reduce | flops 16 | bytes 128 | tf_op jit(solution)/shard_map/psum | solution.py:29
  23.3 11.2 %all_gather.6 = bf16[32,12,1024]{2,1,0:T(8,128)(2,1)S(1)} all-gather(bf16[4,12,1024]{2,1,0:T(8,128)(2,1)S(1)} %copy.28), channel_id=1, replica_groups=mesh['dp'=4,'tensor'=8] {'tensor'}, dimensions={0}, use_global_device_ids=true | all-gather | bytes 884736 | tf_op jit(solution)/shard_map/all_gather | solution.py:33
  34.5 1.2 fusion.29
  35.7 1.0 reshape.38
  36.7 1.7 reshape.39
  38.5 5.3 %convolution_convert_fusion.4 = bf16[128,3584]{1,0:T(8,128)(2,1)} fusion(bf16[128,1024]{1,0:T(8,128)(2,1)S(1)} %reshape.38, bf16[1024,3584]{1,0:T(8,128)(2,1)} %param.10), kind=kOutput, calls=%fused_computation.4 | convolution fusion | flops 939982848 | bytes 8519680 | tf_op jit(solution)/shard_map/dot_general | solution.py:57
  43.8 2.1 convolution_convert_fusion.5
  45.9 3.4 %convolution_convert_fusion.3 = bf16[128,3584]{1,0:T(8,128)(2,1)} fusion(bf16[128,1024]{1,0:T(8,128)(2,1)S(1)} %copy-done.1, bf16[3584,1024]{1,0:T(8,128)(2,1)S(1)} %bitcast.45), kind=kOutput, calls=%fused_computation.3 | convolution fusion | flops 939982848 | bytes 8519680 | tf_op jit(solution)/shard_map/dot_general | solution.py:58
  49.5 9.1 %all-gather = f32[8,4,4]{2,1,0:T(4,128)S(1)} all-gather(f32[1,4,4]{2,1,0:T(4,128)S(1)} %bitcast.54), channel_id=1, replica_groups=mesh['dp'=4,'tensor'=8] {'tensor'}, dimensions={0}, use_global_device_ids=true | all-gather | bytes 576 | tf_op jit(solution)/shard_map/all_gather | solution.py:37
  58.6 1.2 convert_multiply_fusion.5
  59.7 1.0 reshape.42
  60.8 94.3 %all-reduce.3.cloned.1.call-done = (bf16[128,3584]{1,0:T(8,128)(2,1)}, bf16[128,3584]{1,0:T(8,128)(2,1)}, bf16[128,3584]{1,0:T(8,128)(2,1)}) async-done(((bf16[128,3584]{1,0:T(8,128)(2,1)}, bf16[128,3584]{1,0:T(8,128)(2,1)}, bf16[128,3584]{1,0:T(8,128)(2,1)}), (bf16[128,3584]{1,0:T(8,128)(2,1)}, bf16[128,3584]{1,0:T(8,128)(2,1)}, bf16[128,3584]{1,0:T(8,128)(2,1)})) %all-reduce.3.cloned.1.call-update) | async-done | bytes 2752528 | tf_op jit(solution)/shard_map/psum | solution.py:68
  155.1 2.2 fusion.1
  157.4 5.9 %fusion.27 = f32[128,1024]{1,0:T(8,128)S(1)} fusion(bf16[1024,3584]{1,0:T(8,128)(2,1)} %param.9, bf16[128,3584]{1,0:T(8,128)(2,1)S(1)} %copy-done.3, bf16[128,3584]{1,0:T(8,128)(2,1)S(1)} %copy-done.11, bf16[128,3584]{1,0:T(8,128)(2,1)S(1)} %copy-done.4, f32[128]{0:T(128)S(1)} %mul.115), kind=kOutput, calls=%fused_computation.52 | convolution fusion | flops 945946624 | bytes 10617344 | tf_op jit(solution)/shard_map/dot_general | solution.py:80
  163.4 5.4 %convolution_convert_fusion.1 = bf16[1024,3584]{1,0:T(8,128)(2,1)} fusion(bf16[128,1024]{1,0:T(8,128)(2,1)S(1)} %reshape.38, bf16[128,3584]{1,0:T(8,128)(2,1)S(1)} %copy-done.11, f32[128]{0:T(128)S(1)} %mul.115, bf16[128,3584]{1,0:T(8,128)(2,1)S(1)} %copy-done.4), kind=kOutput, calls=%fused_computation.1 | convolution fusion | flops 947322880 | bytes 9437696 | tf_op jit(solution)/shard_map/dot_general | solution.py:113
  168.8 2.6 %multiply_reduce_fusion = (f32[1024]{0:T(1024)S(1)}, bf16[128,1024]{1,0:T(8,128)(2,1)S(1)}) fusion(f32[128,1024]{1,0:T(8,128)S(1)} %copy-done.7, f32[128,1024]{1,0:T(8,128)S(1)} %fusion.27, bf16[1024,3584]{1,0:T(8,128)(2,1)S(1)} %bitcast.49, bf16[128,3584]{1,0:T(8,128)(2,1)S(1)} %copy-done.11, f32[128]{0:T(128)S(1)} %mul.115, ...), kind=kOutput, calls=%fused_computation.27 | convolution fusion | flops 944176128 | bytes 10490368 | tf_op jit(solution)/shard_map/dot_general | solution.py:82
  171.5 4.2 %convolution_convert_fusion.6 = bf16[128,1024]{1,0:T(8,128)(2,1)S(1)} fusion(bf16[128,3584]{1,0:T(8,128)(2,1)S(1)} %fusion.1, bf16[3584,1024]{1,0:T(8,128)(2,1)} %param.11), kind=kOutput, calls=%fused_computation.25 | convolution fusion | flops 939655168 | bytes 8519680 | tf_op jit(solution)/shard_map/dot_general | solution.py:79
  176.0 1.1 copy.31
  177.1 14.2 %psum.47 = f32[1024]{0:T(1024)} all-reduce(f32[1024]{0:T(1024)S(1)} %get-tuple-element.23), channel_id=1, replica_groups=mesh['dp'=4,'tensor'=8] {'tensor'}, use_global_device_ids=true, to_apply=%region_9.0 | all-reduce | flops 1024 | bytes 8192 | tf_op jit(solution)/shard_map/psum | solution.py:98
  191.4 5.1 %convolution_convert_fusion = bf16[3584,1024]{1,0:T(8,128)(2,1)} fusion(bf16[128,3584]{1,0:T(8,128)(2,1)S(1)} %fusion.1, bf16[128,1024]{1,0:T(8,128)(2,1)S(1)} %copy-done.2), kind=kOutput, calls=%fused_computation | convolution fusion | flops 943194112 | bytes 8519680 | tf_op jit(solution)/shard_map/dot_general | solution.py:107
  196.5 5.4 %convolution_convert_fusion.2 = bf16[1024,3584]{1,0:T(8,128)(2,1)} fusion(bf16[128,1024]{1,0:T(8,128)(2,1)S(1)} %reshape.38, bf16[128,3584]{1,0:T(8,128)(2,1)S(1)} %copy-done.3, bf16[128,3584]{1,0:T(8,128)(2,1)S(1)} %copy-done.12, bf16[128,3584]{1,0:T(8,128)(2,1)S(1)} %copy-done.5, f32[128]{0:T(128)S(1)} %mul.115), kind=kOutput, calls=%fused_computation.2 | convolution fusion | flops 949616640 | bytes 10355200 | tf_op jit(solution)/shard_map/dot_general | solution.py:110
  202.0 8.4 %reduce-scatter.2.cloned.1.call-done = bf16[4,8,1024]{2,1,0:T(8,128)(2,1)} async-done(((bf16[32,8,1024]{2,1,0:T(8,128)(2,1)}), bf16[4,8,1024]{2,1,0:T(8,128)(2,1)}) %reduce-scatter.2.cloned.1.call-update) | async-done | bytes 65552 | tf_op jit(solution)/shard_map/reduce_scatter | solution.py:100
  210.4 0.9 copy.32
  211.4 11.6 %psum.46 = f32[4,4]{1,0:T(4,128)S(1)} all-reduce(f32[4,4]{1,0:T(4,128)S(1)} %fusion.16), channel_id=1, replica_groups=mesh['dp'=4,'tensor'=8] {'dp'}, use_global_device_ids=true, to_apply=%region_7.0 | all-reduce | flops 16 | bytes 128 | tf_op jit(solution)/shard_map/psum | solution.py:120
  (64 shorter events, 4.3 us)
Async XLA Ops:
  7.2 148.0 %all-reduce.3.cloned.1.call-start = ((), (), s32[]{:S(2)}) async-start(), calls=%async_computation.2 | async-start | bytes 5505024 | tf_op jit(solution)/shard_map/psum | solution.py:68
  23.3 20.5 %slice-start.2 = ((s8[7340032]{0:T(1024)(128)(4,1)}), s8[3145728]{0:T(1024)(128)(4,1)S(1)}, s32[]{:S(2)}) async-start(s8[7340032]{0:T(1024)(128)(4,1)} %bitcast.46), calls=%async_computation.5 | async-start | bytes 6291456
  34.5 1.2 copy-start
  38.5 5.3 %slice-start.3 = ((s8[7340032]{0:T(1024)(128)(4,1)}), s8[4194304]{0:T(1024)(128)(4,1)S(1)}, s32[]{:S(2)}) async-start(s8[7340032]{0:T(1024)(128)(4,1)} %bitcast.46), calls=%async_computation.6 | async-start | bytes 8388608
  38.5 7.4 %slice-start = ((s8[7340032]{0:T(1024)(128)(4,1)}), s8[4194304]{0:T(1024)(128)(4,1)S(1)}, s32[]{:S(2)}) async-start(s8[7340032]{0:T(1024)(128)(4,1)} %bitcast.44), calls=%async_computation.3 | async-start | bytes 8388608
  43.8 2.1 slice-start.1
  43.8 2.1 copy-start.1
  49.3 11.4 %copy-start.13 = (s32[4]{0:T(128)S(1)}, s32[4]{0:T(128)}, u32[]{:S(2)}) copy-start(s32[4]{0:T(128)} %param.13) | copy-start | bytes 52
  49.3 161.1 %reduce-scatter.2.cloned.1.call-start = ((), (), s32[]{:S(2)}) async-start(), calls=%async_computation.1 | async-start | bytes 589824 | tf_op jit(solution)/shard_map/reduce_scatter | solution.py:100
  155.1 2.3 copy-start.3
  155.1 2.3 copy-start.4
  155.1 2.3 copy-start.11
  155.1 13.6 %slice-start.4 = ((s8[7340032]{0:T(1024)(128)(4,1)}), s8[4194304]{0:T(1024)(128)(4,1)S(1)}, s32[]{:S(2)}) async-start(s8[7340032]{0:T(1024)(128)(4,1)} %bitcast.48), calls=%async_computation.7 | async-start | bytes 8388608
  157.4 11.3 %slice-start.5 = ((s8[7340032]{0:T(1024)(128)(4,1)}), s8[3145728]{0:T(1024)(128)(4,1)S(1)}, s32[]{:S(2)}) async-start(s8[7340032]{0:T(1024)(128)(4,1)} %bitcast.48), calls=%async_computation.8 | async-start | bytes 6291456
  163.4 5.4 %copy-start.7 = (f32[128,1024]{1,0:T(8,128)S(1)}, f32[128,1024]{1,0:T(8,128)}, u32[]{:S(2)}) copy-start(f32[128,1024]{1,0:T(8,128)} %reshape.42) | copy-start | bytes 1572868
  175.7 15.6 %copy-start.2 = (bf16[128,1024]{1,0:T(8,128)(2,1)S(1)}, bf16[128,1024]{1,0:T(8,128)(2,1)}, u32[]{:S(2)}) copy-start(bf16[128,1024]{1,0:T(8,128)(2,1)} %reshape.39) | copy-start | bytes 786436
  191.4 5.2 %copy-start.5 = (bf16[128,3584]{1,0:T(8,128)(2,1)S(1)}, bf16[128,3584]{1,0:T(8,128)(2,1)}, u32[]{:S(2)}) copy-start(bf16[128,3584]{1,0:T(8,128)(2,1)} %get-tuple-element.20) | copy-start | bytes 2752516
  191.4 5.2 %copy-start.12 = (bf16[128,3584]{1,0:T(8,128)(2,1)S(1)}, bf16[128,3584]{1,0:T(8,128)(2,1)}, u32[]{:S(2)}) copy-start(bf16[128,3584]{1,0:T(8,128)(2,1)} %get-tuple-element.19) | copy-start | bytes 2752516
  196.5 14.8 %copy-start.6 = (bf16[4,4,1024]{2,1,0:T(4,128)(2,1)S(1)}, bf16[4,4,1024]{2,1,0:T(4,128)(2,1)}, u32[]{:S(2)}) copy-start(bf16[4,4,1024]{2,1,0:T(4,128)(2,1)} %param.7) | copy-start | bytes 98308
  196.5 14.8 %copy-start.9 = (f32[1024]{0:T(1024)S(1)}, f32[1024]{0:T(1024)}, u32[]{:S(2)}) copy-start(f32[1024]{0:T(1024)} %param.8) | copy-start | bytes 12292
  196.5 26.6 %copy-start.8 = (bf16[4,4,1024]{2,1,0:T(4,128)(2,1)S(1)}, bf16[4,4,1024]{2,1,0:T(4,128)(2,1)}, u32[]{:S(2)}) copy-start(bf16[4,4,1024]{2,1,0:T(4,128)(2,1)} %param.12) | copy-start | bytes 98308
  223.1 0.7 copy-start.10
Sparse Core Ops, SparseCore 0:
  49.5 105.6 all-reduce.2
  177.2 33.1 reduce-scatter.1

commit v5 on v4

--- a/solution.py
+++ b/solution.py
@@ -36,6 +36,7 @@
     inputs_all = both_all[:, 2 * batches :].astype(jnp.float32)
     row_scale_all = lax.all_gather(row_scale.T, "tensor", axis=0, tiled=True)
     rows = normed_all.shape[0]
+    start = tensor_index * local_rows
 
     flat_normed = normed_all.reshape(rows * batches, local_feat)
     flat_grad = grad_all.reshape(rows * batches, local_feat)
@@ -95,7 +96,14 @@
     ).astype(jnp.bfloat16)
     stacked = stacked.reshape(rows, 2 * batches, local_feat)
     scaled_all = (inputs_all * row_scale_all[:, :, None]).reshape(rows * batches, local_feat)
-    d_gain = lax.psum(jnp.sum(normed_part * scaled_all, axis=0), "tensor")
+    gain_part = jnp.sum(normed_part * scaled_all, axis=0)
+    row_all = jnp.sum(
+        normed_part * (norm_gain * inputs_all.reshape(rows * batches, local_feat)), axis=1
+    )
+    reduced = lax.psum(jnp.concatenate([gain_part, row_all]), "tensor")
+    d_gain = reduced[:local_feat]
+    row_all = lax.psum(reduced[local_feat:], "dp").reshape(rows, batches)
+    row_product = lax.dynamic_slice_in_dim(row_all, start, local_rows, axis=0).T
     hidden, flat_grad, _ = lax.optimization_barrier((hidden, flat_grad, stacked))
     shares = lax.psum_scatter(stacked, "tensor", scatter_dimension=0, tiled=True).astype(
         jnp.float32
@@ -116,8 +124,6 @@
 
     wide_grad = d_output.astype(jnp.float32)
     weighted = norm_gain * normed_grad
-    row_part = jnp.sum(weighted * wide_inputs, axis=2)
-    row_product = lax.psum(row_part, "dp")
     outputs = (wide_inputs + down_output).astype(jnp.bfloat16)
     scale_cube = row_scale * row_scale * row_scale
     d_inputs = (

time: 231 us -> 225 us (0.974)
  waiting for transfers between devices: 103 us -> 93.3 us
    reduce_scatter x1, waiting for transfers between devices: 8.45 us -> 0.01 us  [per_device(): lax.psum_scatter(stacked, 'tensor', scatter_dimension=0, tiled=True)]
  transfers between devices with their start and end apart: 2 -> 2, of which waited for: 2 -> 1; matrix products, arithmetic and copies ran while one was open for 6% -> 7% of each run, Pallas kernels for 0% -> 0%
where the time goes in v5:
time: 225 us
  waiting for transfers between devices  93.3 us (41%)
  blocking collectives  57.7 us (26%)
  matrix products  41 us (18%)
  between operations  14.3 us (6%)
  local copies, waits for them, and re-layouts  9.66 us (4%)
  other arithmetic  8.66 us (4%)
    psum x1, waiting for transfers between devices, per_device(): gate_sum, up_sum, back_sum = lax.psum(parts, 'dp')  93.3 us
    psum x1, blocking collectives, per_device(): reduced = lax.psum(jnp.concatenate([gain_part, row_all]), 'tensor')  13.7 us
    psum x1, blocking collectives, per_device(): square_sum = lax.psum(jnp.sum(wide_inputs * wide_inputs, axis=2), 'dp')  13.5 us
    all_gather x1, blocking collectives, per_device(): both_all = lax.all_gather(both, 'tensor', axis=0, tiled=True)  11.2 us
    psum x1, blocking collectives, per_device(): row_all = lax.psum(reduced[local_feat:], 'dp').reshape(rows, batches)  10.2 us
    all_gather x1, blocking collectives, per_device(): row_scale_all = lax.all_gather(row_scale.T, 'tensor', axis=0, tiled=True)  9.07 us
    dot_general x1, matrix products, per_device(): lax.dot_general(flat_normed, gate_grad, contract_rows, preferred_element_...  6.87 us
    dot_general x1, matrix products, per_device(): lax.dot_general(gate_grad, gate_w, contract_cols, preferred_element_type=...  5.93 us
  transfers between devices with their start and end apart: 2, of which 1 were waited for; matrix products, arithmetic and copies ran while one was open for 7% of the time, Pallas kernels for 0%

profile of v5, /device:TPU:0, one launch (start us, length us, event | category | flops | bytes accessed | tf_op | source)
XLA Modules:
  0.0 224.7 jit_solution(1289460142888373839)
XLA Ops:
  8.9 13.5 %psum.42 = f32[4,4]{1,0:T(4,128)S(1)} all-reduce(f32[4,4]{1,0:T(4,128)S(1)} %fusion.12), channel_id=1, replica_groups=mesh['dp'=4,'tensor'=8] {'dp'}, use_global_device_ids=true, to_apply=%region_1.0 | all-reduce | flops 16 | bytes 128 | tf_op jit(solution)/shard_map/psum | solution.py:29
  24.8 11.2 %all_gather.6 = bf16[32,12,1024]{2,1,0:T(8,128)(2,1)S(1)} all-gather(bf16[4,12,1024]{2,1,0:T(8,128)(2,1)S(1)} %maximum_bitcast_fusion), channel_id=1, replica_groups=mesh['dp'=4,'tensor'=8] {'tensor'}, dimensions={0}, use_global_device_ids=true | all-gather | bytes 884736 | tf_op jit(solution)/shard_map/all_gather | solution.py:33
  36.0 1.3 slice_convert_fusion
  37.3 1.0 reshape.45
  38.3 1.7 reshape.46
  40.1 5.3 %convolution_convert_fusion.4 = bf16[128,3584]{1,0:T(8,128)(2,1)} fusion(bf16[128,1024]{1,0:T(8,128)(2,1)S(1)} %reshape.45, bf16[1024,3584]{1,0:T(8,128)(2,1)} %param.10), kind=kOutput, calls=%fused_computation.4 | convolution fusion | flops 939982848 | bytes 8519680 | tf_op jit(solution)/shard_map/dot_general | solution.py:58
  45.4 2.1 convolution_convert_fusion.5
  47.5 3.4 %convolution_convert_fusion.3 = bf16[128,3584]{1,0:T(8,128)(2,1)} fusion(bf16[128,1024]{1,0:T(8,128)(2,1)S(1)} %copy-done.1, bf16[3584,1024]{1,0:T(8,128)(2,1)S(1)} %bitcast.52), kind=kOutput, calls=%fused_computation.3 | convolution fusion | flops 939982848 | bytes 8519680 | tf_op jit(solution)/shard_map/dot_general | solution.py:59
  51.1 9.1 %all-gather = f32[8,4,4]{2,1,0:T(4,128)S(1)} all-gather(f32[1,4,4]{2,1,0:T(4,128)S(1)} %bitcast.60), channel_id=1, replica_groups=mesh['dp'=4,'tensor'=8] {'tensor'}, dimensions={0}, use_global_device_ids=true | all-gather | bytes 576 | tf_op jit(solution)/shard_map/all_gather | solution.py:37
  60.2 1.2 broadcast_multiply_fusion
  61.4 1.0 reshape.49
  62.3 1.0 reshape.50
  63.4 93.3 %all-reduce.3.cloned.1.call-done = (bf16[128,3584]{1,0:T(8,128)(2,1)}, bf16[128,3584]{1,0:T(8,128)(2,1)}, bf16[128,3584]{1,0:T(8,128)(2,1)}) async-done(((bf16[128,3584]{1,0:T(8,128)(2,1)}, bf16[128,3584]{1,0:T(8,128)(2,1)}, bf16[128,3584]{1,0:T(8,128)(2,1)}), (bf16[128,3584]{1,0:T(8,128)(2,1)}, bf16[128,3584]{1,0:T(8,128)(2,1)}, bf16[128,3584]{1,0:T(8,128)(2,1)})) %all-reduce.3.cloned.1.call-update) | async-done | bytes 2752528 | tf_op jit(solution)/shard_map/psum | solution.py:69
  156.7 2.2 fusion.1
  159.0 5.9 %fusion.27 = f32[128,1024]{1,0:T(8,128)S(1)} fusion(bf16[1024,3584]{1,0:T(8,128)(2,1)} %param.9, bf16[128,3584]{1,0:T(8,128)(2,1)S(1)} %copy-done.4, bf16[128,3584]{1,0:T(8,128)(2,1)S(1)} %copy-done.11, bf16[128,3584]{1,0:T(8,128)(2,1)S(1)} %copy-done.5, f32[128]{0:T(128)S(1)} %mul.126), kind=kOutput, calls=%fused_computation.56 | convolution fusion | flops 945946624 | bytes 10617344 | tf_op jit(solution)/shard_map/dot_general | solution.py:81
  165.0 5.4 %convolution_convert_fusion.1 = bf16[1024,3584]{1,0:T(8,128)(2,1)} fusion(bf16[128,1024]{1,0:T(8,128)(2,1)S(1)} %reshape.45, bf16[128,3584]{1,0:T(8,128)(2,1)S(1)} %copy-done.11, f32[128]{0:T(128)S(1)} %mul.126, bf16[128,3584]{1,0:T(8,128)(2,1)S(1)} %copy-done.5), kind=kOutput, calls=%fused_computation.1 | convolution fusion | flops 947322880 | bytes 9437696 | tf_op jit(solution)/shard_map/dot_general | solution.py:121
  170.4 2.7 %multiply_reduce_fusion.1 = (f32[1024]{0:T(1024)S(1)}, f32[128]{0:T(128)S(1)}, bf16[128,1024]{1,0:T(8,128)(2,1)S(1)}) fusion(f32[128,1024]{1,0:T(8,128)S(1)} %copy-done.7, f32[128,1024]{1,0:T(8,128)S(1)} %copy-done.8, f32[1024]{0:T(1024)S(1)} %copy-done.10, f32[128,1024]{1,0:T(8,128)S(1)} %fusion.27, bf16[1024,3584]{1,0:T(8,128)(2,1)S(1)} %bitcast.56, ...), kind=kOutput, calls=%fused_computation.28 | convolution fusion | flops 944569216 | bytes 11019264 | tf_op jit(solution)/shard_map/dot_general | solution.py:83
  173.3 4.2 %convolution_convert_fusion.6 = bf16[128,1024]{1,0:T(8,128)(2,1)S(1)} fusion(bf16[128,3584]{1,0:T(8,128)(2,1)S(1)} %fusion.1, bf16[3584,1024]{1,0:T(8,128)(2,1)} %param.11), kind=kOutput, calls=%fused_computation.25 | convolution fusion | flops 939655168 | bytes 8519680 | tf_op jit(solution)/shard_map/dot_general | solution.py:80
  177.8 1.1 copy.37
  178.9 5.1 %convolution_convert_fusion = bf16[3584,1024]{1,0:T(8,128)(2,1)} fusion(bf16[128,3584]{1,0:T(8,128)(2,1)S(1)} %fusion.1, bf16[128,1024]{1,0:T(8,128)(2,1)S(1)} %copy-done.2), kind=kOutput, calls=%fused_computation | convolution fusion | flops 943194112 | bytes 8519680 | tf_op jit(solution)/shard_map/dot_general | solution.py:115
  184.0 13.7 %psum.46 = f32[1152]{0:T(1024)S(1)} all-reduce(f32[1152]{0:T(1024)S(1)} %pad_maximum_fusion.1), channel_id=1, replica_groups=mesh['dp'=4,'tensor'=8] {'tensor'}, use_global_device_ids=true, to_apply=%region_8.0 | all-reduce | flops 1152 | bytes 9216 | tf_op jit(solution)/shard_map/psum | solution.py:103
  198.5 10.2 %psum.47 = f32[32,4]{0,1:T(4,128)S(1)} all-reduce(f32[32,4]{0,1:T(4,128)S(1)} %copy.42), channel_id=1, replica_groups=mesh['dp'=4,'tensor'=8] {'dp'}, use_global_device_ids=true, to_apply=%region_9.0 | all-reduce | flops 128 | bytes 1024 | tf_op jit(solution)/shard_map/psum | solution.py:105
  209.4 6.9 %convolution_convert_fusion.2 = bf16[1024,3584]{1,0:T(8,128)(2,1)} fusion(bf16[128,1024]{1,0:T(8,128)(2,1)S(1)} %reshape.45, bf16[128,3584]{1,0:T(8,128)(2,1)S(1)} %copy-done.4, bf16[128,3584]{1,0:T(8,128)(2,1)} %get-tuple-element.28, bf16[128,3584]{1,0:T(8,128)(2,1)} %get-tuple-element.29, f32[128]{0:T(128)S(1)} %mul.126), kind=kOutput, calls=%fused_computation.2 | convolution fusion | flops 949616640 | bytes 10355200 | tf_op jit(solution)/shard_map/dot_general | solution.py:118
  216.2 0.9 copy.38
  (69 shorter events, 7.0 us)
Async XLA Ops:
  7.2 149.6 %all-reduce.3.cloned.1.call-start = ((), (), s32[]{:S(2)}) async-start(), calls=%async_computation.2 | async-start | bytes 5505024 | tf_op jit(solution)/shard_map/psum | solution.py:69
  24.8 20.6 %slice-start.2 = ((s8[7340032]{0:T(1024)(128)(4,1)}), s8[3145728]{0:T(1024)(128)(4,1)S(1)}, s32[]{:S(2)}) async-start(s8[7340032]{0:T(1024)(128)(4,1)} %bitcast.53), calls=%async_computation.5 | async-start | bytes 6291456
  36.0 1.3 copy-start
  40.1 5.3 %slice-start.3 = ((s8[7340032]{0:T(1024)(128)(4,1)}), s8[4194304]{0:T(1024)(128)(4,1)S(1)}, s32[]{:S(2)}) async-start(s8[7340032]{0:T(1024)(128)(4,1)} %bitcast.53), calls=%async_computation.6 | async-start | bytes 8388608
  40.1 7.4 %slice-start = ((s8[7340032]{0:T(1024)(128)(4,1)}), s8[4194304]{0:T(1024)(128)(4,1)S(1)}, s32[]{:S(2)}) async-start(s8[7340032]{0:T(1024)(128)(4,1)} %bitcast.51), calls=%async_computation.3 | async-start | bytes 8388608
  45.4 2.1 slice-start.1
  45.4 2.1 copy-start.1
  50.9 11.4 %copy-start.3 = (f32[32,4,1024]{2,1,0:T(4,128)S(1)}, f32[32,4,1024]{2,1,0:T(4,128)}, u32[]{:S(2)}) copy-start(f32[32,4,1024]{2,1,0:T(4,128)} %get-tuple-element.32) | copy-start | bytes 1572868
  51.0 12.4 %copy-start.12 = (s32[4]{0:T(128)S(1)}, s32[4]{0:T(128)}, u32[]{:S(2)}) copy-start(s32[4]{0:T(128)} %param.13) | copy-start | bytes 52
  51.0 165.3 %reduce-scatter.2.cloned.1.call-start = ((), (), s32[]{:S(2)}) async-start(), calls=%async_computation.1 | async-start | bytes 589824 | tf_op jit(solution)/shard_map/reduce_scatter | solution.py:108
  156.7 2.3 %copy-start.4 = (bf16[128,3584]{1,0:T(8,128)(2,1)S(1)}, bf16[128,3584]{1,0:T(8,128)(2,1)}, u32[]{:S(2)}) copy-start(bf16[128,3584]{1,0:T(8,128)(2,1)} %get-tuple-element.27) | copy-start | bytes 2752516
  156.7 2.3 %copy-start.5 = (bf16[128,3584]{1,0:T(8,128)(2,1)S(1)}, bf16[128,3584]{1,0:T(8,128)(2,1)}, u32[]{:S(2)}) copy-start(bf16[128,3584]{1,0:T(8,128)(2,1)} %get-tuple-element.29) | copy-start | bytes 2752516
  156.7 2.3 %copy-start.11 = (bf16[128,3584]{1,0:T(8,128)(2,1)S(1)}, bf16[128,3584]{1,0:T(8,128)(2,1)}, u32[]{:S(2)}) copy-start(bf16[128,3584]{1,0:T(8,128)(2,1)} %get-tuple-element.28) | copy-start | bytes 2752516
  156.7 13.6 %slice-start.4 = ((s8[7340032]{0:T(1024)(128)(4,1)}), s8[4194304]{0:T(1024)(128)(4,1)S(1)}, s32[]{:S(2)}) async-start(s8[7340032]{0:T(1024)(128)(4,1)} %bitcast.55), calls=%async_computation.7 | async-start | bytes 8388608
  159.0 11.4 %slice-start.5 = ((s8[7340032]{0:T(1024)(128)(4,1)}), s8[3145728]{0:T(1024)(128)(4,1)S(1)}, s32[]{:S(2)}) async-start(s8[7340032]{0:T(1024)(128)(4,1)} %bitcast.55), calls=%async_computation.8 | async-start | bytes 6291456
  165.0 5.4 %copy-start.7 = (f32[128,1024]{1,0:T(8,128)S(1)}, f32[128,1024]{1,0:T(8,128)}, u32[]{:S(2)}) copy-start(f32[128,1024]{1,0:T(8,128)} %reshape.49) | copy-start | bytes 1572868
  165.0 5.4 %copy-start.8 = (f32[128,1024]{1,0:T(8,128)S(1)}, f32[128,1024]{1,0:T(8,128)}, u32[]{:S(2)}) copy-start(f32[128,1024]{1,0:T(8,128)} %reshape.50) | copy-start | bytes 1572868
  165.0 5.4 %copy-start.10 = (f32[1024]{0:T(1024)S(1)}, f32[1024]{0:T(1024)}, u32[]{:S(2)}) copy-start(f32[1024]{0:T(1024)} %param.8) | copy-start | bytes 12292
  177.5 1.4 copy-start.2
  209.4 7.8 %copy-start.6 = (bf16[4,4,1024]{2,1,0:T(4,128)(2,1)S(1)}, bf16[4,4,1024]{2,1,0:T(4,128)(2,1)}, u32[]{:S(2)}) copy-start(bf16[4,4,1024]{2,1,0:T(4,128)(2,1)} %param.7) | copy-start | bytes 98308
  209.4 7.8 %copy-start.9 = (bf16[4,4,1024]{2,1,0:T(4,128)(2,1)S(1)}, bf16[4,4,1024]{2,1,0:T(4,128)(2,1)}, u32[]{:S(2)}) copy-start(bf16[4,4,1024]{2,1,0:T(4,128)(2,1)} %param.12) | copy-start | bytes 98308
Sparse Core Ops, SparseCore 0:
  51.1 105.6 all-reduce.2
  179.0 33.1 reduce-scatter.1

commit v6 on v5

--- a/solution.py
+++ b/solution.py
@@ -74,6 +74,7 @@
             back_sum.astype(jnp.float32),
             active_mask,
         )
+        hidden, gate_grad, up_grad = lax.optimization_barrier((hidden, gate_grad, up_grad))
         hiddens.append(hidden)
         gate_grads.append(gate_grad)
         up_grads.append(up_grad)

time: 225 us -> 247 us (1.098)
  waiting for transfers between devices: 93.3 us -> 113 us
    reduce_scatter x1, waiting for transfers between devices: 0.01 us -> 19.6 us  [per_device(): lax.psum_scatter(stacked, 'tensor', scatter_dimension=0, tiled=True)]
  transfers between devices with their start and end apart: 2 -> 2, of which waited for: 1 -> 2; matrix products, arithmetic and copies ran while one was open for 7% -> 6% of each run, Pallas kernels for 0% -> 0%
where the time goes in v6:
time: 247 us; the launch traced here: 246 us
  waiting for transfers between devices  113 us (46%)
  blocking collectives  57.6 us (23%)
  matrix products  39.7 us (16%)
  between operations  14.3 us (6%)
  local copies, waits for them, and re-layouts  10.6 us (4%)
  other arithmetic  10.5 us (4%)
    psum x1, waiting for transfers between devices, per_device(): gate_sum, up_sum, back_sum = lax.psum(parts, 'dp')  93.5 us
    reduce_scatter x1, waiting for transfers between devices, per_device(): lax.psum_scatter(stacked, 'tensor', scatter_dimension=0, tiled=True)  19.6 us
    psum x1, blocking collectives, per_device(): reduced = lax.psum(jnp.concatenate([gain_part, row_all]), 'tensor')  13.9 us
    psum x1, blocking collectives, per_device(): square_sum = lax.psum(jnp.sum(wide_inputs * wide_inputs, axis=2), 'dp')  13.5 us
    all_gather x1, blocking collectives, per_device(): both_all = lax.all_gather(both, 'tensor', axis=0, tiled=True)  11.2 us
    psum x1, blocking collectives, per_device(): row_all = lax.psum(reduced[local_feat:], 'dp').reshape(rows, batches)  10.1 us
    all_gather x1, blocking collectives, per_device(): row_scale_all = lax.all_gather(row_scale.T, 'tensor', axis=0, tiled=True)  8.88 us
    dot_general x1, matrix products, per_device(): lax.dot_general(gate_grad, gate_w, contract_cols, preferred_element_type=...  5.66 us
  transfers between devices with their start and end apart: 2, of which 2 were waited for; matrix products, arithmetic and copies ran while one was open for 6% of the time, Pallas kernels for 0%

profile of v6, /device:TPU:0, one launch (start us, length us, event | category | flops | bytes accessed | tf_op | source)
XLA Modules:
  0.0 245.9 jit_solution(6306668113055835166)
XLA Ops:
  8.9 13.5 %psum.42 = f32[4,4]{1,0:T(4,128)S(1)} all-reduce(f32[4,4]{1,0:T(4,128)S(1)} %fusion.12), channel_id=1, replica_groups=mesh['dp'=4,'tensor'=8] {'dp'}, use_global_device_ids=true, to_apply=%region_1.0 | all-reduce | flops 16 | bytes 128 | tf_op jit(solution)/shard_map/psum | solution.py:29
  24.8 11.2 %all_gather.6 = bf16[32,12,1024]{2,1,0:T(8,128)(2,1)S(1)} all-gather(bf16[4,12,1024]{2,1,0:T(8,128)(2,1)S(1)} %maximum_bitcast_fusion), channel_id=1, replica_groups=mesh['dp'=4,'tensor'=8] {'tensor'}, dimensions={0}, use_global_device_ids=true | all-gather | bytes 884736 | tf_op jit(solution)/shard_map/all_gather | solution.py:33
  36.0 1.3 slice_convert_fusion
  37.3 1.0 reshape.45
  38.3 1.7 reshape.46
  40.1 5.3 %convolution_convert_fusion.4 = bf16[128,3584]{1,0:T(8,128)(2,1)} fusion(bf16[128,1024]{1,0:T(8,128)(2,1)S(1)} %reshape.45, bf16[1024,3584]{1,0:T(8,128)(2,1)} %param.10), kind=kOutput, calls=%fused_computation.4 | convolution fusion | flops 939982848 | bytes 8519680 | tf_op jit(solution)/shard_map/dot_general | solution.py:58
  45.4 2.1 convolution_convert_fusion.5
  47.5 3.5 %convolution_convert_fusion.3 = bf16[128,3584]{1,0:T(8,128)(2,1)} fusion(bf16[128,1024]{1,0:T(8,128)(2,1)S(1)} %copy-done.6, bf16[3584,1024]{1,0:T(8,128)(2,1)S(1)} %bitcast.56), kind=kOutput, calls=%fused_computation.3 | convolution fusion | flops 939982848 | bytes 8519680 | tf_op jit(solution)/shard_map/dot_general | solution.py:59
  51.2 8.9 %all-gather = f32[8,4,4]{2,1,0:T(4,128)S(1)} all-gather(f32[1,4,4]{2,1,0:T(4,128)S(1)} %bitcast.64), channel_id=1, replica_groups=mesh['dp'=4,'tensor'=8] {'tensor'}, dimensions={0}, use_global_device_ids=true | all-gather | bytes 576 | tf_op jit(solution)/shard_map/all_gather | solution.py:37
  60.1 1.2 broadcast_multiply_fusion
  61.3 1.0 reshape.49
  62.3 1.0 reshape.50
  63.3 93.5 %all-reduce.3.cloned.1.call-done = (bf16[128,3584]{1,0:T(8,128)(2,1)}, bf16[128,3584]{1,0:T(8,128)(2,1)}, bf16[128,3584]{1,0:T(8,128)(2,1)}) async-done(((bf16[128,3584]{1,0:T(8,128)(2,1)}, bf16[128,3584]{1,0:T(8,128)(2,1)}, bf16[128,3584]{1,0:T(8,128)(2,1)}), (bf16[128,3584]{1,0:T(8,128)(2,1)}, bf16[128,3584]{1,0:T(8,128)(2,1)}, bf16[128,3584]{1,0:T(8,128)(2,1)})) %all-reduce.3.cloned.1.call-update) | async-done | bytes 2752528 | tf_op jit(solution)/shard_map/psum | solution.py:69
  156.7 4.1 %fusion.6 = (bf16[128,3584]{1,0:T(8,128)(2,1)S(1)}, bf16[128,3584]{1,0:T(8,128)(2,1)S(1)}, bf16[128,3584]{1,0:T(8,128)(2,1)}) fusion(bf16[128,3584]{1,0:T(8,128)(2,1)} %get-tuple-element.35, f32[128]{0:T(128)S(1)} %mul.126, bf16[128,3584]{1,0:T(8,128)(2,1)} %get-tuple-element.34, bf16[128,3584]{1,0:T(8,128)(2,1)} %get-tuple-element.33), kind=kLoop, calls=%fused_computation.18 | loop fusion | flops 9633792 | bytes 5505536 | tf_op jit(solution)/shard_map/convert_element_type | solution.py:17
  161.7 5.7 %fusion.24 = f32[128,1024]{1,0:T(8,128)S(1)} fusion(bf16[128,3584]{1,0:T(8,128)(2,1)S(1)} %get-tuple-element.13, bf16[1024,3584]{1,0:T(8,128)(2,1)} %param.9), kind=kOutput, calls=%fused_computation.56 | convolution fusion | flops 939524096 | bytes 8781824 | tf_op jit(solution)/shard_map/dot_general | solution.py:82
  167.5 3.2 %multiply_reduce_fusion.1 = (f32[1024]{0:T(1024)S(1)}, f32[128]{0:T(128)S(1)}, bf16[128,1024]{1,0:T(8,128)(2,1)}) fusion(f32[128,1024]{1,0:T(8,128)S(1)} %copy-done.9, f32[128,1024]{1,0:T(8,128)S(1)} %copy-done.10, f32[1024]{0:T(1024)S(1)} %copy-done.14, f32[128,1024]{1,0:T(8,128)S(1)} %fusion.24, bf16[128,3584]{1,0:T(8,128)(2,1)S(1)} %get-tuple-element.14, ...), kind=kOutput, calls=%fused_computation.28 | convolution fusion | flops 940440448 | bytes 10101248 | tf_op jit(solution)/shard_map/dot_general | solution.py:84
  170.7 13.9 %psum.46 = f32[1152]{0:T(1024)S(1)} all-reduce(f32[1152]{0:T(1024)S(1)} %pad_maximum_fusion.1), channel_id=1, replica_groups=mesh['dp'=4,'tensor'=8] {'tensor'}, use_global_device_ids=true, to_apply=%region_8.0 | all-reduce | flops 1152 | bytes 9216 | tf_op jit(solution)/shard_map/psum | solution.py:104
  185.1 4.6 %convolution_convert_fusion.6 = bf16[128,1024]{1,0:T(8,128)(2,1)S(1)} fusion(bf16[128,3584]{1,0:T(8,128)(2,1)} %get-tuple-element.15, bf16[3584,1024]{1,0:T(8,128)(2,1)} %param.11), kind=kOutput, calls=%fused_computation.25 | convolution fusion | flops 939655168 | bytes 8519680 | tf_op jit(solution)/shard_map/dot_general | solution.py:81
  190.2 1.1 copy.37
  191.3 5.1 %convolution_convert_fusion.1 = bf16[1024,3584]{1,0:T(8,128)(2,1)} fusion(bf16[128,1024]{1,0:T(8,128)(2,1)S(1)} %reshape.45, bf16[128,3584]{1,0:T(8,128)(2,1)S(1)} %copy-done.4), kind=kOutput, calls=%fused_computation.1 | convolution fusion | flops 943194112 | bytes 8519680 | tf_op jit(solution)/shard_map/dot_general | solution.py:122
  196.7 10.1 %psum.47 = f32[32,4]{0,1:T(4,128)S(1)} all-reduce(f32[32,4]{0,1:T(4,128)S(1)} %copy.42), channel_id=1, replica_groups=mesh['dp'=4,'tensor'=8] {'dp'}, use_global_device_ids=true, to_apply=%region_9.0 | all-reduce | flops 128 | bytes 1024 | tf_op jit(solution)/shard_map/psum | solution.py:106
  207.5 5.1 %convolution_convert_fusion.2 = bf16[1024,3584]{1,0:T(8,128)(2,1)} fusion(bf16[128,1024]{1,0:T(8,128)(2,1)S(1)} %reshape.45, bf16[128,3584]{1,0:T(8,128)(2,1)S(1)} %copy-done.2), kind=kOutput, calls=%fused_computation.2 | convolution fusion | flops 943194112 | bytes 8519680 | tf_op jit(solution)/shard_map/dot_general | solution.py:119
  212.6 5.1 %convolution_convert_fusion = bf16[3584,1024]{1,0:T(8,128)(2,1)} fusion(bf16[128,3584]{1,0:T(8,128)(2,1)S(1)} %copy-done, bf16[128,1024]{1,0:T(8,128)(2,1)S(1)} %copy-done.7), kind=kOutput, calls=%fused_computation | convolution fusion | flops 943194112 | bytes 8519680 | tf_op jit(solution)/shard_map/dot_general | solution.py:116
  217.8 19.6 %reduce-scatter.2.cloned.1.call-done = bf16[4,8,1024]{2,1,0:T(8,128)(2,1)} async-done(((bf16[32,8,1024]{2,1,0:T(8,128)(2,1)}), bf16[4,8,1024]{2,1,0:T(8,128)(2,1)}) %reduce-scatter.2.cloned.1.call-update) | async-done | bytes 65552 | tf_op jit(solution)/shard_map/reduce_scatter | solution.py:109
  (78 shorter events, 8.9 us)
Async XLA Ops:
  7.2 149.6 %all-reduce.3.cloned.1.call-start = ((), (), s32[]{:S(2)}) async-start(), calls=%async_computation.2 | async-start | bytes 5505024 | tf_op jit(solution)/shard_map/psum | solution.py:69
  24.8 20.6 %slice-start.2 = ((s8[7340032]{0:T(1024)(128)(4,1)}), s8[3145728]{0:T(1024)(128)(4,1)S(1)}, s32[]{:S(2)}) async-start(s8[7340032]{0:T(1024)(128)(4,1)} %bitcast.57), calls=%async_computation.5 | async-start | bytes 6291456
  40.1 5.3 %slice-start.3 = ((s8[7340032]{0:T(1024)(128)(4,1)}), s8[4194304]{0:T(1024)(128)(4,1)S(1)}, s32[]{:S(2)}) async-start(s8[7340032]{0:T(1024)(128)(4,1)} %bitcast.57), calls=%async_computation.6 | async-start | bytes 8388608
  40.1 7.4 %slice-start = ((s8[7340032]{0:T(1024)(128)(4,1)}), s8[4194304]{0:T(1024)(128)(4,1)S(1)}, s32[]{:S(2)}) async-start(s8[7340032]{0:T(1024)(128)(4,1)} %bitcast.55), calls=%async_computation.3 | async-start | bytes 8388608
  45.4 2.1 slice-start.1
  45.4 2.1 copy-start.6
  47.5 3.7 %copy-start.16 = (s32[4]{0:T(128)S(1)}, s32[4]{0:T(128)}, u32[]{:S(2)}) copy-start(s32[4]{0:T(128)} %param.13) | copy-start | bytes 52
  47.5 14.8 %copy-start.8 = (f32[32,4,1024]{2,1,0:T(4,128)S(1)}, f32[32,4,1024]{2,1,0:T(4,128)}, u32[]{:S(2)}) copy-start(f32[32,4,1024]{2,1,0:T(4,128)} %get-tuple-element.41) | copy-start | bytes 1572868
  51.0 186.4 %reduce-scatter.2.cloned.1.call-start = ((), (), s32[]{:S(2)}) async-start(), calls=%async_computation.1 | async-start | bytes 589824 | tf_op jit(solution)/shard_map/reduce_scatter | solution.py:109
  63.3 104.1 %slice-start.4 = ((s8[7340032]{0:T(1024)(128)(4,1)}), s8[3145728]{0:T(1024)(128)(4,1)S(1)}, s32[]{:S(2)}) async-start(s8[7340032]{0:T(1024)(128)(4,1)} %bitcast.59), calls=%async_computation.7 | async-start | bytes 6291456
  63.3 104.2 %copy-start.14 = (f32[1024]{0:T(1024)S(1)}, f32[1024]{0:T(1024)}, u32[]{:S(2)}) copy-start(f32[1024]{0:T(1024)} %param.8) | copy-start | bytes 12292
  156.7 10.7 %copy-start.9 = (f32[128,1024]{1,0:T(8,128)S(1)}, f32[128,1024]{1,0:T(8,128)}, u32[]{:S(2)}) copy-start(f32[128,1024]{1,0:T(8,128)} %reshape.49) | copy-start | bytes 1572868
  156.7 10.7 %copy-start.10 = (f32[128,1024]{1,0:T(8,128)S(1)}, f32[128,1024]{1,0:T(8,128)}, u32[]{:S(2)}) copy-start(f32[128,1024]{1,0:T(8,128)} %reshape.50) | copy-start | bytes 1572868
  160.8 9.8 %copy-start.3 = (bf16[128,3584]{1,0:T(8,128)(2,1)}, bf16[128,3584]{1,0:T(8,128)(2,1)S(1)}, u32[]{:S(2)}) copy-start(bf16[128,3584]{1,0:T(8,128)(2,1)S(1)} %get-tuple-element.14) | copy-start | bytes 2752516
  161.7 5.7 %slice-start.5 = ((s8[7340032]{0:T(1024)(128)(4,1)}), s8[4194304]{0:T(1024)(128)(4,1)S(1)}, s32[]{:S(2)}) async-start(s8[7340032]{0:T(1024)(128)(4,1)} %bitcast.59), calls=%async_computation.8 | async-start | bytes 8388608
  184.5 5.2 %copy-start.15 = (f32[1152]{0:T(1024)}, f32[1152]{0:T(1024)S(1)}, u32[]{:S(2)}) copy-start(f32[1152]{0:T(1024)S(1)} %psum.46) | copy-start | bytes 13828
  185.1 4.8 %copy-start.11 = (bf16[128,1024]{1,0:T(8,128)(2,1)S(1)}, bf16[128,1024]{1,0:T(8,128)(2,1)}, u32[]{:S(2)}) copy-start(bf16[128,1024]{1,0:T(8,128)(2,1)} %get-tuple-element.44) | copy-start | bytes 786436
  185.1 6.2 %copy-start.4 = (bf16[128,3584]{1,0:T(8,128)(2,1)S(1)}, bf16[128,3584]{1,0:T(8,128)(2,1)}, u32[]{:S(2)}) copy-start(bf16[128,3584]{1,0:T(8,128)(2,1)} %copy-done.3) | copy-start | bytes 2752516
  189.8 6.6 %slice-start.6 = ((f32[1152]{0:T(1024)}), f32[128]{0:T(128)S(1)}, s32[]{:S(2)}) async-start(f32[1152]{0:T(1024)} %copy-done.15), calls=%async_computation.9 | async-start | bytes 1024 | tf_op jit(solution)/shard_map/slice | solution.py:106
  189.9 17.6 %copy-start.2 = (bf16[128,3584]{1,0:T(8,128)(2,1)S(1)}, bf16[128,3584]{1,0:T(8,128)(2,1)}, u32[]{:S(2)}) copy-start(bf16[128,3584]{1,0:T(8,128)(2,1)} %copy-done.1) | copy-start | bytes 2752516
  196.5 16.1 %copy-start = (bf16[128,3584]{1,0:T(8,128)(2,1)S(1)}, bf16[128,3584]{1,0:T(8,128)(2,1)}, u32[]{:S(2)}) copy-start(bf16[128,3584]{1,0:T(8,128)(2,1)} %get-tuple-element.15) | copy-start | bytes 2752516
  196.5 16.1 %copy-start.7 = (bf16[128,1024]{1,0:T(8,128)(2,1)S(1)}, bf16[128,1024]{1,0:T(8,128)(2,1)}, u32[]{:S(2)}) copy-start(bf16[128,1024]{1,0:T(8,128)(2,1)} %reshape.46) | copy-start | bytes 786436
  212.6 25.7 %copy-start.12 = (bf16[4,4,1024]{2,1,0:T(4,128)(2,1)S(1)}, bf16[4,4,1024]{2,1,0:T(4,128)(2,1)}, u32[]{:S(2)}) copy-start(bf16[4,4,1024]{2,1,0:T(4,128)(2,1)} %param.7) | copy-start | bytes 98308
  212.6 25.7 %copy-start.13 = (bf16[4,4,1024]{2,1,0:T(4,128)(2,1)S(1)}, bf16[4,4,1024]{2,1,0:T(4,128)(2,1)}, u32[]{:S(2)}) copy-start(bf16[4,4,1024]{2,1,0:T(4,128)(2,1)} %param.12) | copy-start | bytes 98308
  (2 other events, 2.2 us)
Sparse Core Ops, SparseCore 0:
  51.1 105.6 all-reduce.2
  206.9 30.4 reduce-scatter.1

commit v7 on v5

--- a/solution.py
+++ b/solution.py
@@ -26,20 +26,25 @@
     full_width = local_feat * lax.axis_size("dp")
     batches, local_rows, _ = inputs.shape
     wide_inputs = inputs.astype(jnp.float32)
-    square_sum = lax.psum(jnp.sum(wide_inputs * wide_inputs, axis=2), "dp")
-    row_scale = lax.rsqrt(square_sum / full_width + epsilon)
-    normed = (wide_inputs * row_scale[:, :, None] * norm_gain).astype(jnp.bfloat16)
-    both = jnp.concatenate([normed, d_output, inputs], axis=0).transpose(1, 0, 2)
+    both = jnp.concatenate([d_output, inputs], axis=0).transpose(1, 0, 2)
     both_all = lax.all_gather(both, "tensor", axis=0, tiled=True)
-    normed_all = both_all[:, :batches]
-    grad_all = both_all[:, batches : 2 * batches]
-    inputs_all = both_all[:, 2 * batches :].astype(jnp.float32)
-    row_scale_all = lax.all_gather(row_scale.T, "tensor", axis=0, tiled=True)
-    rows = normed_all.shape[0]
+    grad_all = both_all[:, :batches]
+    inputs_all = both_all[:, batches:].astype(jnp.float32)
+    rows = grad_all.shape[0]
     start = tensor_index * local_rows
+    flat_grad = grad_all.reshape(rows * batches, local_feat)
+    back_first = lax.psum(
+        lax.dot_general(
+            flat_grad, w_down, contract_cols, preferred_element_type=jnp.float32
+        ).astype(jnp.bfloat16),
+        "dp",
+    )
+    square_sum = lax.psum(jnp.sum(inputs_all * inputs_all, axis=2).T, "dp").T
+    row_scale_all = lax.rsqrt(square_sum / full_width + epsilon)
+    normed_all = (inputs_all * row_scale_all[:, :, None] * norm_gain).astype(jnp.bfloat16)
+    row_scale = lax.dynamic_slice_in_dim(row_scale_all, start, local_rows, axis=0).T
 
     flat_normed = normed_all.reshape(rows * batches, local_feat)
-    flat_grad = grad_all.reshape(rows * batches, local_feat)
     halvings = 3 - level_of_batch
     active = (tensor_index < jnp.right_shift(groups, halvings)).astype(jnp.float32)
     active_mask = jnp.tile(active, rows)[:, None]
@@ -48,7 +53,6 @@
     down_part = None
     normed_part = None
     hiddens, gate_grads, up_grads = [], [], []
-    previous = None
     for chunk in range(chunks):
         cols = slice(chunk * width, (chunk + 1) * width)
         gate_w = w_gate[:, cols]
@@ -56,18 +60,9 @@
         down_w = w_down[cols, :]
         gate_part = jnp.dot(flat_normed, gate_w, preferred_element_type=jnp.float32)
         up_part = jnp.dot(flat_normed, up_w, preferred_element_type=jnp.float32)
-        back_part = lax.dot_general(
-            flat_grad, down_w, contract_cols, preferred_element_type=jnp.float32
-        )
-        parts = (
-            gate_part.astype(jnp.bfloat16),
-            up_part.astype(jnp.bfloat16),
-            back_part.astype(jnp.bfloat16),
-        )
-        if previous is not None:
-            parts, _ = lax.optimization_barrier((parts, previous))
-        gate_sum, up_sum, back_sum = lax.psum(parts, "dp")
-        previous = (gate_sum, up_sum, back_sum)
+        parts = (gate_part.astype(jnp.bfloat16), up_part.astype(jnp.bfloat16))
+        parts, back_sum = lax.optimization_barrier((parts, back_first))
+        gate_sum, up_sum = lax.psum(parts, "dp")
         hidden, gate_grad, up_grad = local_terms(
             gate_sum.astype(jnp.float32),
             up_sum.astype(jnp.float32),

time: 225 us -> 224 us (level)
  waiting for transfers between devices: 93.3 us -> 105 us
  blocking collectives: 57.7 us -> 47.5 us
  matrix products: 41 us -> 44.1 us
  local copies, waits for them, and re-layouts: 9.66 us -> 6.61 us
  other arithmetic: 8.66 us -> 6.09 us
    psum x1 -> x2, waiting for transfers between devices: 93.3 us -> 105 us  [the longest x1 79 us: per_device(): gate_sum, up_sum = lax.psum(parts, 'dp')]
    all_gather x1 -> x0, blocking collectives: 9.07 us -> none  [per_device(): row_scale_all = lax.all_gather(row_scale.T, 'tensor', axis=0, tiled=True)]
    dot_general x1, matrix products: 2.08 us -> 5.35 us  [per_device(): gate_part = jnp.dot(flat_normed, gate_w, preferred_element_type=jnp.float32)]
    dot_general x1, matrix products: 5.29 us -> 2.07 us  [per_device(): up_part = jnp.dot(flat_normed, up_w, preferred_element_type=jnp.float32)]
    dot_general x1, matrix products: 3.45 us -> 6.65 us  [per_device(): lax.dot_general(flat_grad, w_down, contract_cols, preferred_element_type=...]
  transfers between devices with their start and end apart: 2 -> 3, of which waited for: 1 -> 2; matrix products, arithmetic and copies ran while one was open for 7% -> 11% of each run, Pallas kernels for 0% -> 0%
where the time goes in v7:
time: 224 us
  waiting for transfers between devices  105 us (47%)
  blocking collectives  47.5 us (21%)
  matrix products  44.1 us (20%)
  between operations  14 us (6%)
  local copies, waits for them, and re-layouts  6.61 us (3%)
  other arithmetic  6.09 us (3%)
    psum x1, waiting for transfers between devices, per_device(): gate_sum, up_sum = lax.psum(parts, 'dp')  79 us
    psum x1, waiting for transfers between devices, per_device(): lax.psum(lax.dot_general(flat_grad, w_down, contract_cols, preferred_elem...  25.9 us
    psum x1, blocking collectives, per_device(): reduced = lax.psum(jnp.concatenate([gain_part, row_all]), 'tensor')  12.8 us
    psum x1, blocking collectives, per_device(): square_sum = lax.psum(jnp.sum(inputs_all * inputs_all, axis=2).T, 'dp').T  12.2 us
    all_gather x1, blocking collectives, per_device(): both_all = lax.all_gather(both, 'tensor', axis=0, tiled=True)  11.3 us
    psum x1, blocking collectives, per_device(): row_all = lax.psum(reduced[local_feat:], 'dp').reshape(rows, batches)  11.2 us
    dot_general x1, matrix products, per_device(): lax.dot_general(flat_grad, w_down, contract_cols, preferred_element_type=...  6.65 us
    dot_general x1, matrix products, per_device(): lax.dot_general(flat_normed, gate_grad, contract_rows, preferred_element_...  6.6 us
  transfers between devices with their start and end apart: 3, of which 2 were waited for; matrix products, arithmetic and copies ran while one was open for 11% of the time, Pallas kernels for 0%

profile of v7, /device:TPU:0, one launch (start us, length us, event | category | flops | bytes accessed | tf_op | source)
XLA Modules:
  0.0 223.5 jit_solution(11046760997081748049)
XLA Ops:
  7.2 0.8 copy.31
  8.0 0.8 copy.30
  8.8 11.3 %all_gather.3 = bf16[32,8,1024]{2,1,0:T(8,128)(2,1)S(1)} all-gather(bf16[4,8,1024]{2,1,0:T(8,128)(2,1)S(1)} %maximum_bitcast_fusion), channel_id=1, replica_groups=mesh['dp'=4,'tensor'=8] {'tensor'}, dimensions={0}, use_global_device_ids=true | all-gather | bytes 589824 | tf_op jit(solution)/shard_map/all_gather | solution.py:30
  20.2 1.0 slice_convert_fusion
  21.2 6.7 %convolution_convert_fusion.3 = bf16[128,3584]{1,0:T(8,128)(2,1)} fusion(bf16[128,1024]{1,0:T(8,128)(2,1)S(1)} %reshape.46, bf16[3584,1024]{1,0:T(8,128)(2,1)} %param.11), kind=kOutput, calls=%fused_computation.3 | convolution fusion | flops 939982848 | bytes 8519680 | tf_op jit(solution)/shard_map/dot_general | solution.py:37
  28.3 12.2 %psum.42 = f32[4,32]{1,0:T(4,128)S(1)} all-reduce(f32[4,32]{1,0:T(4,128)S(1)} %bitcast.56), channel_id=1, replica_groups=mesh['dp'=4,'tensor'=8] {'dp'}, use_global_device_ids=true, to_apply=%region_1.0 | all-reduce | flops 128 | bytes 1024 | tf_op jit(solution)/shard_map/psum | solution.py:42
  40.7 1.1 broadcast_multiply_fusion
  41.8 1.2 reshape.45
  43.0 5.3 %convolution_convert_fusion.5 = bf16[128,3584]{1,0:T(8,128)(2,1)} fusion(bf16[128,1024]{1,0:T(8,128)(2,1)S(1)} %reshape.45, bf16[1024,3584]{1,0:T(8,128)(2,1)} %param.9), kind=kOutput, calls=%fused_computation.5 | convolution fusion | flops 939982848 | bytes 8519680 | tf_op jit(solution)/shard_map/dot_general | solution.py:61
  48.3 2.1 convolution_convert_fusion.4
  50.4 25.9 %all-reduce.4.cloned.1.call-done = bf16[128,3584]{1,0:T(8,128)(2,1)} async-done(((bf16[128,3584]{1,0:T(8,128)(2,1)}), bf16[128,3584]{1,0:T(8,128)(2,1)}) %all-reduce.4.cloned.1.call-update) | async-done | bytes 917520 | tf_op jit(solution)/shard_map/psum | solution.py:36
  77.0 79.0 %all-reduce.6.cloned.1.call-done = (bf16[128,3584]{1,0:T(8,128)(2,1)}, bf16[128,3584]{1,0:T(8,128)(2,1)}) async-done(((bf16[128,3584]{1,0:T(8,128)(2,1)}, bf16[128,3584]{1,0:T(8,128)(2,1)}), (bf16[128,3584]{1,0:T(8,128)(2,1)}, bf16[128,3584]{1,0:T(8,128)(2,1)})) %all-reduce.6.cloned.1.call-update) | async-done | bytes 1835024 | tf_op jit(solution)/shard_map/psum | solution.py:65
  156.0 2.2 %fusion.1 = bf16[128,3584]{1,0:T(8,128)(2,1)S(1)} fusion(bf16[128,3584]{1,0:T(8,128)(2,1)} %get-tuple-element.33, f32[128]{0:T(128)S(1)} %mul.126, bf16[128,3584]{1,0:T(8,128)(2,1)} %get-tuple-element.34), kind=kLoop, calls=%fused_computation.13 | loop fusion | flops 4128768 | bytes 2753024 | tf_op jit(solution)/shard_map/convert_element_type | solution.py:15
  158.3 6.0 %fusion.25 = f32[128,1024]{1,0:T(8,128)S(1)} fusion(bf16[1024,3584]{1,0:T(8,128)(2,1)} %param.9, bf16[128,3584]{1,0:T(8,128)(2,1)S(1)} %copy-done.4, bf16[128,3584]{1,0:T(8,128)(2,1)} %all-reduce.4.cloned.1.call-done, bf16[128,3584]{1,0:T(8,128)(2,1)S(1)} %copy-done.5, f32[128]{0:T(128)S(1)} %mul.126), kind=kOutput, calls=%fused_computation.54 | convolution fusion | flops 945946624 | bytes 10617344 | tf_op jit(solution)/shard_map/dot_general | solution.py:76
  164.4 5.4 %convolution_convert_fusion.1 = bf16[1024,3584]{1,0:T(8,128)(2,1)} fusion(bf16[128,1024]{1,0:T(8,128)(2,1)S(1)} %reshape.45, bf16[128,3584]{1,0:T(8,128)(2,1)S(1)} %copy-done.10, f32[128]{0:T(128)S(1)} %mul.126, bf16[128,3584]{1,0:T(8,128)(2,1)S(1)} %copy-done.5), kind=kOutput, calls=%fused_computation.1 | convolution fusion | flops 947322880 | bytes 9437696 | tf_op jit(solution)/shard_map/dot_general | solution.py:116
  169.7 2.7 %multiply_reduce_fusion.1 = (f32[1024]{0:T(1024)S(1)}, f32[128]{0:T(128)S(1)}, bf16[128,1024]{1,0:T(8,128)(2,1)S(1)}) fusion(f32[128,1024]{1,0:T(8,128)S(1)} %reshape.49, f32[128,1024]{1,0:T(8,128)S(1)} %reshape.50, f32[1024]{0:T(1024)S(1)} %copy-done.9, f32[128,1024]{1,0:T(8,128)S(1)} %fusion.25, bf16[1024,3584]{1,0:T(8,128)(2,1)S(1)} %bitcast.53, ...), kind=kOutput, calls=%fused_computation.28 | convolution fusion | flops 944569216 | bytes 11019264 | tf_op jit(solution)/shard_map/dot_general | solution.py:78
  172.6 4.2 %convolution_convert_fusion.6 = bf16[128,1024]{1,0:T(8,128)(2,1)S(1)} fusion(bf16[128,3584]{1,0:T(8,128)(2,1)S(1)} %fusion.1, bf16[3584,1024]{1,0:T(8,128)(2,1)} %param.11), kind=kOutput, calls=%fused_computation.25 | convolution fusion | flops 939655168 | bytes 8519680 | tf_op jit(solution)/shard_map/dot_general | solution.py:75
  177.1 1.1 copy.36
  178.2 5.1 %convolution_convert_fusion = bf16[3584,1024]{1,0:T(8,128)(2,1)} fusion(bf16[128,3584]{1,0:T(8,128)(2,1)S(1)} %fusion.1, bf16[128,1024]{1,0:T(8,128)(2,1)S(1)} %copy-done.1), kind=kOutput, calls=%fused_computation | convolution fusion | flops 943194112 | bytes 8519680 | tf_op jit(solution)/shard_map/dot_general | solution.py:110
  183.4 12.8 %psum.46 = f32[1152]{0:T(1024)S(1)} all-reduce(f32[1152]{0:T(1024)S(1)} %pad_maximum_fusion.1), channel_id=1, replica_groups=mesh['dp'=4,'tensor'=8] {'tensor'}, use_global_device_ids=true, to_apply=%region_8.0 | all-reduce | flops 1152 | bytes 9216 | tf_op jit(solution)/shard_map/psum | solution.py:98
  196.9 11.2 %psum.47 = f32[32,4]{0,1:T(4,128)S(1)} all-reduce(f32[32,4]{0,1:T(4,128)S(1)} %copy.39), channel_id=1, replica_groups=mesh['dp'=4,'tensor'=8] {'dp'}, use_global_device_ids=true, to_apply=%region_9.0 | all-reduce | flops 128 | bytes 1024 | tf_op jit(solution)/shard_map/psum | solution.py:100
  208.8 6.6 %convolution_convert_fusion.2 = bf16[1024,3584]{1,0:T(8,128)(2,1)} fusion(bf16[128,1024]{1,0:T(8,128)(2,1)S(1)} %reshape.45, bf16[128,3584]{1,0:T(8,128)(2,1)S(1)} %copy-done.4, bf16[128,3584]{1,0:T(8,128)(2,1)} %all-reduce.4.cloned.1.call-done, bf16[128,3584]{1,0:T(8,128)(2,1)S(1)} %copy-done.6, f32[128]{0:T(128)S(1)} %mul.126), kind=kOutput, calls=%fused_computation.2 | convolution fusion | flops 949616640 | bytes 10355200 | tf_op jit(solution)/shard_map/dot_general | solution.py:113
  215.4 0.9 copy.40
  216.3 0.7 fusion.14
  (63 shorter events, 3.3 us)
Async XLA Ops:
  7.2 69.1 %all-reduce.4.cloned.1.call-start = ((), (), s32[]{:S(2)}) async-start(), calls=%async_computation.1 | async-start | bytes 1835008 | tf_op jit(solution)/shard_map/psum | solution.py:36
  21.2 6.7 %copy-start = (bf16[128,1024]{1,0:T(8,128)(2,1)}, bf16[128,1024]{1,0:T(8,128)(2,1)S(1)}, u32[]{:S(2)}) copy-start(bf16[128,1024]{1,0:T(8,128)(2,1)S(1)} %reshape.46) | copy-start | bytes 786436
  21.2 19.5 %copy-start.9 = (f32[1024]{0:T(1024)S(1)}, f32[1024]{0:T(1024)}, u32[]{:S(2)}) copy-start(f32[1024]{0:T(1024)} %param.8) | copy-start | bytes 12292
  27.9 128.1 %all-reduce.6.cloned.1.call-start = ((), (), s32[]{:S(2)}) async-start(), calls=%async_computation.3 | async-start | bytes 3670016 | tf_op jit(solution)/shard_map/psum | solution.py:65
  41.8 6.5 %slice-start = ((s8[7340032]{0:T(1024)(128)(4,1)}), s8[3145728]{0:T(1024)(128)(4,1)S(1)}, s32[]{:S(2)}) async-start(s8[7340032]{0:T(1024)(128)(4,1)} %bitcast.50), calls=%async_computation.4 | async-start | bytes 6291456
  42.9 5.4 %slice-start.1 = ((s8[7340032]{0:T(1024)(128)(4,1)}), s8[4194304]{0:T(1024)(128)(4,1)S(1)}, s32[]{:S(2)}) async-start(s8[7340032]{0:T(1024)(128)(4,1)} %bitcast.50), calls=%async_computation.5 | async-start | bytes 8388608
  50.4 26.1 %copy-start.3 = (f32[32,4,1024]{2,1,0:T(4,128)S(1)}, f32[32,4,1024]{2,1,0:T(4,128)}, u32[]{:S(2)}) copy-start(f32[32,4,1024]{2,1,0:T(4,128)} %get-tuple-element.38) | copy-start | bytes 1572868
  50.4 26.3 %copy-start.2 = (f32[32,4,1024]{2,1,0:T(4,128)S(1)}, f32[32,4,1024]{2,1,0:T(4,128)}, u32[]{:S(2)}) copy-start(f32[32,4,1024]{2,1,0:T(4,128)} %get-tuple-element.41) | copy-start | bytes 1572868
  50.4 26.5 %copy-start.11 = (s32[4]{0:T(128)S(1)}, s32[4]{0:T(128)}, u32[]{:S(2)}) copy-start(s32[4]{0:T(128)} %param.13) | copy-start | bytes 52
  76.3 139.1 %reduce-scatter.2.cloned.1.call-start = ((), (), s32[]{:S(2)}) async-start(), calls=%async_computation.2 | async-start | bytes 589824 | tf_op jit(solution)/shard_map/reduce_scatter | solution.py:103
  156.0 2.3 %copy-start.4 = (bf16[128,3584]{1,0:T(8,128)(2,1)S(1)}, bf16[128,3584]{1,0:T(8,128)(2,1)}, u32[]{:S(2)}) copy-start(bf16[128,3584]{1,0:T(8,128)(2,1)} %get-tuple-element.33) | copy-start | bytes 2752516
  156.0 2.3 %copy-start.5 = (bf16[128,3584]{1,0:T(8,128)(2,1)S(1)}, bf16[128,3584]{1,0:T(8,128)(2,1)}, u32[]{:S(2)}) copy-start(bf16[128,3584]{1,0:T(8,128)(2,1)} %get-tuple-element.34) | copy-start | bytes 2752516
  156.0 13.7 %slice-start.2 = ((s8[7340032]{0:T(1024)(128)(4,1)}), s8[4194304]{0:T(1024)(128)(4,1)S(1)}, s32[]{:S(2)}) async-start(s8[7340032]{0:T(1024)(128)(4,1)} %bitcast.52), calls=%async_computation.6 | async-start | bytes 8388608
  158.3 6.1 %copy-start.10 = (bf16[128,3584]{1,0:T(8,128)(2,1)S(1)}, bf16[128,3584]{1,0:T(8,128)(2,1)}, u32[]{:S(2)}) copy-start(bf16[128,3584]{1,0:T(8,128)(2,1)} %all-reduce.4.cloned.1.call-done) | copy-start | bytes 2752516
  158.3 11.5 %slice-start.3 = ((s8[7340032]{0:T(1024)(128)(4,1)}), s8[3145728]{0:T(1024)(128)(4,1)S(1)}, s32[]{:S(2)}) async-start(s8[7340032]{0:T(1024)(128)(4,1)} %bitcast.52), calls=%async_computation.7 | async-start | bytes 6291456
  176.8 1.4 copy-start.1
  178.2 30.6 %copy-start.6 = (bf16[128,3584]{1,0:T(8,128)(2,1)S(1)}, bf16[128,3584]{1,0:T(8,128)(2,1)}, u32[]{:S(2)}) copy-start(bf16[128,3584]{1,0:T(8,128)(2,1)} %get-tuple-element.34) | copy-start | bytes 2752516
  208.8 7.5 %copy-start.7 = (bf16[4,4,1024]{2,1,0:T(4,128)(2,1)S(1)}, bf16[4,4,1024]{2,1,0:T(4,128)(2,1)}, u32[]{:S(2)}) copy-start(bf16[4,4,1024]{2,1,0:T(4,128)(2,1)} %param.7) | copy-start | bytes 98308
  208.8 7.5 %copy-start.8 = (bf16[4,4,1024]{2,1,0:T(4,128)(2,1)S(1)}, bf16[4,4,1024]{2,1,0:T(4,128)(2,1)}, u32[]{:S(2)}) copy-start(bf16[4,4,1024]{2,1,0:T(4,128)(2,1)} %param.12) | copy-start | bytes 98308
Sparse Core Ops, SparseCore 0:
  28.0 48.1 all-reduce.3
  79.2 76.7 all-reduce.5
  178.3 33.1 reduce-scatter.1

commit v8 on v7

--- a/solution.py
+++ b/solution.py
@@ -1,6 +1,7 @@
 import jax
 import jax.numpy as jnp
 from jax import lax
+from jax.experimental import pallas as pl
 from jax.sharding import PartitionSpec as P
 
 epsilon = 1e-05
@@ -16,6 +17,45 @@
     gate_grad = (back_sum * up_sum * slope * active_mask).astype(jnp.bfloat16)
     up_grad = (back_sum * silu_gate * active_mask).astype(jnp.bfloat16)
     return (hidden, gate_grad, up_grad)
+
+
+def outer_kernel(left_ref, right_ref, out_ref):
+    out_ref[...] = lax.dot_general(
+        left_ref[...], right_ref[...], contract_rows, preferred_element_type=jnp.float32
+    ).astype(out_ref.dtype)
+
+
+def outer_product(left, right):
+    depth, m = left.shape
+    n = right.shape[1]
+    if n >= m:
+        tile = n // 2 if n % 256 == 0 else n
+        grid = (n // tile,)
+        in_specs = [
+            pl.BlockSpec((depth, m), lambda j: (0, 0)),
+            pl.BlockSpec((depth, tile), lambda j: (0, j)),
+        ]
+        out_specs = pl.BlockSpec((m, tile), lambda j: (0, j))
+    else:
+        tile = m // 2 if m % 256 == 0 else m
+        grid = (m // tile,)
+        in_specs = [
+            pl.BlockSpec((depth, tile), lambda i: (0, i)),
+            pl.BlockSpec((depth, n), lambda i: (0, 0)),
+        ]
+        out_specs = pl.BlockSpec((tile, n), lambda i: (i, 0))
+    return pl.pallas_call(
+        outer_kernel,
+        grid=grid,
+        in_specs=in_specs,
+        out_specs=out_specs,
+        out_shape=jax.ShapeDtypeStruct((m, n), jnp.bfloat16),
+        cost_estimate=pl.CostEstimate(
+            flops=2 * depth * m * n,
+            bytes_accessed=2 * (depth * m + depth * n + m * n),
+            transcendentals=0,
+        ),
+    )(left, right)
 
 
 def per_device(inputs, norm_gain, w_gate, w_up, w_down, d_output, level_of_batch):
@@ -107,15 +147,9 @@
     down_output = shares[:, 0].transpose(1, 0, 2)
     normed_grad = shares[:, 1].transpose(1, 0, 2)
 
-    down_out = lax.dot_general(
-        hidden, flat_grad, contract_rows, preferred_element_type=jnp.float32
-    ).astype(jnp.bfloat16)
-    gate_out = lax.dot_general(
-        flat_normed, gate_grad, contract_rows, preferred_element_type=jnp.float32
-    ).astype(jnp.bfloat16)
-    up_out = lax.dot_general(
-        flat_normed, up_grad, contract_rows, preferred_element_type=jnp.float32
-    ).astype(jnp.bfloat16)
+    down_out = outer_product(hidden, flat_grad)
+    gate_out = outer_product(flat_normed, gate_grad)
+    up_out = outer_product(flat_normed, up_grad)
 
     wide_grad = d_output.astype(jnp.float32)
     weighted = norm_gain * normed_grad

time: 224 us -> 229 us (1.022)
  Pallas kernels: 0 us -> 15.9 us
  matrix products: 44.1 us -> 30.4 us
  local copies, waits for them, and re-layouts: 6.61 us -> 11.2 us
  waiting for transfers between devices: 105 us -> 102 us
    dot_general x3 -> x0, matrix products: 17.1 us -> none  [the longest x1 6.6 us: per_device(): lax.dot_general(flat_normed, gate_grad, contract_rows, preferred_element_...]
    pallas_call x0 -> x3, Pallas kernels: none -> 15.9 us  [outer_product(): pl.pallas_call(outer_kernel, grid=grid, in_specs=in_specs, out_specs=out_...]
    dot_general x1, matrix products: 5.35 us -> 2.06 us  [per_device(): gate_part = jnp.dot(flat_normed, gate_w, preferred_element_type=jnp.float32)]
    dot_general x1, matrix products: 2.07 us -> 5.35 us  [per_device(): up_part = jnp.dot(flat_normed, up_w, preferred_element_type=jnp.float32)]
    dot_general x1, matrix products: 2.65 us -> 5.66 us  [per_device(): lax.dot_general(up_grad, up_w, contract_cols, preferred_element_type=jnp....]
    psum x1, waiting for transfers between devices: 79 us -> 76.3 us  [per_device(): gate_sum, up_sum = lax.psum(parts, 'dp')]
  transfers between devices with their start and end apart: 3 -> 3, of which waited for: 2 -> 2; matrix products, arithmetic and copies ran while one was open for 11% -> 7% of each run, Pallas kernels for 0% -> 7%
where the time goes in v8:
time: 229 us; the launch traced here: 228 us
  waiting for transfers between devices  102 us (45%)
  blocking collectives  47.5 us (21%)
  matrix products  30.4 us (13%)
  Pallas kernels  15.9 us (7%)
  between operations  14 us (6%)
  local copies, waits for them, and re-layouts  11.2 us (5%)
  other arithmetic  6.9 us (3%)
    psum x1, waiting for transfers between devices, per_device(): gate_sum, up_sum = lax.psum(parts, 'dp')  76.3 us
    psum x1, waiting for transfers between devices, per_device(): lax.psum(lax.dot_general(flat_grad, w_down, contract_cols, preferred_elem...  25.9 us
    pallas_call x3, Pallas kernels, outer_product(): pl.pallas_call(outer_kernel, grid=grid, in_specs=in_specs, out_specs=out_...  15.9 us
    psum x1, blocking collectives, per_device(): reduced = lax.psum(jnp.concatenate([gain_part, row_all]), 'tensor')  13 us
    psum x1, blocking collectives, per_device(): square_sum = lax.psum(jnp.sum(inputs_all * inputs_all, axis=2).T, 'dp').T  12.3 us
    all_gather x1, blocking collectives, per_device(): both_all = lax.all_gather(both, 'tensor', axis=0, tiled=True)  11.3 us
    psum x1, blocking collectives, per_device(): row_all = lax.psum(reduced[local_feat:], 'dp').reshape(rows, batches)  11 us
    dot_general x1, matrix products, per_device(): lax.dot_general(flat_grad, w_down, contract_cols, preferred_element_type=...  6.65 us
  transfers between devices with their start and end apart: 3, of which 2 were waited for; matrix products, arithmetic and copies ran while one was open for 7% of the time, Pallas kernels for 7%

profile of v8, /device:TPU:0, one launch (start us, length us, event | category | flops | bytes accessed | tf_op | source)
XLA Modules:
  0.0 228.2 jit_solution(10342101635687896860)
XLA Ops:
  8.8 11.3 %all_gather.3 = bf16[32,8,1024]{2,1,0:T(8,128)(2,1)S(1)} all-gather(bf16[4,8,1024]{2,1,0:T(8,128)(2,1)S(1)} %maximum_bitcast_fusion), channel_id=1, replica_groups=mesh['dp'=4,'tensor'=8] {'tensor'}, dimensions={0}, use_global_device_ids=true | all-gather | bytes 589824 | tf_op jit(solution)/shard_map/all_gather | solution.py:70
  20.2 1.0 slice_convert_fusion
  21.2 6.6 %convolution_convert_fusion = bf16[128,3584]{1,0:T(8,128)(2,1)} fusion(bf16[128,1024]{1,0:T(8,128)(2,1)S(1)} %reshape.46.right_ref, bf16[3584,1024]{1,0:T(8,128)(2,1)} %param.11), kind=kOutput, calls=%fused_computation | convolution fusion | flops 939982848 | bytes 8519680 | tf_op jit(solution)/shard_map/dot_general | solution.py:77
  28.3 12.3 %psum.42 = f32[4,32]{1,0:T(4,128)S(1)} all-reduce(f32[4,32]{1,0:T(4,128)S(1)} %bitcast.52), channel_id=1, replica_groups=mesh['dp'=4,'tensor'=8] {'dp'}, use_global_device_ids=true, to_apply=%region_1.0 | all-reduce | flops 128 | bytes 1024 | tf_op jit(solution)/shard_map/psum | solution.py:82
  40.7 1.1 broadcast_multiply_fusion
  41.8 1.2 reshape.45.left_ref
  43.0 5.3 %convolution_convert_fusion.1 = bf16[128,3584]{1,0:T(8,128)(2,1)} fusion(bf16[128,1024]{1,0:T(8,128)(2,1)S(1)} %reshape.45.left_ref, bf16[1024,3584]{1,0:T(8,128)(2,1)} %param.10), kind=kOutput, calls=%fused_computation.1 | convolution fusion | flops 939982848 | bytes 8519680 | tf_op jit(solution)/shard_map/dot_general | solution.py:102
  48.3 2.1 convolution_convert_fusion.2
  50.4 25.9 %all-reduce.4.cloned.1.call-done = bf16[128,3584]{1,0:T(8,128)(2,1)} async-done(((bf16[128,3584]{1,0:T(8,128)(2,1)}), bf16[128,3584]{1,0:T(8,128)(2,1)}) %all-reduce.4.cloned.1.call-update) | async-done | bytes 917520 | tf_op jit(solution)/shard_map/psum | solution.py:76
  76.5 1.2 reshape.49
  77.7 2.0 reshape.50
  79.7 76.3 %all-reduce.6.cloned.1.call-done = (bf16[128,3584]{1,0:T(8,128)(2,1)}, bf16[128,3584]{1,0:T(8,128)(2,1)}) async-done(((bf16[128,3584]{1,0:T(8,128)(2,1)}, bf16[128,3584]{1,0:T(8,128)(2,1)}), (bf16[128,3584]{1,0:T(8,128)(2,1)}, bf16[128,3584]{1,0:T(8,128)(2,1)})) %all-reduce.6.cloned.1.call-update) | async-done | bytes 1835024 | tf_op jit(solution)/shard_map/psum | solution.py:105
  156.0 3.0 %fusion.1 = (bf16[128,3584]{1,0:T(8,128)(2,1)S(1)}, bf16[128,3584]{1,0:T(8,128)(2,1)S(1)}, bf16[128,3584]{1,0:T(8,128)(2,1)S(1)}) fusion(bf16[128,3584]{1,0:T(8,128)(2,1)} %get-tuple-element.33, f32[128]{0:T(128)S(1)} %mul.126, bf16[128,3584]{1,0:T(8,128)(2,1)} %get-tuple-element.34, bf16[128,3584]{1,0:T(8,128)(2,1)} %all-reduce.4.cloned.1.call-done), kind=kLoop, calls=%fused_computation.10 | loop fusion | flops 9633792 | bytes 5505536 | tf_op jit(solution)/shard_map/convert_element_type | solution.py:16
  159.1 5.2 %convolution_convert_fusion.3 = bf16[128,1024]{1,0:T(8,128)(2,1)S(1)} fusion(bf16[128,3584]{1,0:T(8,128)(2,1)S(1)} %get-tuple-element.15.left_ref, bf16[3584,1024]{1,0:T(8,128)(2,1)} %param.11), kind=kOutput, calls=%fused_computation.22 | convolution fusion | flops 939655168 | bytes 8519680 | tf_op jit(solution)/shard_map/dot_general | solution.py:115
  165.1 1.1 copy.36
  166.2 5.5 %fusion.22 = f32[128,1024]{1,0:T(8,128)S(1)} fusion(bf16[128,3584]{1,0:T(8,128)(2,1)S(1)} %get-tuple-element.39.right_ref, bf16[1024,3584]{1,0:T(8,128)(2,1)} %param.9), kind=kOutput, calls=%fused_computation.51 | convolution fusion | flops 939524096 | bytes 8781824 | tf_op jit(solution)/shard_map/dot_general | solution.py:116
  171.7 5.7 %multiply_reduce_fusion.1 = (f32[1024]{0:T(1024)S(1)}, f32[128]{0:T(128)S(1)}, bf16[128,1024]{1,0:T(8,128)(2,1)S(1)}) fusion(f32[128,1024]{1,0:T(8,128)S(1)} %reshape.49, f32[128,1024]{1,0:T(8,128)S(1)} %copy-done.5, f32[1024]{0:T(1024)S(1)} %copy-done.8, f32[128,1024]{1,0:T(8,128)S(1)} %fusion.22, bf16[128,3584]{1,0:T(8,128)(2,1)S(1)} %get-tuple-element.40.right_ref, ...), kind=kOutput, calls=%fused_computation.25 | convolution fusion | flops 940440448 | bytes 10101248 | tf_op jit(solution)/shard_map/dot_general | solution.py:118
  177.6 1.1 copy.38
  178.8 13.0 %psum.46 = f32[1152]{0:T(1024)S(1)} all-reduce(f32[1152]{0:T(1024)S(1)} %pad_maximum_fusion.1), channel_id=1, replica_groups=mesh['dp'=4,'tensor'=8] {'tensor'}, use_global_device_ids=true, to_apply=%region_8.0 | all-reduce | flops 1152 | bytes 9216 | tf_op jit(solution)/shard_map/psum | solution.py:138
  192.6 11.0 %psum.47 = f32[32,4]{0,1:T(4,128)S(1)} all-reduce(f32[32,4]{0,1:T(4,128)S(1)} %copy.41), channel_id=1, replica_groups=mesh['dp'=4,'tensor'=8] {'dp'}, use_global_device_ids=true, to_apply=%region_9.0 | all-reduce | flops 128 | bytes 1024 | tf_op jit(solution)/shard_map/psum | solution.py:140
  203.5 5.3 %shard_map.127 = bf16[1024,3584]{1,0:T(8,128)(2,1)} custom-call(bf16[128,1024]{1,0:T(8,128)(2,1)} %copy-done.1, bf16[128,3584]{1,0:T(8,128)(2,1)} %copy-done.3), custom_call_target="tpu_custom_call" | custom-call | flops 939524096 | bytes 8519680 | tf_op jit(solution)/shard_map/pallas_call | solution.py:47
  208.8 5.3 %shard_map.126 = bf16[1024,3584]{1,0:T(8,128)(2,1)} custom-call(bf16[128,1024]{1,0:T(8,128)(2,1)} %copy-done.1, bf16[128,3584]{1,0:T(8,128)(2,1)} %copy-done.2), custom_call_target="tpu_custom_call" | custom-call | flops 939524096 | bytes 8519680 | tf_op jit(solution)/shard_map/pallas_call | solution.py:47
  214.1 5.3 %shard_map.128 = bf16[3584,1024]{1,0:T(8,128)(2,1)} custom-call(bf16[128,3584]{1,0:T(8,128)(2,1)} %copy-done, bf16[128,1024]{1,0:T(8,128)(2,1)} %copy-done.4), custom_call_target="tpu_custom_call" | custom-call | flops 939524096 | bytes 8519680 | tf_op jit(solution)/shard_map/pallas_call | solution.py:47
  220.1 0.9 copy.42
  (54 shorter events, 5.6 us)
Async XLA Ops:
  7.2 33.5 %copy-start.8 = (f32[1024]{0:T(1024)S(1)}, f32[1024]{0:T(1024)}, u32[]{:S(2)}) copy-start(f32[1024]{0:T(1024)} %param.8) | copy-start | bytes 12292
  7.2 69.1 %all-reduce.4.cloned.1.call-start = ((), (), s32[]{:S(2)}) async-start(), calls=%async_computation.1 | async-start | bytes 1835008 | tf_op jit(solution)/shard_map/psum | solution.py:76
  21.2 20.6 %copy-start.4 = (bf16[128,1024]{1,0:T(8,128)(2,1)}, bf16[128,1024]{1,0:T(8,128)(2,1)S(1)}, u32[]{:S(2)}) copy-start(bf16[128,1024]{1,0:T(8,128)(2,1)S(1)} %reshape.46.right_ref) | copy-start | bytes 786436
  27.9 128.1 %all-reduce.6.cloned.1.call-start = ((), (), s32[]{:S(2)}) async-start(), calls=%async_computation.3 | async-start | bytes 3670016 | tf_op jit(solution)/shard_map/psum | solution.py:105
  41.8 6.5 %slice-start = ((s8[7340032]{0:T(1024)(128)(4,1)}), s8[3145728]{0:T(1024)(128)(4,1)S(1)}, s32[]{:S(2)}) async-start(s8[7340032]{0:T(1024)(128)(4,1)} %bitcast.48), calls=%async_computation.4 | async-start | bytes 6291456
  43.0 7.4 %copy-start.1 = (bf16[128,1024]{1,0:T(8,128)(2,1)}, bf16[128,1024]{1,0:T(8,128)(2,1)S(1)}, u32[]{:S(2)}) copy-start(bf16[128,1024]{1,0:T(8,128)(2,1)S(1)} %reshape.45.left_ref) | copy-start | bytes 786436
  43.0 5.4 %slice-start.1 = ((s8[7340032]{0:T(1024)(128)(4,1)}), s8[4194304]{0:T(1024)(128)(4,1)S(1)}, s32[]{:S(2)}) async-start(s8[7340032]{0:T(1024)(128)(4,1)} %bitcast.48), calls=%async_computation.5 | async-start | bytes 8388608
  48.3 28.0 %copy-start.9 = (s32[4]{0:T(128)S(1)}, s32[4]{0:T(128)}, u32[]{:S(2)}) copy-start(s32[4]{0:T(128)} %param.13) | copy-start | bytes 52
  76.3 143.8 %reduce-scatter.2.cloned.1.call-start = ((), (), s32[]{:S(2)}) async-start(), calls=%async_computation.2 | async-start | bytes 589824 | tf_op jit(solution)/shard_map/reduce_scatter | solution.py:143
  159.1 5.2 %copy-start = (bf16[128,3584]{1,0:T(8,128)(2,1)}, bf16[128,3584]{1,0:T(8,128)(2,1)S(1)}, u32[]{:S(2)}) copy-start(bf16[128,3584]{1,0:T(8,128)(2,1)S(1)} %get-tuple-element.15.left_ref) | copy-start | bytes 2752516
  159.1 7.1 %copy-start.2 = (bf16[128,3584]{1,0:T(8,128)(2,1)}, bf16[128,3584]{1,0:T(8,128)(2,1)S(1)}, u32[]{:S(2)}) copy-start(bf16[128,3584]{1,0:T(8,128)(2,1)S(1)} %get-tuple-element.39.right_ref) | copy-start | bytes 2752516
  159.1 12.6 %copy-start.3 = (bf16[128,3584]{1,0:T(8,128)(2,1)}, bf16[128,3584]{1,0:T(8,128)(2,1)S(1)}, u32[]{:S(2)}) copy-start(bf16[128,3584]{1,0:T(8,128)(2,1)S(1)} %get-tuple-element.40.right_ref) | copy-start | bytes 2752516
  165.1 6.6 %copy-start.5 = (f32[128,1024]{1,0:T(8,128)S(1)}, f32[128,1024]{1,0:T(8,128)}, u32[]{:S(2)}) copy-start(f32[128,1024]{1,0:T(8,128)} %reshape.50) | copy-start | bytes 1572868
  208.8 12.1 %copy-start.6 = (bf16[4,4,1024]{2,1,0:T(4,128)(2,1)S(1)}, bf16[4,4,1024]{2,1,0:T(4,128)(2,1)}, u32[]{:S(2)}) copy-start(bf16[4,4,1024]{2,1,0:T(4,128)(2,1)} %param.7) | copy-start | bytes 98308
  208.8 12.1 %copy-start.7 = (bf16[4,4,1024]{2,1,0:T(4,128)(2,1)S(1)}, bf16[4,4,1024]{2,1,0:T(4,128)(2,1)}, u32[]{:S(2)}) copy-start(bf16[4,4,1024]{2,1,0:T(4,128)(2,1)} %param.12) | copy-start | bytes 98308
Sparse Core Ops, SparseCore 0:
  28.0 48.1 all-reduce.3
  79.2 76.7 all-reduce.5
  178.9 33.1 reduce-scatter.1

commit v9 on v7

--- a/solution.py
+++ b/solution.py
@@ -26,19 +26,16 @@
     full_width = local_feat * lax.axis_size("dp")
     batches, local_rows, _ = inputs.shape
     wide_inputs = inputs.astype(jnp.float32)
-    both = jnp.concatenate([d_output, inputs], axis=0).transpose(1, 0, 2)
-    both_all = lax.all_gather(both, "tensor", axis=0, tiled=True)
-    grad_all = both_all[:, :batches]
-    inputs_all = both_all[:, batches:].astype(jnp.float32)
+    grad_all = lax.all_gather(d_output.transpose(1, 0, 2), "tensor", axis=0, tiled=True)
     rows = grad_all.shape[0]
     start = tensor_index * local_rows
     flat_grad = grad_all.reshape(rows * batches, local_feat)
-    back_first = lax.psum(
-        lax.dot_general(
-            flat_grad, w_down, contract_cols, preferred_element_type=jnp.float32
-        ).astype(jnp.bfloat16),
-        "dp",
-    )
+    back_part = lax.dot_general(
+        flat_grad, w_down, contract_cols, preferred_element_type=jnp.float32
+    ).astype(jnp.bfloat16)
+    back_first = lax.psum(back_part, "dp")
+    inputs_all, _ = lax.optimization_barrier((inputs.transpose(1, 0, 2), back_part))
+    inputs_all = lax.all_gather(inputs_all, "tensor", axis=0, tiled=True).astype(jnp.float32)
     square_sum = lax.psum(jnp.sum(inputs_all * inputs_all, axis=2).T, "dp").T
     row_scale_all = lax.rsqrt(square_sum / full_width + epsilon)
     normed_all = (inputs_all * row_scale_all[:, :, None] * norm_gain).astype(jnp.bfloat16)

time: 224 us -> 223 us (level)
  waiting for transfers between devices: 105 us -> 94.3 us
  blocking collectives: 47.5 us -> 56.5 us
    psum x1, waiting for transfers between devices: 25.9 us -> 16.7 us  [per_device(): back_first = lax.psum(back_part, 'dp')]
    all_gather x1 -> x2, blocking collectives: 11.3 us -> 20.1 us  [the longest x1 10.8 us: per_device(): lax.all_gather(d_output.transpose(1, 0, 2), 'tensor', axis=0, tiled=True)]
where the time goes in v9:
time: 223 us; the launch traced here: 222 us
  waiting for transfers between devices  94.3 us (42%)
  blocking collectives  56.5 us (25%)
  matrix products  44 us (20%)
  between operations  14 us (6%)
  local copies, waits for them, and re-layouts  8.07 us (4%)
  other arithmetic  4.98 us (2%)
    psum x1, waiting for transfers between devices, per_device(): gate_sum, up_sum = lax.psum(parts, 'dp')  77.6 us
    psum x1, waiting for transfers between devices, per_device(): back_first = lax.psum(back_part, 'dp')  16.7 us
    psum x1, blocking collectives, per_device(): reduced = lax.psum(jnp.concatenate([gain_part, row_all]), 'tensor')  12.8 us
    psum x1, blocking collectives, per_device(): square_sum = lax.psum(jnp.sum(inputs_all * inputs_all, axis=2).T, 'dp').T  12.4 us
    psum x1, blocking collectives, per_device(): row_all = lax.psum(reduced[local_feat:], 'dp').reshape(rows, batches)  11.1 us
    all_gather x1, blocking collectives, per_device(): lax.all_gather(d_output.transpose(1, 0, 2), 'tensor', axis=0, tiled=True)  10.8 us
    all_gather x1, blocking collectives, per_device(): lax.all_gather(inputs_all, 'tensor', axis=0, tiled=True).astype(jnp.float32)  9.28 us
    dot_general x1, matrix products, per_device(): lax.dot_general(flat_grad, w_down, contract_cols, preferred_element_type=...  6.65 us
  transfers between devices with their start and end apart: 3, of which 2 were waited for; matrix products, arithmetic and copies ran while one was open for 11% of the time, Pallas kernels for 0%

profile of v9, /device:TPU:0, one launch (start us, length us, event | category | flops | bytes accessed | tf_op | source)
XLA Modules:
  0.0 222.1 jit_solution(7097210431955141305)
XLA Ops:
  7.2 0.8 copy.45
  8.8 10.8 %all_gather.6 = bf16[32,4,1024]{2,1,0:T(4,128)(2,1)S(1)} all-gather(bf16[4,4,1024]{2,1,0:T(4,128)(2,1)S(1)} %bitcast.61), channel_id=1, replica_groups=mesh['dp'=4,'tensor'=8] {'tensor'}, dimensions={0}, use_global_device_ids=true | all-gather | bytes 294912 | tf_op jit(solution)/shard_map/all_gather | solution.py:29
  19.6 6.6 %convolution_convert_fusion.5 = bf16[128,3584]{1,0:T(8,128)(2,1)} fusion(bf16[128,1024]{1,0:T(8,128)(2,1)S(1)} %reshape.45, bf16[3584,1024]{1,0:T(8,128)(2,1)} %param.11), kind=kOutput, calls=%fused_computation.5 | convolution fusion | flops 939982848 | bytes 8519680 | tf_op jit(solution)/shard_map/dot_general | solution.py:33
  26.4 9.3 %all_gather.7 = bf16[32,4,1024]{2,1,0:T(4,128)(2,1)S(1)} all-gather(bf16[4,4,1024]{2,1,0:T(4,128)(2,1)S(1)} %bitcast.60), channel_id=1, replica_groups=mesh['dp'=4,'tensor'=8] {'tensor'}, dimensions={0}, use_global_device_ids=true | all-gather | bytes 294912 | tf_op jit(solution)/shard_map/all_gather | solution.py:38
  36.0 12.4 %psum.42 = f32[4,32]{1,0:T(4,128)S(1)} all-reduce(f32[4,32]{1,0:T(4,128)S(1)} %bitcast.62), channel_id=1, replica_groups=mesh['dp'=4,'tensor'=8] {'dp'}, use_global_device_ids=true, to_apply=%region_1.0 | all-reduce | flops 128 | bytes 1024 | tf_op jit(solution)/shard_map/psum | solution.py:39
  48.5 1.1 broadcast_multiply_fusion
  49.6 1.2 reshape.46
  50.8 5.3 %convolution_convert_fusion.4 = bf16[128,3584]{1,0:T(8,128)(2,1)} fusion(bf16[128,1024]{1,0:T(8,128)(2,1)S(1)} %reshape.46, bf16[1024,3584]{1,0:T(8,128)(2,1)} %param.9), kind=kOutput, calls=%fused_computation.4 | convolution fusion | flops 939982848 | bytes 8519680 | tf_op jit(solution)/shard_map/dot_general | solution.py:58
  56.1 2.1 convolution_convert_fusion.3
  58.2 16.7 %all-reduce.4.cloned.1.call-done = bf16[128,3584]{1,0:T(8,128)(2,1)} async-done(((bf16[128,3584]{1,0:T(8,128)(2,1)}), bf16[128,3584]{1,0:T(8,128)(2,1)}) %all-reduce.4.cloned.1.call-update) | async-done | bytes 917520 | tf_op jit(solution)/shard_map/psum | solution.py:36
  75.1 0.8 reshape.50
  75.9 1.0 reshape.49
  77.0 77.6 %all-reduce.6.cloned.1.call-done = (bf16[128,3584]{1,0:T(8,128)(2,1)}, bf16[128,3584]{1,0:T(8,128)(2,1)}) async-done(((bf16[128,3584]{1,0:T(8,128)(2,1)}, bf16[128,3584]{1,0:T(8,128)(2,1)}), (bf16[128,3584]{1,0:T(8,128)(2,1)}, bf16[128,3584]{1,0:T(8,128)(2,1)})) %all-reduce.6.cloned.1.call-update) | async-done | bytes 1835024 | tf_op jit(solution)/shard_map/psum | solution.py:62
  154.6 2.2 %fusion.1 = bf16[128,3584]{1,0:T(8,128)(2,1)S(1)} fusion(bf16[128,3584]{1,0:T(8,128)(2,1)} %get-tuple-element.35, f32[128]{0:T(128)S(1)} %mul.126, bf16[128,3584]{1,0:T(8,128)(2,1)} %get-tuple-element.36), kind=kLoop, calls=%fused_computation.13 | loop fusion | flops 4128768 | bytes 2753024 | tf_op jit(solution)/shard_map/convert_element_type | solution.py:15
  156.9 6.0 %fusion.25 = f32[128,1024]{1,0:T(8,128)S(1)} fusion(bf16[1024,3584]{1,0:T(8,128)(2,1)} %param.9, bf16[128,3584]{1,0:T(8,128)(2,1)S(1)} %copy-done.5, bf16[128,3584]{1,0:T(8,128)(2,1)} %all-reduce.4.cloned.1.call-done, bf16[128,3584]{1,0:T(8,128)(2,1)S(1)} %copy-done.6, f32[128]{0:T(128)S(1)} %mul.126), kind=kOutput, calls=%fused_computation.54 | convolution fusion | flops 945946624 | bytes 10617344 | tf_op jit(solution)/shard_map/dot_general | solution.py:73
  163.0 5.4 %convolution_convert_fusion.1 = bf16[1024,3584]{1,0:T(8,128)(2,1)} fusion(bf16[128,1024]{1,0:T(8,128)(2,1)S(1)} %reshape.46, bf16[128,3584]{1,0:T(8,128)(2,1)S(1)} %copy-done.13, f32[128]{0:T(128)S(1)} %mul.126, bf16[128,3584]{1,0:T(8,128)(2,1)S(1)} %copy-done.6), kind=kOutput, calls=%fused_computation.1 | convolution fusion | flops 947322880 | bytes 9437696 | tf_op jit(solution)/shard_map/dot_general | solution.py:113
  168.4 2.7 %multiply_reduce_fusion.1 = (f32[1024]{0:T(1024)S(1)}, f32[128]{0:T(128)S(1)}, bf16[128,1024]{1,0:T(8,128)(2,1)S(1)}) fusion(f32[128,1024]{1,0:T(8,128)S(1)} %copy-done.9, f32[128,1024]{1,0:T(8,128)S(1)} %copy-done.8, f32[1024]{0:T(1024)S(1)} %copy-done.12, f32[128,1024]{1,0:T(8,128)S(1)} %fusion.25, bf16[1024,3584]{1,0:T(8,128)(2,1)S(1)} %bitcast.57, ...), kind=kOutput, calls=%fused_computation.28 | convolution fusion | flops 944569216 | bytes 11019264 | tf_op jit(solution)/shard_map/dot_general | solution.py:75
  171.2 4.2 %convolution_convert_fusion.6 = bf16[128,1024]{1,0:T(8,128)(2,1)S(1)} fusion(bf16[128,3584]{1,0:T(8,128)(2,1)S(1)} %fusion.1, bf16[3584,1024]{1,0:T(8,128)(2,1)} %param.11), kind=kOutput, calls=%fused_computation.25 | convolution fusion | flops 939655168 | bytes 8519680 | tf_op jit(solution)/shard_map/dot_general | solution.py:72
  175.7 1.1 copy.36
  176.8 5.1 %convolution_convert_fusion = bf16[3584,1024]{1,0:T(8,128)(2,1)} fusion(bf16[128,3584]{1,0:T(8,128)(2,1)S(1)} %fusion.1, bf16[128,1024]{1,0:T(8,128)(2,1)S(1)} %copy-done.3), kind=kOutput, calls=%fused_computation | convolution fusion | flops 943194112 | bytes 8519680 | tf_op jit(solution)/shard_map/dot_general | solution.py:107
  182.0 12.8 %psum.46 = f32[1152]{0:T(1024)S(1)} all-reduce(f32[1152]{0:T(1024)S(1)} %pad_maximum_fusion.1), channel_id=1, replica_groups=mesh['dp'=4,'tensor'=8] {'tensor'}, use_global_device_ids=true, to_apply=%region_8.0 | all-reduce | flops 1152 | bytes 9216 | tf_op jit(solution)/shard_map/psum | solution.py:95
  195.6 11.1 %psum.47 = f32[32,4]{0,1:T(4,128)S(1)} all-reduce(f32[32,4]{0,1:T(4,128)S(1)} %copy.39), channel_id=1, replica_groups=mesh['dp'=4,'tensor'=8] {'dp'}, use_global_device_ids=true, to_apply=%region_9.0 | all-reduce | flops 128 | bytes 1024 | tf_op jit(solution)/shard_map/psum | solution.py:97
  207.4 6.6 %convolution_convert_fusion.2 = bf16[1024,3584]{1,0:T(8,128)(2,1)} fusion(bf16[128,1024]{1,0:T(8,128)(2,1)S(1)} %reshape.46, bf16[128,3584]{1,0:T(8,128)(2,1)S(1)} %copy-done.5, bf16[128,3584]{1,0:T(8,128)(2,1)} %all-reduce.4.cloned.1.call-done, bf16[128,3584]{1,0:T(8,128)(2,1)S(1)} %copy-done.7, f32[128]{0:T(128)S(1)} %mul.126), kind=kOutput, calls=%fused_computation.2 | convolution fusion | flops 949616640 | bytes 10355200 | tf_op jit(solution)/shard_map/dot_general | solution.py:110
  214.0 0.9 copy.40
  (68 shorter events, 4.4 us)
Async XLA Ops:
  7.2 67.7 %all-reduce.4.cloned.1.call-start = ((), (), s32[]{:S(2)}) async-start(), calls=%async_computation.1 | async-start | bytes 1835008 | tf_op jit(solution)/shard_map/psum | solution.py:36
  19.6 6.7 %copy-start.2 = (bf16[128,1024]{1,0:T(8,128)(2,1)}, bf16[128,1024]{1,0:T(8,128)(2,1)S(1)}, u32[]{:S(2)}) copy-start(bf16[128,1024]{1,0:T(8,128)(2,1)S(1)} %reshape.45) | copy-start | bytes 786436
  19.6 28.9 %copy-start.12 = (f32[1024]{0:T(1024)S(1)}, f32[1024]{0:T(1024)}, u32[]{:S(2)}) copy-start(f32[1024]{0:T(1024)} %param.8) | copy-start | bytes 12292
  26.3 128.3 %all-reduce.6.cloned.1.call-start = ((), (), s32[]{:S(2)}) async-start(), calls=%async_computation.3 | async-start | bytes 3670016 | tf_op jit(solution)/shard_map/psum | solution.py:62
  35.7 13.9 %copy-start = (bf16[32,4,1024]{2,1,0:T(4,128)(2,1)}, bf16[32,4,1024]{2,1,0:T(4,128)(2,1)S(1)}, u32[]{:S(2)}) copy-start(bf16[32,4,1024]{2,1,0:T(4,128)(2,1)S(1)} %all_gather.7) | copy-start | bytes 786436
  49.6 6.5 %slice-start = ((s8[7340032]{0:T(1024)(128)(4,1)}), s8[3145728]{0:T(1024)(128)(4,1)S(1)}, s32[]{:S(2)}) async-start(s8[7340032]{0:T(1024)(128)(4,1)} %bitcast.54), calls=%async_computation.4 | async-start | bytes 6291456
  50.8 5.3 %slice-start.1 = ((s8[7340032]{0:T(1024)(128)(4,1)}), s8[4194304]{0:T(1024)(128)(4,1)S(1)}, s32[]{:S(2)}) async-start(s8[7340032]{0:T(1024)(128)(4,1)} %bitcast.54), calls=%async_computation.5 | async-start | bytes 8388608
  58.2 17.0 %copy-start.1 = (bf16[32,4,1024]{2,1,0:T(4,128)(2,1)S(1)}, bf16[32,4,1024]{2,1,0:T(4,128)(2,1)}, u32[]{:S(2)}) copy-start(bf16[32,4,1024]{2,1,0:T(4,128)(2,1)} %copy-done) | copy-start | bytes 786436
  58.2 17.8 %copy-start.4 = (f32[32,4,1024]{2,1,0:T(4,128)S(1)}, f32[32,4,1024]{2,1,0:T(4,128)}, u32[]{:S(2)}) copy-start(f32[32,4,1024]{2,1,0:T(4,128)} %get-tuple-element.41) | copy-start | bytes 1572868
  58.2 18.8 %copy-start.14 = (s32[4]{0:T(128)S(1)}, s32[4]{0:T(128)}, u32[]{:S(2)}) copy-start(s32[4]{0:T(128)} %param.13) | copy-start | bytes 52
  74.9 139.1 %reduce-scatter.2.cloned.1.call-start = ((), (), s32[]{:S(2)}) async-start(), calls=%async_computation.2 | async-start | bytes 589824 | tf_op jit(solution)/shard_map/reduce_scatter | solution.py:100
  154.6 2.3 %copy-start.5 = (bf16[128,3584]{1,0:T(8,128)(2,1)S(1)}, bf16[128,3584]{1,0:T(8,128)(2,1)}, u32[]{:S(2)}) copy-start(bf16[128,3584]{1,0:T(8,128)(2,1)} %get-tuple-element.35) | copy-start | bytes 2752516
  154.6 2.3 %copy-start.6 = (bf16[128,3584]{1,0:T(8,128)(2,1)S(1)}, bf16[128,3584]{1,0:T(8,128)(2,1)}, u32[]{:S(2)}) copy-start(bf16[128,3584]{1,0:T(8,128)(2,1)} %get-tuple-element.36) | copy-start | bytes 2752516
  154.6 13.7 %slice-start.2 = ((s8[7340032]{0:T(1024)(128)(4,1)}), s8[4194304]{0:T(1024)(128)(4,1)S(1)}, s32[]{:S(2)}) async-start(s8[7340032]{0:T(1024)(128)(4,1)} %bitcast.56), calls=%async_computation.6 | async-start | bytes 8388608
  156.9 6.1 %copy-start.13 = (bf16[128,3584]{1,0:T(8,128)(2,1)S(1)}, bf16[128,3584]{1,0:T(8,128)(2,1)}, u32[]{:S(2)}) copy-start(bf16[128,3584]{1,0:T(8,128)(2,1)} %all-reduce.4.cloned.1.call-done) | copy-start | bytes 2752516
  156.9 11.5 %slice-start.3 = ((s8[7340032]{0:T(1024)(128)(4,1)}), s8[3145728]{0:T(1024)(128)(4,1)S(1)}, s32[]{:S(2)}) async-start(s8[7340032]{0:T(1024)(128)(4,1)} %bitcast.56), calls=%async_computation.7 | async-start | bytes 6291456
  162.9 5.4 %copy-start.8 = (f32[128,1024]{1,0:T(8,128)S(1)}, f32[128,1024]{1,0:T(8,128)}, u32[]{:S(2)}) copy-start(f32[128,1024]{1,0:T(8,128)} %reshape.50) | copy-start | bytes 1572868
  163.0 5.4 %copy-start.9 = (f32[128,1024]{1,0:T(8,128)S(1)}, f32[128,1024]{1,0:T(8,128)}, u32[]{:S(2)}) copy-start(f32[128,1024]{1,0:T(8,128)} %reshape.49) | copy-start | bytes 1572868
  175.5 1.4 copy-start.3
  176.8 30.5 %copy-start.7 = (bf16[128,3584]{1,0:T(8,128)(2,1)S(1)}, bf16[128,3584]{1,0:T(8,128)(2,1)}, u32[]{:S(2)}) copy-start(bf16[128,3584]{1,0:T(8,128)(2,1)} %get-tuple-element.36) | copy-start | bytes 2752516
  207.4 7.5 %copy-start.10 = (bf16[4,4,1024]{2,1,0:T(4,128)(2,1)S(1)}, bf16[4,4,1024]{2,1,0:T(4,128)(2,1)}, u32[]{:S(2)}) copy-start(bf16[4,4,1024]{2,1,0:T(4,128)(2,1)} %param.7) | copy-start | bytes 98308
  207.4 7.5 %copy-start.11 = (bf16[4,4,1024]{2,1,0:T(4,128)(2,1)S(1)}, bf16[4,4,1024]{2,1,0:T(4,128)(2,1)}, u32[]{:S(2)}) copy-start(bf16[4,4,1024]{2,1,0:T(4,128)(2,1)} %param.12) | copy-start | bytes 98308
Sparse Core Ops, SparseCore 0:
  26.4 48.3 all-reduce.3
  77.8 76.7 all-reduce.5
  176.9 33.0 reduce-scatter.1

commit v10 on v9

--- a/solution.py
+++ b/solution.py
@@ -1,3 +1,5 @@
+import functools
+
 import jax
 import jax.numpy as jnp
 from jax import lax
@@ -45,6 +47,21 @@
     halvings = 3 - level_of_batch
     active = (tensor_index < jnp.right_shift(groups, halvings)).astype(jnp.float32)
     active_mask = jnp.tile(active, rows)[:, None]
+    levels = jnp.arange(batches, dtype=jnp.int32)
+    active_count = jnp.sum(
+        (tensor_index < jnp.right_shift(groups, batches - 1 - levels)).astype(jnp.int32)
+    )
+    order = jnp.sum(
+        jnp.where(level_of_batch[None, :] == batches - 1 - levels[:, None], levels[None, :], 0),
+        axis=1,
+    )
+
+    def active_psum(count, pair):
+        summed = lax.psum(tuple(part[:, :count] for part in pair), "dp")
+        return tuple(
+            jnp.pad(total, ((0, 0), (0, batches - count), (0, 0))) for total in summed
+        )
+
     chunks = 1
     width = local_cols // chunks
     down_part = None
@@ -59,7 +76,16 @@
         up_part = jnp.dot(flat_normed, up_w, preferred_element_type=jnp.float32)
         parts = (gate_part.astype(jnp.bfloat16), up_part.astype(jnp.bfloat16))
         parts, back_sum = lax.optimization_barrier((parts, back_first))
-        gate_sum, up_sum = lax.psum(parts, "dp")
+        ranked = tuple(jnp.take(part.reshape(rows, batches, -1), order, axis=1) for part in parts)
+        ranked = lax.switch(
+            active_count - 1,
+            [functools.partial(active_psum, count) for count in range(1, batches + 1)],
+            ranked,
+        )
+        gate_sum, up_sum = (
+            jnp.take(part, batches - 1 - level_of_batch, axis=1).reshape(rows * batches, -1)
+            for part in ranked
+        )
         hidden, gate_grad, up_grad = local_terms(
             gate_sum.astype(jnp.float32),
             up_sum.astype(jnp.float32),

time: 223 us -> 268 us (1.20)
  local copies, waits for them, and re-layouts: 8.07 us -> 33.6 us
  waiting for transfers between devices: 94.3 us -> 108 us
  other arithmetic: 4.98 us -> 11.2 us
    reduce_scatter x1, waiting for transfers between devices: 0.01 us -> 19.5 us  [per_device(): lax.psum_scatter(stacked, 'tensor', scatter_dimension=0, tiled=True)]
    convert_element_type x0 -> x4, local copies, waits for them, and re-layouts: none -> 11.1 us  [the longest x2 6.8 us: per_device(): up_sum.astype(jnp.float32)]
    gather x0 -> x4, local copies, waits for them, and re-layouts: none -> 5.45 us  [the longest x2 3.05 us: per_device(): jnp.take(part.reshape(rows, batches, -1), order, axis=1)]
    dot_general x1, matrix products: 2.07 us -> 5.41 us  [per_device(): up_part = jnp.dot(flat_normed, up_w, preferred_element_type=jnp.float32)]
    psum x1, waiting for transfers between devices: 16.7 us -> 13.4 us  [per_device(): back_first = lax.psum(back_part, 'dp')]
    another operation x0 -> x2, local copies, waits for them, and re-layouts: none -> 3.27 us
    dot_general x1, matrix products: 5.3 us -> 2.07 us  [per_device(): gate_part = jnp.dot(flat_normed, gate_w, preferred_element_type=jnp.float32)]
  transfers between devices with their start and end apart: 3 -> 3, of which waited for: 2 -> 3; matrix products, arithmetic and copies ran while one was open for 11% -> 9% of each run, Pallas kernels for 0% -> 0%
where the time goes in v10:
time: 268 us; the launch traced here: 267 us
  waiting for transfers between devices  108 us (40%)
  blocking collectives  54.7 us (20%)
  matrix products  44 us (16%)
  local copies, waits for them, and re-layouts  33.6 us (13%)
  between operations  14.7 us (5%)
  other arithmetic  11.2 us (4%)
    psum x1, waiting for transfers between devices, active_psum(): summed = lax.psum(tuple((part[:, :count] for part in pair)), 'dp')  75.2 us
    reduce_scatter x1, waiting for transfers between devices, per_device(): lax.psum_scatter(stacked, 'tensor', scatter_dimension=0, tiled=True)  19.5 us
    psum x1, waiting for transfers between devices, per_device(): back_first = lax.psum(back_part, 'dp')  13.4 us
    psum x1, blocking collectives, per_device(): square_sum = lax.psum(jnp.sum(inputs_all * inputs_all, axis=2).T, 'dp').T  12.5 us
    psum x1, blocking collectives, per_device(): reduced = lax.psum(jnp.concatenate([gain_part, row_all]), 'tensor')  12.1 us
    all_gather x1, blocking collectives, per_device(): lax.all_gather(d_output.transpose(1, 0, 2), 'tensor', axis=0, tiled=True)  10.8 us
    psum x1, blocking collectives, per_device(): row_all = lax.psum(reduced[local_feat:], 'dp').reshape(rows, batches)  10.1 us
    all_gather x1, blocking collectives, per_device(): lax.all_gather(inputs_all, 'tensor', axis=0, tiled=True).astype(jnp.float32)  9.28 us
  transfers between devices with their start and end apart: 3, of which 3 were waited for; matrix products, arithmetic and copies ran while one was open for 9% of the time, Pallas kernels for 0%

profile of v10, /device:TPU:0, one launch (start us, length us, event | category | flops | bytes accessed | tf_op | source)
XLA Modules:
  0.0 266.9 jit_solution(11105121261949424199)
XLA Ops:
  8.8 10.8 %all_gather.6 = bf16[32,4,1024]{2,1,0:T(4,128)(2,1)S(1)} all-gather(bf16[4,4,1024]{2,1,0:T(4,128)(2,1)S(1)} %bitcast.88), channel_id=1, replica_groups=mesh['dp'=4,'tensor'=8] {'tensor'}, dimensions={0}, use_global_device_ids=true | all-gather | bytes 294912 | tf_op jit(solution)/shard_map/all_gather | solution.py:31
  19.7 6.6 %convolution_convert_fusion.5 = bf16[128,3584]{1,0:T(8,128)(2,1)} fusion(bf16[128,1024]{1,0:T(8,128)(2,1)S(1)} %reshape.90, bf16[3584,1024]{1,0:T(8,128)(2,1)} %param.17), kind=kOutput, calls=%fused_computation.11 | convolution fusion | flops 939982848 | bytes 8519680 | tf_op jit(solution)/shard_map/dot_general | solution.py:35
  27.2 9.3 %all_gather.7 = bf16[32,4,1024]{2,1,0:T(4,128)(2,1)S(1)} all-gather(bf16[4,4,1024]{2,1,0:T(4,128)(2,1)S(1)} %bitcast.87), channel_id=1, replica_groups=mesh['dp'=4,'tensor'=8] {'tensor'}, dimensions={0}, use_global_device_ids=true | all-gather | bytes 294912 | tf_op jit(solution)/shard_map/all_gather | solution.py:40
  37.7 12.5 %psum.84 = f32[4,32]{1,0:T(4,128)S(1)} all-reduce(f32[4,32]{1,0:T(4,128)S(1)} %bitcast.89), channel_id=1, replica_groups=mesh['dp'=4,'tensor'=8] {'dp'}, use_global_device_ids=true, to_apply=%region_2.0 | all-reduce | flops 128 | bytes 1024 | tf_op jit(solution)/shard_map/psum | solution.py:41
  54.0 5.4 %convolution_convert_fusion.3 = bf16[128,3584]{1,0:T(8,128)(2,1)} fusion(bf16[128,1024]{1,0:T(8,128)(2,1)S(1)} %reshape.91, bf16[1024,3584]{1,0:T(8,128)(2,1)} %param.16), kind=kOutput, calls=%fused_computation.9 | convolution fusion | flops 939982848 | bytes 8519680 | tf_op jit(solution)/shard_map/dot_general | solution.py:76
  59.4 2.1 convolution_convert_fusion.4
  61.5 13.4 %all-reduce.24.cloned.1.call-done = bf16[128,3584]{1,0:T(8,128)(2,1)} async-done(((bf16[128,3584]{1,0:T(8,128)(2,1)}), bf16[128,3584]{1,0:T(8,128)(2,1)}) %all-reduce.24.cloned.1.call-update) | async-done | bytes 917520 | tf_op jit(solution)/shard_map/psum | solution.py:38
  81.7 81.2 %conditional.1 = (bf16[32,4,3584]{2,0,1:T(8,128)(2,1)}, bf16[32,4,3584]{2,0,1:T(8,128)(2,1)S(1)}) conditional(s32[]{:T(128)} %clamp.3, (bf16[32,4,3584]{2,0,1:T(8,128)(2,1)S(1)}, bf16[32,4,3584]{2,0,1:T(8,128)(2,1)S(1)}) %tuple.30, (bf16[32,4,3584]{2,0,1:T(8,128)(2,1)S(1)}, ...), branch_computations={%region_5.9_spmd, %region_8.12_spmd, %region_11.0_spmd, %region_14... | conditional | flops 917504 | bytes 22020180 | solution.py:80
  85.3 75.2 %all-reduce.22.cloned.1.call-done = (bf16[32,4,3584]{2,1,0:T(4,128)(2,1)}, bf16[32,4,3584]{2,1,0:T(4,128)(2,1)}) async-done(((bf16[32,4,3584]{2,1,0:T(4,128)(2,1)}, bf16[32,4,3584]{2,1,0:T(4,128)(2,1)}), (bf16[32,4,3584]{2,1,0:T(4,128)(2,1)}, bf16[32,4,3584]{2,1,0:T(4,128)(2,1)})) %all-reduce.22.cloned.1.call-update) | async-done | bytes 1835024 | tf_op jit(solution)/shard_map/cond/branch_3_fun/psum | solution.py:60
  160.5 2.3 copy.93
  165.7 5.3 %fusion.11 = bf16[32,1,4,1024]{3,0,2,1:T(8,128)(2,1)} fusion(bf16[3584,1024]{1,0:T(8,128)(2,1)} %param.17, f32[4]{0:T(128)S(1)} %get-tuple-element.112, bf16[4,32,3584]{2,1,0:T(8,128)(2,1)S(1)} %gather_fusion.2, pred[4]{0:T(512)(128)(4,1)S(1)} %get-tuple-element.101, bf16[4,32,3584]{2,1,0:T(8,128)(2,1)S(1)} %gather_fusion.3), kind=kOutput, calls=%fused_computation.25 | convolution fusion | flops 944701440 | bytes 9437204 | tf_op jit(solution)/shard_map/dot_general | solution.py:98
  172.5 2.4 copy.84
  174.9 1.9 reshape.100
  176.9 3.9 %copy.83 = f32[32,4,3584]{2,1,0:T(4,128)} copy(f32[32,4,3584]{2,0,1:T(8,128)} %get-tuple-element.114) | data formatting | bytes 3670016 | tf_op jit(solution)/shard_map/convert_element_type | solution.py:91
  180.8 2.9 %reshape.99 = f32[128,3584]{1,0:T(8,128)} reshape(f32[32,4,3584]{2,1,0:T(4,128)} %copy.83) | data formatting | bytes 3670016 | tf_op jit(solution)/shard_map/convert_element_type | solution.py:91
  183.7 3.9 %multiply_convert_fusion = (bf16[128,3584]{1,0:T(8,128)(2,1)}, bf16[128,3584]{1,0:T(8,128)(2,1)S(1)}) fusion(f32[128,3584]{1,0:T(8,128)} %reshape.99, f32[128]{0:T(128)S(1)} %mul.146, f32[128,3584]{1,0:T(8,128)S(1)} %reshape.100, bf16[128,3584]{1,0:T(8,128)(2,1)} %all-reduce.24.cloned.1.call-done), kind=kLoop, calls=%fused_computation.19 | loop fusion | flops 7340032 | bytes 6423040 | tf_op jit(solution)/shard_map/convert_element_type | solution.py:17
  187.6 5.7 %fusion.30 = f32[128,1024]{1,0:T(8,128)S(1)} fusion(bf16[128,3584]{1,0:T(8,128)(2,1)S(1)} %get-tuple-element.104, bf16[1024,3584]{1,0:T(8,128)(2,1)} %param.15), kind=kOutput, calls=%fused_computation.71 | convolution fusion | flops 939524096 | bytes 8781824 | tf_op jit(solution)/shard_map/dot_general | solution.py:99
  193.3 3.3 %multiply_reduce_fusion.1 = (f32[1024]{0:T(1024)S(1)}, f32[128]{0:T(128)S(1)}, bf16[128,1024]{1,0:T(8,128)(2,1)}) fusion(f32[128,1024]{1,0:T(8,128)S(1)} %copy-done.10, f32[128,1024]{1,0:T(8,128)S(1)} %copy-done.9, f32[1024]{0:T(1024)S(1)} %copy-done.13, f32[128,1024]{1,0:T(8,128)S(1)} %fusion.30, bf16[1024,3584]{1,0:T(8,128)(2,1)S(1)} %bitcast.82, ...), kind=kOutput, calls=%fused_computation.34 | convolution fusion | flops 944110464 | bytes 11936768 | tf_op jit(solution)/shard_map/dot_general | solution.py:101
  196.6 12.1 %psum.86 = f32[1152]{0:T(1024)S(1)} all-reduce(f32[1152]{0:T(1024)S(1)} %pad_maximum_fusion.1), channel_id=1, replica_groups=mesh['dp'=4,'tensor'=8] {'tensor'}, use_global_device_ids=true, to_apply=%region_20.22 | all-reduce | flops 1152 | bytes 9216 | tf_op jit(solution)/shard_map/psum | solution.py:121
  209.4 5.1 %convolution_convert_fusion.2 = bf16[1024,3584]{1,0:T(8,128)(2,1)} fusion(bf16[128,1024]{1,0:T(8,128)(2,1)S(1)} %reshape.91, bf16[128,3584]{1,0:T(8,128)(2,1)S(1)} %get-tuple-element.104), kind=kOutput, calls=%fused_computation.6 | convolution fusion | flops 943194112 | bytes 8519680 | tf_op jit(solution)/shard_map/dot_general | solution.py:136
  214.7 10.1 %psum.87 = f32[32,4]{0,1:T(4,128)S(1)} all-reduce(f32[32,4]{0,1:T(4,128)S(1)} %copy.89), channel_id=1, replica_groups=mesh['dp'=4,'tensor'=8] {'dp'}, use_global_device_ids=true, to_apply=%region_21.23 | all-reduce | flops 128 | bytes 1024 | tf_op jit(solution)/shard_map/psum | solution.py:123
  228.9 5.1 %convolution_convert_fusion = bf16[3584,1024]{1,0:T(8,128)(2,1)} fusion(bf16[128,3584]{1,0:T(8,128)(2,1)S(1)} %copy-done, bf16[128,1024]{1,0:T(8,128)(2,1)S(1)} %copy-done.6), kind=kOutput, calls=%fused_computation.4 | convolution fusion | flops 943194112 | bytes 8519680 | tf_op jit(solution)/shard_map/dot_general | solution.py:133
  234.0 5.3 %convolution_convert_fusion.1 = bf16[1024,3584]{1,0:T(8,128)(2,1)} fusion(bf16[128,1024]{1,0:T(8,128)(2,1)S(1)} %reshape.91, bf16[128,3584]{1,0:T(8,128)(2,1)S(1)} %copy-done.2, f32[128]{0:T(128)S(1)} %mul.146, f32[128,3584]{1,0:T(8,128)S(1)} %reshape.100), kind=kOutput, calls=%fused_computation.5 | convolution fusion | flops 946864128 | bytes 10355200 | tf_op jit(solution)/shard_map/dot_general | solution.py:139
  239.3 19.5 %reduce-scatter.2.cloned.1.call-done = bf16[4,8,1024]{2,1,0:T(8,128)(2,1)} async-done(((bf16[32,8,1024]{2,1,0:T(8,128)(2,1)}), bf16[4,8,1024]{2,1,0:T(8,128)(2,1)}) %reduce-scatter.2.cloned.1.call-update) | async-done | bytes 65552 | tf_op jit(solution)/shard_map/reduce_scatter | solution.py:126
  (89 shorter events, 27.9 us)
Async XLA Ops:
  7.2 67.7 %all-reduce.24.cloned.1.call-start = ((), (), s32[]{:S(2)}) async-start(), calls=%async_computation.5 | async-start | bytes 1835008 | tf_op jit(solution)/shard_map/psum | solution.py:38
  19.6 6.7 %copy-start.5 = (bf16[128,1024]{1,0:T(8,128)(2,1)}, bf16[128,1024]{1,0:T(8,128)(2,1)S(1)}, u32[]{:S(2)}) copy-start(bf16[128,1024]{1,0:T(8,128)(2,1)S(1)} %reshape.90) | copy-start | bytes 786436
  19.6 7.3 %copy-start.14 = (s32[4]{0:T(128)S(1)}, s32[4]{0:T(128)}, u32[]{:S(2)}) copy-start(s32[4]{0:T(128)} %param.19) | copy-start | bytes 52
  26.3 24.0 %copy-start.13 = (f32[1024]{0:T(1024)S(1)}, f32[1024]{0:T(1024)}, u32[]{:S(2)}) copy-start(f32[1024]{0:T(1024)} %param.14) | copy-start | bytes 12292
  52.2 7.2 %slice-start = ((s8[7340032]{0:T(1024)(128)(4,1)}), s8[3145728]{0:T(1024)(128)(4,1)S(1)}, s32[]{:S(2)}) async-start(s8[7340032]{0:T(1024)(128)(4,1)} %bitcast.79), calls=%async_computation.7 | async-start | bytes 6291456
  54.0 5.4 %slice-start.1 = ((s8[7340032]{0:T(1024)(128)(4,1)}), s8[4194304]{0:T(1024)(128)(4,1)S(1)}, s32[]{:S(2)}) async-start(s8[7340032]{0:T(1024)(128)(4,1)} %bitcast.79), calls=%async_computation.8 | async-start | bytes 8388608
  61.5 15.4 %copy-start.3 = (bf16[128,3584]{1,0:T(8,128)(2,1)S(1)}, bf16[128,3584]{1,0:T(8,128)(2,1)}, u32[]{:S(2)}) copy-start(bf16[128,3584]{1,0:T(8,128)(2,1)} %convolution_convert_fusion.3) | copy-start | bytes 2752516
  78.8 1.5 copy-start.4
  82.0 78.5 %all-reduce.22.cloned.1.call-start = ((), (), s32[]{:S(2)}) async-start(), calls=%async_computation.4 | async-start | bytes 3670016 | tf_op jit(solution)/shard_map/cond/branch_3_fun/psum | solution.py:60
  160.5 2.3 copy-start.8
  163.0 95.8 %reduce-scatter.2.cloned.1.call-start = ((), (), s32[]{:S(2)}) async-start(), calls=%async_computation.6 | async-start | bytes 589824 | tf_op jit(solution)/shard_map/reduce_scatter | solution.py:126
  183.7 9.6 %slice-start.2 = ((s8[7340032]{0:T(1024)(128)(4,1)}), s8[4194304]{0:T(1024)(128)(4,1)S(1)}, s32[]{:S(2)}) async-start(s8[7340032]{0:T(1024)(128)(4,1)} %bitcast.81), calls=%async_computation.9 | async-start | bytes 8388608
  187.6 5.7 %slice-start.3 = ((s8[7340032]{0:T(1024)(128)(4,1)}), s8[3145728]{0:T(1024)(128)(4,1)S(1)}, s32[]{:S(2)}) async-start(s8[7340032]{0:T(1024)(128)(4,1)} %bitcast.81), calls=%async_computation.10 | async-start | bytes 6291456
  187.6 5.7 %copy-start.1 = (bf16[128,3584]{1,0:T(8,128)(2,1)S(1)}, bf16[128,3584]{1,0:T(8,128)(2,1)}, u32[]{:S(2)}) copy-start(bf16[128,3584]{1,0:T(8,128)(2,1)} %all-reduce.24.cloned.1.call-done) | copy-start | bytes 2752516
  187.6 5.7 %copy-start.9 = (f32[128,1024]{1,0:T(8,128)S(1)}, f32[128,1024]{1,0:T(8,128)}, u32[]{:S(2)}) copy-start(f32[128,1024]{1,0:T(8,128)} %reshape.97) | copy-start | bytes 1572868
  187.6 5.7 %copy-start.10 = (f32[128,1024]{1,0:T(8,128)S(1)}, f32[128,1024]{1,0:T(8,128)}, u32[]{:S(2)}) copy-start(f32[128,1024]{1,0:T(8,128)} %reshape.96) | copy-start | bytes 1572868
  224.8 4.1 %copy-start = (bf16[128,3584]{1,0:T(8,128)(2,1)S(1)}, bf16[128,3584]{1,0:T(8,128)(2,1)}, u32[]{:S(2)}) copy-start(bf16[128,3584]{1,0:T(8,128)(2,1)} %get-tuple-element.46) | copy-start | bytes 2752516
  224.8 4.1 %copy-start.6 = (bf16[128,1024]{1,0:T(8,128)(2,1)S(1)}, bf16[128,1024]{1,0:T(8,128)(2,1)}, u32[]{:S(2)}) copy-start(bf16[128,1024]{1,0:T(8,128)(2,1)} %copy-done.5) | copy-start | bytes 786436
  228.9 5.1 %copy-start.2 = (bf16[128,3584]{1,0:T(8,128)(2,1)S(1)}, bf16[128,3584]{1,0:T(8,128)(2,1)}, u32[]{:S(2)}) copy-start(bf16[128,3584]{1,0:T(8,128)(2,1)} %all-reduce.24.cloned.1.call-done) | copy-start | bytes 2752516
  234.0 25.7 %copy-start.11 = (bf16[4,4,1024]{2,1,0:T(4,128)(2,1)S(1)}, bf16[4,4,1024]{2,1,0:T(4,128)(2,1)}, u32[]{:S(2)}) copy-start(bf16[4,4,1024]{2,1,0:T(4,128)(2,1)} %param.13) | copy-start | bytes 98308
  234.0 25.7 %copy-start.12 = (bf16[4,4,1024]{2,1,0:T(4,128)(2,1)S(1)}, bf16[4,4,1024]{2,1,0:T(4,128)(2,1)}, u32[]{:S(2)}) copy-start(bf16[4,4,1024]{2,1,0:T(4,128)(2,1)} %param.18) | copy-start | bytes 98308
Sparse Core Ops, SparseCore 0:
  26.4 48.4 all-reduce.23
  85.8 74.6 all-reduce.21
  228.3 30.4 reduce-scatter.1

commit v11 on v9

--- a/solution.py
+++ b/solution.py
@@ -1,6 +1,7 @@
 import jax
 import jax.numpy as jnp
 from jax import lax
+from jax.experimental import pallas as pl
 from jax.sharding import PartitionSpec as P
 
 epsilon = 1e-05
@@ -18,6 +19,31 @@
     return (hidden, gate_grad, up_grad)
 
 
+def back_kernel(grad_ref, weight_ref, out_ref):
+    out_ref[...] = lax.dot_general(
+        grad_ref[...], weight_ref[...], contract_cols, preferred_element_type=jnp.float32
+    ).astype(out_ref.dtype)
+
+
+def back_project(grad, weight):
+    m, k = grad.shape
+    n = weight.shape[0]
+    tile = n // 4 if n % 512 == 0 else n
+    return pl.pallas_call(
+        back_kernel,
+        grid=(n // tile,),
+        in_specs=[
+            pl.BlockSpec((m, k), lambda j: (0, 0)),
+            pl.BlockSpec((tile, k), lambda j: (j, 0)),
+        ],
+        out_specs=pl.BlockSpec((m, tile), lambda j: (0, j)),
+        out_shape=jax.ShapeDtypeStruct((m, n), jnp.bfloat16),
+        cost_estimate=pl.CostEstimate(
+            flops=2 * m * k * n, bytes_accessed=2 * (m * k + n * k + m * n), transcendentals=0
+        ),
+    )(grad, weight)
+
+
 def per_device(inputs, norm_gain, w_gate, w_up, w_down, d_output, level_of_batch):
     groups = lax.axis_size("tensor")
     tensor_index = lax.axis_index("tensor")
@@ -30,9 +56,7 @@
     rows = grad_all.shape[0]
     start = tensor_index * local_rows
     flat_grad = grad_all.reshape(rows * batches, local_feat)
-    back_part = lax.dot_general(
-        flat_grad, w_down, contract_cols, preferred_element_type=jnp.float32
-    ).astype(jnp.bfloat16)
+    back_part = back_project(flat_grad, w_down)
     back_first = lax.psum(back_part, "dp")
     inputs_all, _ = lax.optimization_barrier((inputs.transpose(1, 0, 2), back_part))
     inputs_all = lax.all_gather(inputs_all, "tensor", axis=0, tiled=True).astype(jnp.float32)

time: 223 us -> 223 us (level)
  matrix products: 44 us -> 37.4 us
  Pallas kernels: 0 us -> 6.06 us
    dot_general x1 -> x0, matrix products: 6.65 us -> none  [per_device(): lax.dot_general(flat_grad, w_down, contract_cols, preferred_element_type=...]
    pallas_call x0 -> x1, Pallas kernels: none -> 6.06 us  [back_project(): pl.pallas_call(back_kernel, grid=(n // tile,), in_specs=[pl.BlockSpec((m,...]
where the time goes in v11:
time: 223 us; the launch traced here: 222 us
  waiting for transfers between devices  94.3 us (42%)
  blocking collectives  56.5 us (25%)
  matrix products  37.4 us (17%)
  between operations  14 us (6%)
  local copies, waits for them, and re-layouts  8.77 us (4%)
  Pallas kernels  6.06 us (3%)
  other arithmetic  4.98 us (2%)
    psum x1, waiting for transfers between devices, per_device(): gate_sum, up_sum = lax.psum(parts, 'dp')  77.6 us
    psum x1, waiting for transfers between devices, per_device(): back_first = lax.psum(back_part, 'dp')  16.7 us
    psum x1, blocking collectives, per_device(): reduced = lax.psum(jnp.concatenate([gain_part, row_all]), 'tensor')  12.8 us
    psum x1, blocking collectives, per_device(): square_sum = lax.psum(jnp.sum(inputs_all * inputs_all, axis=2).T, 'dp').T  12.5 us
    psum x1, blocking collectives, per_device(): row_all = lax.psum(reduced[local_feat:], 'dp').reshape(rows, batches)  11.2 us
    all_gather x1, blocking collectives, per_device(): lax.all_gather(d_output.transpose(1, 0, 2), 'tensor', axis=0, tiled=True)  10.8 us
    all_gather x1, blocking collectives, per_device(): lax.all_gather(inputs_all, 'tensor', axis=0, tiled=True).astype(jnp.float32)  9.28 us
    dot_general x1, matrix products, per_device(): lax.dot_general(flat_normed, gate_grad, contract_rows, preferred_element_...  6.6 us
  transfers between devices with their start and end apart: 3, of which 2 were waited for; matrix products, arithmetic and copies ran while one was open for 11% of the time, Pallas kernels for 0%

profile of v11, /device:TPU:0, one launch (start us, length us, event | category | flops | bytes accessed | tf_op | source)
XLA Modules:
  0.0 222.2 jit_solution(2074439776846959023)
XLA Ops:
  7.2 0.8 copy.46
  8.8 10.8 %all_gather.6 = bf16[32,4,1024]{2,1,0:T(4,128)(2,1)S(1)} all-gather(bf16[4,4,1024]{2,1,0:T(4,128)(2,1)S(1)} %bitcast.59), channel_id=1, replica_groups=mesh['dp'=4,'tensor'=8] {'tensor'}, dimensions={0}, use_global_device_ids=true | all-gather | bytes 294912 | tf_op jit(solution)/shard_map/all_gather | solution.py:55
  20.3 6.1 %shard_map.126 = bf16[128,3584]{1,0:T(8,128)(2,1)} custom-call(bf16[128,1024]{1,0:T(8,128)(2,1)} %reshape.45.grad_ref, bf16[3584,1024]{1,0:T(8,128)(2,1)} %weight_ref.1), custom_call_target="tpu_custom_call" | custom-call | flops 939524096 | bytes 8519680 | tf_op jit(solution)/shard_map/pallas_call | solution.py:32
  26.5 9.3 %all_gather.7 = bf16[32,4,1024]{2,1,0:T(4,128)(2,1)S(1)} all-gather(bf16[4,4,1024]{2,1,0:T(4,128)(2,1)S(1)} %bitcast.58), channel_id=1, replica_groups=mesh['dp'=4,'tensor'=8] {'tensor'}, dimensions={0}, use_global_device_ids=true | all-gather | bytes 294912 | tf_op jit(solution)/shard_map/all_gather | solution.py:62
  36.0 12.5 %psum.42 = f32[4,32]{1,0:T(4,128)S(1)} all-reduce(f32[4,32]{1,0:T(4,128)S(1)} %bitcast.60), channel_id=1, replica_groups=mesh['dp'=4,'tensor'=8] {'dp'}, use_global_device_ids=true, to_apply=%region_1.0 | all-reduce | flops 128 | bytes 1024 | tf_op jit(solution)/shard_map/psum | solution.py:63
  48.6 1.1 broadcast_multiply_fusion
  49.7 1.2 reshape.46
  50.9 5.3 %convolution_convert_fusion.4 = bf16[128,3584]{1,0:T(8,128)(2,1)} fusion(bf16[128,1024]{1,0:T(8,128)(2,1)S(1)} %reshape.46, bf16[1024,3584]{1,0:T(8,128)(2,1)} %param.9), kind=kOutput, calls=%fused_computation.4 | convolution fusion | flops 939982848 | bytes 8519680 | tf_op jit(solution)/shard_map/dot_general | solution.py:82
  56.2 2.1 convolution_convert_fusion.3
  58.3 16.7 %all-reduce.4.cloned.1.call-done = bf16[128,3584]{1,0:T(8,128)(2,1)} async-done(((bf16[128,3584]{1,0:T(8,128)(2,1)}), bf16[128,3584]{1,0:T(8,128)(2,1)}) %all-reduce.4.cloned.1.call-update) | async-done | bytes 917520 | tf_op jit(solution)/shard_map/psum | solution.py:60
  75.2 0.8 reshape.50
  76.0 1.0 reshape.49
  77.1 77.6 %all-reduce.6.cloned.1.call-done = (bf16[128,3584]{1,0:T(8,128)(2,1)}, bf16[128,3584]{1,0:T(8,128)(2,1)}) async-done(((bf16[128,3584]{1,0:T(8,128)(2,1)}, bf16[128,3584]{1,0:T(8,128)(2,1)}), (bf16[128,3584]{1,0:T(8,128)(2,1)}, bf16[128,3584]{1,0:T(8,128)(2,1)})) %all-reduce.6.cloned.1.call-update) | async-done | bytes 1835024 | tf_op jit(solution)/shard_map/psum | solution.py:86
  154.7 2.2 %fusion.1 = bf16[128,3584]{1,0:T(8,128)(2,1)S(1)} fusion(bf16[128,3584]{1,0:T(8,128)(2,1)} %get-tuple-element.35, f32[128]{0:T(128)S(1)} %mul.126, bf16[128,3584]{1,0:T(8,128)(2,1)} %get-tuple-element.36), kind=kLoop, calls=%fused_computation.12 | loop fusion | flops 4128768 | bytes 2753024 | tf_op jit(solution)/shard_map/convert_element_type | solution.py:16
  157.0 6.0 %fusion.25 = f32[128,1024]{1,0:T(8,128)S(1)} fusion(bf16[1024,3584]{1,0:T(8,128)(2,1)} %param.9, bf16[128,3584]{1,0:T(8,128)(2,1)S(1)} %copy-done.4, bf16[128,3584]{1,0:T(8,128)(2,1)} %all-reduce.4.cloned.1.call-done, bf16[128,3584]{1,0:T(8,128)(2,1)S(1)} %copy-done.5, f32[128]{0:T(128)S(1)} %mul.126), kind=kOutput, calls=%fused_computation.53 | convolution fusion | flops 945946624 | bytes 10617344 | tf_op jit(solution)/shard_map/dot_general | solution.py:97
  163.0 5.4 %convolution_convert_fusion.1 = bf16[1024,3584]{1,0:T(8,128)(2,1)} fusion(bf16[128,1024]{1,0:T(8,128)(2,1)S(1)} %reshape.46, bf16[128,3584]{1,0:T(8,128)(2,1)S(1)} %copy-done.12, f32[128]{0:T(128)S(1)} %mul.126, bf16[128,3584]{1,0:T(8,128)(2,1)S(1)} %copy-done.5), kind=kOutput, calls=%fused_computation.1 | convolution fusion | flops 947322880 | bytes 9437696 | tf_op jit(solution)/shard_map/dot_general | solution.py:137
  168.5 2.7 %multiply_reduce_fusion.1 = (f32[1024]{0:T(1024)S(1)}, f32[128]{0:T(128)S(1)}, bf16[128,1024]{1,0:T(8,128)(2,1)S(1)}) fusion(f32[128,1024]{1,0:T(8,128)S(1)} %copy-done.8, f32[128,1024]{1,0:T(8,128)S(1)} %copy-done.7, f32[1024]{0:T(1024)S(1)} %copy-done.11, f32[128,1024]{1,0:T(8,128)S(1)} %fusion.25, bf16[1024,3584]{1,0:T(8,128)(2,1)S(1)} %bitcast.55, ...), kind=kOutput, calls=%fused_computation.27 | convolution fusion | flops 944569216 | bytes 11019264 | tf_op jit(solution)/shard_map/dot_general | solution.py:99
  171.3 4.2 %convolution_convert_fusion.5 = bf16[128,1024]{1,0:T(8,128)(2,1)S(1)} fusion(bf16[128,3584]{1,0:T(8,128)(2,1)S(1)} %fusion.1, bf16[3584,1024]{1,0:T(8,128)(2,1)} %weight_ref.1), kind=kOutput, calls=%fused_computation.24 | convolution fusion | flops 939655168 | bytes 8519680 | tf_op jit(solution)/shard_map/dot_general | solution.py:96
  175.8 1.1 copy.37
  176.9 5.1 %convolution_convert_fusion = bf16[3584,1024]{1,0:T(8,128)(2,1)} fusion(bf16[128,3584]{1,0:T(8,128)(2,1)S(1)} %fusion.1, bf16[128,1024]{1,0:T(8,128)(2,1)S(1)} %copy-done.2), kind=kOutput, calls=%fused_computation | convolution fusion | flops 943194112 | bytes 8519680 | tf_op jit(solution)/shard_map/dot_general | solution.py:131
  182.1 12.8 %psum.46 = f32[1152]{0:T(1024)S(1)} all-reduce(f32[1152]{0:T(1024)S(1)} %pad_maximum_fusion.1), channel_id=1, replica_groups=mesh['dp'=4,'tensor'=8] {'tensor'}, use_global_device_ids=true, to_apply=%region_8.0 | all-reduce | flops 1152 | bytes 9216 | tf_op jit(solution)/shard_map/psum | solution.py:119
  195.7 11.2 %psum.47 = f32[32,4]{0,1:T(4,128)S(1)} all-reduce(f32[32,4]{0,1:T(4,128)S(1)} %copy.40), channel_id=1, replica_groups=mesh['dp'=4,'tensor'=8] {'dp'}, use_global_device_ids=true, to_apply=%region_9.0 | all-reduce | flops 128 | bytes 1024 | tf_op jit(solution)/shard_map/psum | solution.py:121
  207.5 6.6 %convolution_convert_fusion.2 = bf16[1024,3584]{1,0:T(8,128)(2,1)} fusion(bf16[128,1024]{1,0:T(8,128)(2,1)S(1)} %reshape.46, bf16[128,3584]{1,0:T(8,128)(2,1)S(1)} %copy-done.4, bf16[128,3584]{1,0:T(8,128)(2,1)} %all-reduce.4.cloned.1.call-done, bf16[128,3584]{1,0:T(8,128)(2,1)S(1)} %copy-done.6, f32[128]{0:T(128)S(1)} %mul.126), kind=kOutput, calls=%fused_computation.2 | convolution fusion | flops 949616640 | bytes 10355200 | tf_op jit(solution)/shard_map/dot_general | solution.py:134
  214.1 0.9 copy.41
  (66 shorter events, 5.1 us)
Async XLA Ops:
  7.2 67.8 %all-reduce.4.cloned.1.call-start = ((), (), s32[]{:S(2)}) async-start(), calls=%async_computation.1 | async-start | bytes 1835008 | tf_op jit(solution)/shard_map/psum | solution.py:60
  20.3 28.3 %copy-start.11 = (f32[1024]{0:T(1024)S(1)}, f32[1024]{0:T(1024)}, u32[]{:S(2)}) copy-start(f32[1024]{0:T(1024)} %param.8) | copy-start | bytes 12292
  26.4 128.3 %all-reduce.6.cloned.1.call-start = ((), (), s32[]{:S(2)}) async-start(), calls=%async_computation.3 | async-start | bytes 3670016 | tf_op jit(solution)/shard_map/psum | solution.py:86
  35.7 13.9 %copy-start = (bf16[32,4,1024]{2,1,0:T(4,128)(2,1)}, bf16[32,4,1024]{2,1,0:T(4,128)(2,1)S(1)}, u32[]{:S(2)}) copy-start(bf16[32,4,1024]{2,1,0:T(4,128)(2,1)S(1)} %all_gather.7) | copy-start | bytes 786436
  49.7 6.5 %slice-start = ((s8[7340032]{0:T(1024)(128)(4,1)}), s8[3145728]{0:T(1024)(128)(4,1)S(1)}, s32[]{:S(2)}) async-start(s8[7340032]{0:T(1024)(128)(4,1)} %bitcast.52), calls=%async_computation.4 | async-start | bytes 6291456
  50.9 5.3 %slice-start.1 = ((s8[7340032]{0:T(1024)(128)(4,1)}), s8[4194304]{0:T(1024)(128)(4,1)S(1)}, s32[]{:S(2)}) async-start(s8[7340032]{0:T(1024)(128)(4,1)} %bitcast.52), calls=%async_computation.5 | async-start | bytes 8388608
  58.2 16.9 %copy-start.1 = (bf16[32,4,1024]{2,1,0:T(4,128)(2,1)S(1)}, bf16[32,4,1024]{2,1,0:T(4,128)(2,1)}, u32[]{:S(2)}) copy-start(bf16[32,4,1024]{2,1,0:T(4,128)(2,1)} %copy-done) | copy-start | bytes 786436
  58.2 17.8 %copy-start.3 = (f32[32,4,1024]{2,1,0:T(4,128)S(1)}, f32[32,4,1024]{2,1,0:T(4,128)}, u32[]{:S(2)}) copy-start(f32[32,4,1024]{2,1,0:T(4,128)} %get-tuple-element.41) | copy-start | bytes 1572868
  58.2 18.8 %copy-start.13 = (s32[4]{0:T(128)S(1)}, s32[4]{0:T(128)}, u32[]{:S(2)}) copy-start(s32[4]{0:T(128)} %param.13) | copy-start | bytes 52
  75.0 139.1 %reduce-scatter.2.cloned.1.call-start = ((), (), s32[]{:S(2)}) async-start(), calls=%async_computation.2 | async-start | bytes 589824 | tf_op jit(solution)/shard_map/reduce_scatter | solution.py:124
  154.7 2.3 %copy-start.4 = (bf16[128,3584]{1,0:T(8,128)(2,1)S(1)}, bf16[128,3584]{1,0:T(8,128)(2,1)}, u32[]{:S(2)}) copy-start(bf16[128,3584]{1,0:T(8,128)(2,1)} %get-tuple-element.35) | copy-start | bytes 2752516
  154.7 2.3 %copy-start.5 = (bf16[128,3584]{1,0:T(8,128)(2,1)S(1)}, bf16[128,3584]{1,0:T(8,128)(2,1)}, u32[]{:S(2)}) copy-start(bf16[128,3584]{1,0:T(8,128)(2,1)} %get-tuple-element.36) | copy-start | bytes 2752516
  154.7 13.7 %slice-start.2 = ((s8[7340032]{0:T(1024)(128)(4,1)}), s8[4194304]{0:T(1024)(128)(4,1)S(1)}, s32[]{:S(2)}) async-start(s8[7340032]{0:T(1024)(128)(4,1)} %bitcast.54), calls=%async_computation.6 | async-start | bytes 8388608
  157.0 6.1 %copy-start.12 = (bf16[128,3584]{1,0:T(8,128)(2,1)S(1)}, bf16[128,3584]{1,0:T(8,128)(2,1)}, u32[]{:S(2)}) copy-start(bf16[128,3584]{1,0:T(8,128)(2,1)} %all-reduce.4.cloned.1.call-done) | copy-start | bytes 2752516
  157.0 11.5 %slice-start.3 = ((s8[7340032]{0:T(1024)(128)(4,1)}), s8[3145728]{0:T(1024)(128)(4,1)S(1)}, s32[]{:S(2)}) async-start(s8[7340032]{0:T(1024)(128)(4,1)} %bitcast.54), calls=%async_computation.7 | async-start | bytes 6291456
  163.0 5.4 %copy-start.7 = (f32[128,1024]{1,0:T(8,128)S(1)}, f32[128,1024]{1,0:T(8,128)}, u32[]{:S(2)}) copy-start(f32[128,1024]{1,0:T(8,128)} %reshape.50) | copy-start | bytes 1572868
  163.0 5.4 %copy-start.8 = (f32[128,1024]{1,0:T(8,128)S(1)}, f32[128,1024]{1,0:T(8,128)}, u32[]{:S(2)}) copy-start(f32[128,1024]{1,0:T(8,128)} %reshape.49) | copy-start | bytes 1572868
  175.5 1.4 copy-start.2
  176.9 30.6 %copy-start.6 = (bf16[128,3584]{1,0:T(8,128)(2,1)S(1)}, bf16[128,3584]{1,0:T(8,128)(2,1)}, u32[]{:S(2)}) copy-start(bf16[128,3584]{1,0:T(8,128)(2,1)} %get-tuple-element.36) | copy-start | bytes 2752516
  207.5 7.5 %copy-start.9 = (bf16[4,4,1024]{2,1,0:T(4,128)(2,1)S(1)}, bf16[4,4,1024]{2,1,0:T(4,128)(2,1)}, u32[]{:S(2)}) copy-start(bf16[4,4,1024]{2,1,0:T(4,128)(2,1)} %param.7) | copy-start | bytes 98308
  207.5 7.5 %copy-start.10 = (bf16[4,4,1024]{2,1,0:T(4,128)(2,1)S(1)}, bf16[4,4,1024]{2,1,0:T(4,128)(2,1)}, u32[]{:S(2)}) copy-start(bf16[4,4,1024]{2,1,0:T(4,128)(2,1)} %param.12) | copy-start | bytes 98308
Sparse Core Ops, SparseCore 0:
  26.5 48.3 all-reduce.3
  77.9 76.7 all-reduce.5
  177.0 33.1 reduce-scatter.1

commit v12 on v11

--- a/solution.py
+++ b/solution.py
@@ -103,14 +103,9 @@
     gate_grad = jnp.concatenate(gate_grads, axis=1)
     up_grad = jnp.concatenate(up_grads, axis=1)
 
-    stacked = jnp.stack(
-        [
-            down_part.reshape(rows, batches, local_feat),
-            normed_part.reshape(rows, batches, local_feat),
-        ],
-        axis=1,
-    ).astype(jnp.bfloat16)
-    stacked = stacked.reshape(rows, 2 * batches, local_feat)
+    stacked = jnp.concatenate(
+        [down_part.astype(jnp.bfloat16), normed_part.astype(jnp.bfloat16)], axis=1
+    ).reshape(rows, 2 * batches, local_feat)
     scaled_all = (inputs_all * row_scale_all[:, :, None]).reshape(rows * batches, local_feat)
     gain_part = jnp.sum(normed_part * scaled_all, axis=0)
     row_all = jnp.sum(
@@ -124,9 +119,9 @@
     shares = lax.psum_scatter(stacked, "tensor", scatter_dimension=0, tiled=True).astype(
         jnp.float32
     )
-    shares = shares.reshape(local_rows, 2, batches, local_feat)
-    down_output = shares[:, 0].transpose(1, 0, 2)
-    normed_grad = shares[:, 1].transpose(1, 0, 2)
+    shares = shares.reshape(local_rows, batches, 2, local_feat)
+    down_output = shares[:, :, 0].transpose(1, 0, 2)
+    normed_grad = shares[:, :, 1].transpose(1, 0, 2)
 
     down_out = lax.dot_general(
         hidden, flat_grad, contract_rows, preferred_element_type=jnp.float32

time: 223 us -> 220 us (0.987)
  matrix products: 37.4 us -> 34.9 us
    dot_general x1, matrix products: 4.2 us -> 1.24 us  [per_device(): down_term = jnp.dot(hidden, down_w, preferred_element_type=jnp.float32)]
where the time goes in v12:
time: 220 us
  waiting for transfers between devices  95.9 us (44%)
  blocking collectives  56.4 us (26%)
  matrix products  34.9 us (16%)
  between operations  14 us (6%)
  local copies, waits for them, and re-layouts  7.31 us (3%)
  Pallas kernels  6.05 us (3%)
  other arithmetic  4.96 us (2%)
    psum x1, waiting for transfers between devices, per_device(): gate_sum, up_sum = lax.psum(parts, 'dp')  79.1 us
    psum x1, waiting for transfers between devices, per_device(): back_first = lax.psum(back_part, 'dp')  16.7 us
    psum x1, blocking collectives, per_device(): reduced = lax.psum(jnp.concatenate([gain_part, row_all]), 'tensor')  12.8 us
    psum x1, blocking collectives, per_device(): square_sum = lax.psum(jnp.sum(inputs_all * inputs_all, axis=2).T, 'dp').T  12.4 us
    psum x1, blocking collectives, per_device(): row_all = lax.psum(reduced[local_feat:], 'dp').reshape(rows, batches)  11.1 us
    all_gather x1, blocking collectives, per_device(): lax.all_gather(d_output.transpose(1, 0, 2), 'tensor', axis=0, tiled=True)  10.8 us
    all_gather x1, blocking collectives, per_device(): lax.all_gather(inputs_all, 'tensor', axis=0, tiled=True).astype(jnp.float32)  9.28 us
    dot_general x1, matrix products, per_device(): lax.dot_general(flat_normed, gate_grad, contract_rows, preferred_element_...  6.6 us
  transfers between devices with their start and end apart: 3, of which 2 were waited for; matrix products, arithmetic and copies ran while one was open for 11% of the time, Pallas kernels for 0%

profile of v12, /device:TPU:0, one launch (start us, length us, event | category | flops | bytes accessed | tf_op | source)
XLA Modules:
  0.0 219.8 jit_solution(6099926884935335489)
XLA Ops:
  7.2 0.8 copy.43
  8.0 0.8 copy.42
  8.8 10.8 %all_gather.6 = bf16[32,4,1024]{2,1,0:T(4,128)(2,1)S(1)} all-gather(bf16[4,4,1024]{2,1,0:T(4,128)(2,1)S(1)} %bitcast.61), channel_id=1, replica_groups=mesh['dp'=4,'tensor'=8] {'tensor'}, dimensions={0}, use_global_device_ids=true | all-gather | bytes 294912 | tf_op jit(solution)/shard_map/all_gather | solution.py:55
  19.6 0.8 reshape.45.grad_ref
  20.3 6.1 %shard_map.126 = bf16[128,3584]{1,0:T(8,128)(2,1)} custom-call(bf16[128,1024]{1,0:T(8,128)(2,1)} %reshape.45.grad_ref, bf16[3584,1024]{1,0:T(8,128)(2,1)} %weight_ref.1), custom_call_target="tpu_custom_call" | custom-call | flops 939524096 | bytes 8519680 | tf_op jit(solution)/shard_map/pallas_call | solution.py:32
  26.4 9.3 %all_gather.7 = bf16[32,4,1024]{2,1,0:T(4,128)(2,1)S(1)} all-gather(bf16[4,4,1024]{2,1,0:T(4,128)(2,1)S(1)} %bitcast.60), channel_id=1, replica_groups=mesh['dp'=4,'tensor'=8] {'tensor'}, dimensions={0}, use_global_device_ids=true | all-gather | bytes 294912 | tf_op jit(solution)/shard_map/all_gather | solution.py:62
  36.0 12.4 %psum.42 = f32[4,32]{1,0:T(4,128)S(1)} all-reduce(f32[4,32]{1,0:T(4,128)S(1)} %bitcast.62), channel_id=1, replica_groups=mesh['dp'=4,'tensor'=8] {'dp'}, use_global_device_ids=true, to_apply=%region_1.0 | all-reduce | flops 128 | bytes 1024 | tf_op jit(solution)/shard_map/psum | solution.py:63
  48.6 1.1 broadcast_multiply_fusion
  49.7 1.2 reshape.46
  50.9 5.3 %convolution_convert_fusion.4 = bf16[128,3584]{1,0:T(8,128)(2,1)} fusion(bf16[128,1024]{1,0:T(8,128)(2,1)S(1)} %reshape.46, bf16[1024,3584]{1,0:T(8,128)(2,1)} %param.9), kind=kOutput, calls=%fused_computation.4 | convolution fusion | flops 939982848 | bytes 8519680 | tf_op jit(solution)/shard_map/dot_general | solution.py:82
  56.2 2.1 convolution_convert_fusion.3
  58.2 16.7 %all-reduce.4.cloned.1.call-done = bf16[128,3584]{1,0:T(8,128)(2,1)} async-done(((bf16[128,3584]{1,0:T(8,128)(2,1)}), bf16[128,3584]{1,0:T(8,128)(2,1)}) %all-reduce.4.cloned.1.call-update) | async-done | bytes 917520 | tf_op jit(solution)/shard_map/psum | solution.py:60
  75.6 79.1 %all-reduce.6.cloned.1.call-done = (bf16[128,3584]{1,0:T(8,128)(2,1)}, bf16[128,3584]{1,0:T(8,128)(2,1)}) async-done(((bf16[128,3584]{1,0:T(8,128)(2,1)}, bf16[128,3584]{1,0:T(8,128)(2,1)}), (bf16[128,3584]{1,0:T(8,128)(2,1)}, bf16[128,3584]{1,0:T(8,128)(2,1)})) %all-reduce.6.cloned.1.call-update) | async-done | bytes 1835024 | tf_op jit(solution)/shard_map/psum | solution.py:86
  154.7 2.2 %fusion.1 = bf16[128,3584]{1,0:T(8,128)(2,1)S(1)} fusion(bf16[128,3584]{1,0:T(8,128)(2,1)} %get-tuple-element.35, f32[128]{0:T(128)S(1)} %mul.126, bf16[128,3584]{1,0:T(8,128)(2,1)} %get-tuple-element.36), kind=kLoop, calls=%fused_computation.12 | loop fusion | flops 4128768 | bytes 2753024 | tf_op jit(solution)/shard_map/convert_element_type | solution.py:16
  157.0 6.0 %fusion.25 = f32[128,1024]{1,0:T(8,128)S(1)} fusion(bf16[1024,3584]{1,0:T(8,128)(2,1)} %param.9, bf16[128,3584]{1,0:T(8,128)(2,1)S(1)} %copy-done.4, bf16[128,3584]{1,0:T(8,128)(2,1)} %all-reduce.4.cloned.1.call-done, bf16[128,3584]{1,0:T(8,128)(2,1)S(1)} %copy-done.5, f32[128]{0:T(128)S(1)} %mul.126), kind=kOutput, calls=%fused_computation.53 | convolution fusion | flops 945946624 | bytes 10617344 | tf_op jit(solution)/shard_map/dot_general | solution.py:97
  163.0 5.4 %convolution_convert_fusion.1 = bf16[1024,3584]{1,0:T(8,128)(2,1)} fusion(bf16[128,1024]{1,0:T(8,128)(2,1)S(1)} %reshape.46, bf16[128,3584]{1,0:T(8,128)(2,1)S(1)} %copy-done.11, f32[128]{0:T(128)S(1)} %mul.126, bf16[128,3584]{1,0:T(8,128)(2,1)S(1)} %copy-done.5), kind=kOutput, calls=%fused_computation.1 | convolution fusion | flops 947322880 | bytes 9437696 | tf_op jit(solution)/shard_map/dot_general | solution.py:132
  168.4 1.2 convolution_convert_fusion.5
  170.3 3.2 %multiply_reduce_fusion.1 = (f32[1024]{0:T(1024)S(1)}, f32[128]{0:T(128)}, bf16[128,1024]{1,0:T(8,128)(2,1)S(1)}) fusion(f32[128,1024]{1,0:T(8,128)S(1)} %reshape.50, f32[128,1024]{1,0:T(8,128)S(1)} %reshape.51, f32[1024]{0:T(1024)S(1)} %copy-done.9, f32[128,1024]{1,0:T(8,128)S(1)} %fusion.25, bf16[1024,3584]{1,0:T(8,128)(2,1)S(1)} %bitcast.58, ...), kind=kOutput, calls=%fused_computation.27 | convolution fusion | flops 944569216 | bytes 11019264 | tf_op jit(solution)/shard_map/dot_general | solution.py:99
  173.5 1.0 reshape.47
  174.6 5.1 %convolution_convert_fusion = bf16[3584,1024]{1,0:T(8,128)(2,1)} fusion(bf16[128,3584]{1,0:T(8,128)(2,1)S(1)} %fusion.1, bf16[128,1024]{1,0:T(8,128)(2,1)S(1)} %copy-done.2), kind=kOutput, calls=%fused_computation | convolution fusion | flops 943194112 | bytes 8519680 | tf_op jit(solution)/shard_map/dot_general | solution.py:126
  179.7 12.8 %psum.46 = f32[1152]{0:T(1024)S(1)} all-reduce(f32[1152]{0:T(1024)S(1)} %pad_maximum_fusion.1), channel_id=1, replica_groups=mesh['dp'=4,'tensor'=8] {'tensor'}, use_global_device_ids=true, to_apply=%region_8.0 | all-reduce | flops 1152 | bytes 9216 | tf_op jit(solution)/shard_map/psum | solution.py:114
  193.3 11.1 %psum.47 = f32[32,4]{0,1:T(4,128)S(1)} all-reduce(f32[32,4]{0,1:T(4,128)S(1)} %copy.37), channel_id=1, replica_groups=mesh['dp'=4,'tensor'=8] {'dp'}, use_global_device_ids=true, to_apply=%region_9.0 | all-reduce | flops 128 | bytes 1024 | tf_op jit(solution)/shard_map/psum | solution.py:116
  205.1 6.6 %convolution_convert_fusion.2 = bf16[1024,3584]{1,0:T(8,128)(2,1)} fusion(bf16[128,1024]{1,0:T(8,128)(2,1)S(1)} %reshape.46, bf16[128,3584]{1,0:T(8,128)(2,1)S(1)} %copy-done.4, bf16[128,3584]{1,0:T(8,128)(2,1)} %all-reduce.4.cloned.1.call-done, bf16[128,3584]{1,0:T(8,128)(2,1)S(1)} %copy-done.6, f32[128]{0:T(128)S(1)} %mul.126), kind=kOutput, calls=%fused_computation.2 | convolution fusion | flops 949616640 | bytes 10355200 | tf_op jit(solution)/shard_map/dot_general | solution.py:129
  211.7 0.9 copy.35
  (65 shorter events, 4.0 us)
Async XLA Ops:
  7.2 67.8 %all-reduce.4.cloned.1.call-start = ((), (), s32[]{:S(2)}) async-start(), calls=%async_computation.1 | async-start | bytes 1835008 | tf_op jit(solution)/shard_map/psum | solution.py:60
  20.3 28.3 %copy-start.9 = (f32[1024]{0:T(1024)S(1)}, f32[1024]{0:T(1024)}, u32[]{:S(2)}) copy-start(f32[1024]{0:T(1024)} %param.8) | copy-start | bytes 12292
  26.4 128.3 %all-reduce.6.cloned.1.call-start = ((), (), s32[]{:S(2)}) async-start(), calls=%async_computation.3 | async-start | bytes 3670016 | tf_op jit(solution)/shard_map/psum | solution.py:86
  35.7 13.9 %copy-start = (bf16[32,4,1024]{2,1,0:T(4,128)(2,1)}, bf16[32,4,1024]{2,1,0:T(4,128)(2,1)S(1)}, u32[]{:S(2)}) copy-start(bf16[32,4,1024]{2,1,0:T(4,128)(2,1)S(1)} %all_gather.7) | copy-start | bytes 786436
  49.7 6.5 %slice-start.2 = ((s8[7340032]{0:T(1024)(128)(4,1)}), s8[3145728]{0:T(1024)(128)(4,1)S(1)}, s32[]{:S(2)}) async-start(s8[7340032]{0:T(1024)(128)(4,1)} %bitcast.55), calls=%async_computation.6 | async-start | bytes 6291456
  50.8 5.3 %slice-start.3 = ((s8[7340032]{0:T(1024)(128)(4,1)}), s8[4194304]{0:T(1024)(128)(4,1)S(1)}, s32[]{:S(2)}) async-start(s8[7340032]{0:T(1024)(128)(4,1)} %bitcast.55), calls=%async_computation.7 | async-start | bytes 8388608
  58.2 17.0 %copy-start.1 = (bf16[32,4,1024]{2,1,0:T(4,128)(2,1)S(1)}, bf16[32,4,1024]{2,1,0:T(4,128)(2,1)}, u32[]{:S(2)}) copy-start(bf16[32,4,1024]{2,1,0:T(4,128)(2,1)} %copy-done) | copy-start | bytes 786436
  58.2 17.0 %copy-start.3 = (f32[32,4,1024]{2,1,0:T(4,128)S(1)}, f32[32,4,1024]{2,1,0:T(4,128)}, u32[]{:S(2)}) copy-start(f32[32,4,1024]{2,1,0:T(4,128)} %get-tuple-element.41) | copy-start | bytes 1572868
  58.2 17.2 %copy-start.12 = (s32[4]{0:T(128)S(1)}, s32[4]{0:T(128)}, u32[]{:S(2)}) copy-start(s32[4]{0:T(128)} %param.13) | copy-start | bytes 52
  74.9 136.7 %reduce-scatter.2.cloned.1.call-start = ((), (), s32[]{:S(2)}) async-start(), calls=%async_computation.2 | async-start | bytes 589824 | tf_op jit(solution)/shard_map/reduce_scatter | solution.py:119
  154.7 2.3 %copy-start.4 = (bf16[128,3584]{1,0:T(8,128)(2,1)S(1)}, bf16[128,3584]{1,0:T(8,128)(2,1)}, u32[]{:S(2)}) copy-start(bf16[128,3584]{1,0:T(8,128)(2,1)} %get-tuple-element.35) | copy-start | bytes 2752516
  154.7 2.3 %copy-start.5 = (bf16[128,3584]{1,0:T(8,128)(2,1)S(1)}, bf16[128,3584]{1,0:T(8,128)(2,1)}, u32[]{:S(2)}) copy-start(bf16[128,3584]{1,0:T(8,128)(2,1)} %get-tuple-element.36) | copy-start | bytes 2752516
  154.7 13.7 %slice-start = ((s8[7340032]{0:T(1024)(128)(4,1)}), s8[4194304]{0:T(1024)(128)(4,1)S(1)}, s32[]{:S(2)}) async-start(s8[7340032]{0:T(1024)(128)(4,1)} %bitcast.53), calls=%async_computation.4 | async-start | bytes 8388608
  156.9 6.1 %copy-start.11 = (bf16[128,3584]{1,0:T(8,128)(2,1)S(1)}, bf16[128,3584]{1,0:T(8,128)(2,1)}, u32[]{:S(2)}) copy-start(bf16[128,3584]{1,0:T(8,128)(2,1)} %all-reduce.4.cloned.1.call-done) | copy-start | bytes 2752516
  157.0 11.5 %slice-start.1 = ((s8[7340032]{0:T(1024)(128)(4,1)}), s8[3145728]{0:T(1024)(128)(4,1)S(1)}, s32[]{:S(2)}) async-start(s8[7340032]{0:T(1024)(128)(4,1)} %bitcast.53), calls=%async_computation.5 | async-start | bytes 6291456
  163.0 6.7 %slice-start.4 = ((s8[7340032]{0:T(1024)(128)(4,1)}), s8[4194304]{0:T(1024)(128)(4,1)S(1)}, s32[]{:S(2)}) async-start(s8[7340032]{0:T(1024)(128)(4,1)} %bitcast.57), calls=%async_computation.8 | async-start | bytes 8388608
  168.4 1.9 slice-start.5
  173.5 1.0 copy-start.2
  174.5 5.2 %copy-start.10 = (f32[128]{0:T(128)S(1)}, f32[128]{0:T(128)}, u32[]{:S(2)}) copy-start(f32[128]{0:T(128)} %get-tuple-element.34) | copy-start | bytes 1540
  174.6 30.5 %copy-start.6 = (bf16[128,3584]{1,0:T(8,128)(2,1)S(1)}, bf16[128,3584]{1,0:T(8,128)(2,1)}, u32[]{:S(2)}) copy-start(bf16[128,3584]{1,0:T(8,128)(2,1)} %get-tuple-element.36) | copy-start | bytes 2752516
  205.1 7.5 %copy-start.7 = (bf16[4,4,1024]{2,1,0:T(4,128)(2,1)S(1)}, bf16[4,4,1024]{2,1,0:T(4,128)(2,1)}, u32[]{:S(2)}) copy-start(bf16[4,4,1024]{2,1,0:T(4,128)(2,1)} %param.7) | copy-start | bytes 98308
  205.1 7.5 %copy-start.8 = (bf16[4,4,1024]{2,1,0:T(4,128)(2,1)S(1)}, bf16[4,4,1024]{2,1,0:T(4,128)(2,1)}, u32[]{:S(2)}) copy-start(bf16[4,4,1024]{2,1,0:T(4,128)(2,1)} %param.12) | copy-start | bytes 98308
Sparse Core Ops, SparseCore 0:
  26.5 48.3 all-reduce.3
  77.9 76.7 all-reduce.5
  174.6 33.1 reduce-scatter.1

commit v13 on v12

--- a/solution.py
+++ b/solution.py
@@ -52,23 +52,23 @@
     full_width = local_feat * lax.axis_size("dp")
     batches, local_rows, _ = inputs.shape
     wide_inputs = inputs.astype(jnp.float32)
-    grad_all = lax.all_gather(d_output.transpose(1, 0, 2), "tensor", axis=0, tiled=True)
-    rows = grad_all.shape[0]
+    grad_all = lax.all_gather(d_output, "tensor", axis=1, tiled=True)
+    rows = grad_all.shape[1]
     start = tensor_index * local_rows
     flat_grad = grad_all.reshape(rows * batches, local_feat)
     back_part = back_project(flat_grad, w_down)
     back_first = lax.psum(back_part, "dp")
-    inputs_all, _ = lax.optimization_barrier((inputs.transpose(1, 0, 2), back_part))
-    inputs_all = lax.all_gather(inputs_all, "tensor", axis=0, tiled=True).astype(jnp.float32)
-    square_sum = lax.psum(jnp.sum(inputs_all * inputs_all, axis=2).T, "dp").T
+    inputs_all, _ = lax.optimization_barrier((inputs, back_part))
+    inputs_all = lax.all_gather(inputs_all, "tensor", axis=1, tiled=True).astype(jnp.float32)
+    square_sum = lax.psum(jnp.sum(inputs_all * inputs_all, axis=2), "dp")
     row_scale_all = lax.rsqrt(square_sum / full_width + epsilon)
     normed_all = (inputs_all * row_scale_all[:, :, None] * norm_gain).astype(jnp.bfloat16)
-    row_scale = lax.dynamic_slice_in_dim(row_scale_all, start, local_rows, axis=0).T
+    row_scale = lax.dynamic_slice_in_dim(row_scale_all, start, local_rows, axis=1)
 
     flat_normed = normed_all.reshape(rows * batches, local_feat)
     halvings = 3 - level_of_batch
     active = (tensor_index < jnp.right_shift(groups, halvings)).astype(jnp.float32)
-    active_mask = jnp.tile(active, rows)[:, None]
+    active_mask = jnp.repeat(active, rows)[:, None]
     chunks = 1
     width = local_cols // chunks
     down_part = None
@@ -105,7 +105,8 @@
 
     stacked = jnp.concatenate(
         [down_part.astype(jnp.bfloat16), normed_part.astype(jnp.bfloat16)], axis=1
-    ).reshape(rows, 2 * batches, local_feat)
+    ).reshape(batches, rows, 2 * local_feat)
+    stacked = stacked.transpose(1, 0, 2).reshape(rows, 2 * batches, local_feat)
     scaled_all = (inputs_all * row_scale_all[:, :, None]).reshape(rows * batches, local_feat)
     gain_part = jnp.sum(normed_part * scaled_all, axis=0)
     row_all = jnp.sum(
@@ -113,8 +114,8 @@
     )
     reduced = lax.psum(jnp.concatenate([gain_part, row_all]), "tensor")
     d_gain = reduced[:local_feat]
-    row_all = lax.psum(reduced[local_feat:], "dp").reshape(rows, batches)
-    row_product = lax.dynamic_slice_in_dim(row_all, start, local_rows, axis=0).T
+    row_all = lax.psum(reduced[local_feat:], "dp").reshape(batches, rows)
+    row_product = lax.dynamic_slice_in_dim(row_all, start, local_rows, axis=1)
     hidden, flat_grad, _ = lax.optimization_barrier((hidden, flat_grad, stacked))
     shares = lax.psum_scatter(stacked, "tensor", scatter_dimension=0, tiled=True).astype(
         jnp.float32

time: 220 us -> 219 us (level)
  waiting for transfers between devices: 95.9 us -> 98.2 us
    psum x1, waiting for transfers between devices: 16.7 us -> 18.9 us  [per_device(): back_first = lax.psum(back_part, 'dp')]
  transfers between devices with their start and end apart: 3 -> 3, of which waited for: 2 -> 2; matrix products, arithmetic and copies ran while one was open for 11% -> 10% of each run, Pallas kernels for 0% -> 0%
where the time goes in v13:
time: 219 us
  waiting for transfers between devices  98.2 us (45%)
  blocking collectives  56.5 us (26%)
  matrix products  34.4 us (16%)
  between operations  14 us (6%)
  Pallas kernels  6.05 us (3%)
  local copies, waits for them, and re-layouts  5.36 us (2%)
  other arithmetic  4.04 us (2%)
    psum x1, waiting for transfers between devices, per_device(): gate_sum, up_sum = lax.psum(parts, 'dp')  79.2 us
    psum x1, waiting for transfers between devices, per_device(): back_first = lax.psum(back_part, 'dp')  18.9 us
    psum x1, blocking collectives, per_device(): reduced = lax.psum(jnp.concatenate([gain_part, row_all]), 'tensor')  12.8 us
    psum x1, blocking collectives, per_device(): square_sum = lax.psum(jnp.sum(inputs_all * inputs_all, axis=2), 'dp')  12.5 us
    psum x1, blocking collectives, per_device(): row_all = lax.psum(reduced[local_feat:], 'dp').reshape(batches, rows)  11.1 us
    all_gather x1, blocking collectives, per_device(): grad_all = lax.all_gather(d_output, 'tensor', axis=1, tiled=True)  10.8 us
    all_gather x1, blocking collectives, per_device(): lax.all_gather(inputs_all, 'tensor', axis=1, tiled=True).astype(jnp.float32)  9.28 us
    dot_general x1, matrix products, per_device(): lax.dot_general(flat_normed, gate_grad, contract_rows, preferred_element_...  6.6 us
  transfers between devices with their start and end apart: 3, of which 2 were waited for; matrix products, arithmetic and copies ran while one was open for 10% of the time, Pallas kernels for 0%

profile of v13, /device:TPU:0, one launch (start us, length us, event | category | flops | bytes accessed | tf_op | source)
XLA Modules:
  0.0 218.8 jit_solution(1829429125315129699)
XLA Ops:
  7.2 0.8 copy.26
  8.0 10.8 %all_gather.6 = bf16[4,32,1024]{2,0,1:T(4,128)(2,1)S(1)} all-gather(bf16[4,4,1024]{2,0,1:T(4,128)(2,1)S(1)} %copy.26), channel_id=1, replica_groups=mesh['dp'=4,'tensor'=8] {'tensor'}, dimensions={1}, use_global_device_ids=true | all-gather | bytes 294912 | tf_op jit(solution)/shard_map/all_gather | solution.py:55
  18.8 0.8 copy.27
  19.6 6.1 %shard_map.126 = bf16[128,3584]{1,0:T(8,128)(2,1)} custom-call(bf16[128,1024]{1,0:T(8,128)(2,1)} %bitcast.67, bf16[3584,1024]{1,0:T(8,128)(2,1)} %weight_ref.1), custom_call_target="tpu_custom_call" | custom-call | flops 939524096 | bytes 8519680 | tf_op jit(solution)/shard_map/pallas_call | solution.py:32
  25.8 9.3 %all_gather.7 = bf16[4,32,1024]{2,0,1:T(4,128)(2,1)S(1)} all-gather(bf16[4,4,1024]{2,0,1:T(4,128)(2,1)S(1)} %copy.28), channel_id=1, replica_groups=mesh['dp'=4,'tensor'=8] {'tensor'}, dimensions={1}, use_global_device_ids=true | all-gather | bytes 294912 | tf_op jit(solution)/shard_map/all_gather | solution.py:62
  35.2 12.5 %psum.42 = f32[4,32]{1,0:T(4,128)S(1)} all-reduce(f32[4,32]{1,0:T(4,128)S(1)} %multiply_reduce_fusion), channel_id=1, replica_groups=mesh['dp'=4,'tensor'=8] {'dp'}, use_global_device_ids=true, to_apply=%region_1.0 | all-reduce | flops 128 | bytes 1024 | tf_op jit(solution)/shard_map/psum | solution.py:63
  47.9 5.3 %convolution_convert_fusion.4 = bf16[128,3584]{1,0:T(8,128)(2,1)} fusion(bf16[128,1024]{1,0:T(8,128)(2,1)S(1)} %bitcast.63, bf16[1024,3584]{1,0:T(8,128)(2,1)} %param.9), kind=kOutput, calls=%fused_computation.4 | convolution fusion | flops 939982848 | bytes 8519680 | tf_op jit(solution)/shard_map/dot_general | solution.py:82
  53.2 2.1 convolution_convert_fusion.3
  55.3 18.9 %all-reduce.4.cloned.1.call-done = bf16[128,3584]{1,0:T(8,128)(2,1)} async-done(((bf16[128,3584]{1,0:T(8,128)(2,1)}), bf16[128,3584]{1,0:T(8,128)(2,1)}) %all-reduce.4.cloned.1.call-update) | async-done | bytes 917520 | tf_op jit(solution)/shard_map/psum | solution.py:60
  74.7 79.2 %all-reduce.6.cloned.1.call-done = (bf16[128,3584]{1,0:T(8,128)(2,1)}, bf16[128,3584]{1,0:T(8,128)(2,1)}) async-done(((bf16[128,3584]{1,0:T(8,128)(2,1)}, bf16[128,3584]{1,0:T(8,128)(2,1)}), (bf16[128,3584]{1,0:T(8,128)(2,1)}, bf16[128,3584]{1,0:T(8,128)(2,1)})) %all-reduce.6.cloned.1.call-update) | async-done | bytes 1835024 | tf_op jit(solution)/shard_map/psum | solution.py:86
  154.0 2.2 %fusion.1 = bf16[128,3584]{1,0:T(8,128)(2,1)S(1)} fusion(bf16[128,3584]{1,0:T(8,128)(2,1)} %get-tuple-element.21, f32[128]{0:T(128)S(1)} %mul.126, bf16[128,3584]{1,0:T(8,128)(2,1)} %get-tuple-element.22), kind=kLoop, calls=%fused_computation.12 | loop fusion | flops 4128768 | bytes 2753024 | tf_op jit(solution)/shard_map/convert_element_type | solution.py:16
  156.2 6.0 %fusion.27 = f32[128,1024]{1,0:T(8,128)S(1)} fusion(bf16[1024,3584]{1,0:T(8,128)(2,1)} %param.9, bf16[128,3584]{1,0:T(8,128)(2,1)S(1)} %copy-done.1, bf16[128,3584]{1,0:T(8,128)(2,1)} %all-reduce.4.cloned.1.call-done, bf16[128,3584]{1,0:T(8,128)(2,1)S(1)} %copy-done.2, f32[128]{0:T(128)S(1)} %mul.126), kind=kOutput, calls=%fused_computation.55 | convolution fusion | flops 945946624 | bytes 10617344 | tf_op jit(solution)/shard_map/dot_general | solution.py:97
  162.3 5.4 %convolution_convert_fusion.1 = bf16[1024,3584]{1,0:T(8,128)(2,1)} fusion(bf16[128,1024]{1,0:T(8,128)(2,1)S(1)} %bitcast.65, bf16[128,3584]{1,0:T(8,128)(2,1)S(1)} %copy-done.7, f32[128]{0:T(128)S(1)} %mul.126, bf16[128,3584]{1,0:T(8,128)(2,1)S(1)} %copy-done.2), kind=kOutput, calls=%fused_computation.1 | convolution fusion | flops 947322880 | bytes 9437696 | tf_op jit(solution)/shard_map/dot_general | solution.py:133
  167.7 1.2 convolution_convert_fusion.5
  169.0 0.6 slice-done.5
  169.6 2.6 %fusion.14 = (f32[1024]{0:T(1024)S(1)}, f32[128]{0:T(128)S(1)}, bf16[128,1024]{1,0:T(8,128)(2,1)S(1)}) fusion(f32[4,32,1024]{2,1,0:T(8,128)S(1)} %get-tuple-element.27, f32[4,32,1024]{2,1,0:T(8,128)S(1)} %copy_convert_fusion, f32[1024]{0:T(1024)S(1)} %copy-done.6, f32[128,1024]{1,0:T(8,128)S(1)} %fusion.27, bf16[1024,3584]{1,0:T(8,128)(2,1)S(1)} %bitcast.62, ...), kind=kOutput, calls=%fused_computation.30 | convolution fusion | flops 944569216 | bytes 11019264 | tf_op jit(solution)/shard_map/dot_general | solution.py:99
  172.7 0.9 reshape.50
  173.7 5.1 %convolution_convert_fusion = bf16[3584,1024]{1,0:T(8,128)(2,1)} fusion(bf16[128,3584]{1,0:T(8,128)(2,1)S(1)} %fusion.1, bf16[128,1024]{1,0:T(8,128)(2,1)S(1)} %bitcast.68), kind=kOutput, calls=%fused_computation | convolution fusion | flops 943194112 | bytes 8519680 | tf_op jit(solution)/shard_map/dot_general | solution.py:127
  178.8 12.8 %psum.46 = f32[1152]{0:T(1024)S(1)} all-reduce(f32[1152]{0:T(1024)S(1)} %pad_maximum_fusion.1), channel_id=1, replica_groups=mesh['dp'=4,'tensor'=8] {'tensor'}, use_global_device_ids=true, to_apply=%region_8.0 | all-reduce | flops 1152 | bytes 9216 | tf_op jit(solution)/shard_map/psum | solution.py:115
  192.3 11.1 %psum.47 = f32[4,32]{1,0:T(4,128)S(1)} all-reduce(f32[4,32]{1,0:T(4,128)S(1)} %reshape.55), channel_id=1, replica_groups=mesh['dp'=4,'tensor'=8] {'dp'}, use_global_device_ids=true, to_apply=%region_9.0 | all-reduce | flops 128 | bytes 1024 | tf_op jit(solution)/shard_map/psum | solution.py:117
  203.4 0.7 fusion.23
  204.1 6.6 %convolution_convert_fusion.2 = bf16[1024,3584]{1,0:T(8,128)(2,1)} fusion(bf16[128,1024]{1,0:T(8,128)(2,1)S(1)} %bitcast.66, bf16[128,3584]{1,0:T(8,128)(2,1)S(1)} %copy-done.1, bf16[128,3584]{1,0:T(8,128)(2,1)} %all-reduce.4.cloned.1.call-done, bf16[128,3584]{1,0:T(8,128)(2,1)S(1)} %copy-done.3, f32[128]{0:T(128)S(1)} %mul.126), kind=kOutput, calls=%fused_computation.2 | convolution fusion | flops 949616640 | bytes 10355200 | tf_op jit(solution)/shard_map/dot_general | solution.py:130
  210.7 0.9 copy.31
  211.6 0.7 fusion.17
  (53 shorter events, 2.1 us)
Async XLA Ops:
  7.2 67.0 %all-reduce.4.cloned.1.call-start = ((), (), s32[]{:S(2)}) async-start(), calls=%async_computation.1 | async-start | bytes 1835008 | tf_op jit(solution)/shard_map/psum | solution.py:60
  19.6 6.1 %copy-start.4 = (bf16[4,4,1024]{2,1,0:T(4,128)(2,1)S(1)}, bf16[4,4,1024]{2,1,0:T(4,128)(2,1)}, u32[]{:S(2)}) copy-start(bf16[4,4,1024]{2,1,0:T(4,128)(2,1)} %param.7) | copy-start | bytes 98308
  19.6 28.1 %copy-start.6 = (f32[1024]{0:T(1024)S(1)}, f32[1024]{0:T(1024)}, u32[]{:S(2)}) copy-start(f32[1024]{0:T(1024)} %param.8) | copy-start | bytes 12292
  25.7 128.3 %all-reduce.6.cloned.1.call-start = ((), (), s32[]{:S(2)}) async-start(), calls=%async_computation.3 | async-start | bytes 3670016 | tf_op jit(solution)/shard_map/psum | solution.py:86
  47.7 5.5 %slice-start.2 = ((s8[7340032]{0:T(1024)(128)(4,1)}), s8[4194304]{0:T(1024)(128)(4,1)S(1)}, s32[]{:S(2)}) async-start(s8[7340032]{0:T(1024)(128)(4,1)} %bitcast.59), calls=%async_computation.6 | async-start | bytes 8388608
  47.8 5.4 %slice-start.3 = ((s8[7340032]{0:T(1024)(128)(4,1)}), s8[3145728]{0:T(1024)(128)(4,1)S(1)}, s32[]{:S(2)}) async-start(s8[7340032]{0:T(1024)(128)(4,1)} %bitcast.59), calls=%async_computation.7 | async-start | bytes 6291456
  55.3 19.2 %copy-start.8 = (s32[4]{0:T(128)S(1)}, s32[4]{0:T(128)}, u32[]{:S(2)}) copy-start(s32[4]{0:T(128)} %param.13) | copy-start | bytes 52
  74.2 136.5 %reduce-scatter.2.cloned.1.call-start = ((), (), s32[]{:S(2)}) async-start(), calls=%async_computation.2 | async-start | bytes 589824 | tf_op jit(solution)/shard_map/reduce_scatter | solution.py:120
  154.0 2.3 %copy-start.1 = (bf16[128,3584]{1,0:T(8,128)(2,1)S(1)}, bf16[128,3584]{1,0:T(8,128)(2,1)}, u32[]{:S(2)}) copy-start(bf16[128,3584]{1,0:T(8,128)(2,1)} %get-tuple-element.21) | copy-start | bytes 2752516
  154.0 2.3 %copy-start.2 = (bf16[128,3584]{1,0:T(8,128)(2,1)S(1)}, bf16[128,3584]{1,0:T(8,128)(2,1)}, u32[]{:S(2)}) copy-start(bf16[128,3584]{1,0:T(8,128)(2,1)} %get-tuple-element.22) | copy-start | bytes 2752516
  154.0 13.7 %slice-start = ((s8[7340032]{0:T(1024)(128)(4,1)}), s8[4194304]{0:T(1024)(128)(4,1)S(1)}, s32[]{:S(2)}) async-start(s8[7340032]{0:T(1024)(128)(4,1)} %bitcast.57), calls=%async_computation.4 | async-start | bytes 8388608
  156.2 6.1 %copy-start.7 = (bf16[128,3584]{1,0:T(8,128)(2,1)S(1)}, bf16[128,3584]{1,0:T(8,128)(2,1)}, u32[]{:S(2)}) copy-start(bf16[128,3584]{1,0:T(8,128)(2,1)} %all-reduce.4.cloned.1.call-done) | copy-start | bytes 2752516
  156.2 11.5 %slice-start.1 = ((s8[7340032]{0:T(1024)(128)(4,1)}), s8[3145728]{0:T(1024)(128)(4,1)S(1)}, s32[]{:S(2)}) async-start(s8[7340032]{0:T(1024)(128)(4,1)} %bitcast.57), calls=%async_computation.5 | async-start | bytes 6291456
  162.3 6.7 %slice-start.4 = ((s8[7340032]{0:T(1024)(128)(4,1)}), s8[4194304]{0:T(1024)(128)(4,1)S(1)}, s32[]{:S(2)}) async-start(s8[7340032]{0:T(1024)(128)(4,1)} %bitcast.61), calls=%async_computation.8 | async-start | bytes 8388608
  167.7 1.9 slice-start.5
  172.2 1.4 copy-start
  173.7 30.4 %copy-start.3 = (bf16[128,3584]{1,0:T(8,128)(2,1)S(1)}, bf16[128,3584]{1,0:T(8,128)(2,1)}, u32[]{:S(2)}) copy-start(bf16[128,3584]{1,0:T(8,128)(2,1)} %get-tuple-element.22) | copy-start | bytes 2752516
  204.1 7.5 %copy-start.5 = (bf16[4,4,1024]{2,1,0:T(4,128)(2,1)S(1)}, bf16[4,4,1024]{2,1,0:T(4,128)(2,1)}, u32[]{:S(2)}) copy-start(bf16[4,4,1024]{2,1,0:T(4,128)(2,1)} %param.12) | copy-start | bytes 98308
Sparse Core Ops, SparseCore 0:
  25.8 48.3 all-reduce.3
  77.2 76.7 all-reduce.5
  173.8 33.1 reduce-scatter.1

commit v14 on v13

--- a/solution.py
+++ b/solution.py
@@ -112,9 +112,12 @@
     row_all = jnp.sum(
         normed_part * (norm_gain * inputs_all.reshape(rows * batches, local_feat)), axis=1
     )
-    reduced = lax.psum(jnp.concatenate([gain_part, row_all]), "tensor")
+    reduced = jnp.sum(
+        lax.all_gather(jnp.concatenate([gain_part, row_all]), "tensor", axis=0), axis=0
+    )
     d_gain = reduced[:local_feat]
-    row_all = lax.psum(reduced[local_feat:], "dp").reshape(batches, rows)
+    row_all = jnp.sum(lax.all_gather(reduced[local_feat:], "dp", axis=0), axis=0)
+    row_all = row_all.reshape(batches, rows)
     row_product = lax.dynamic_slice_in_dim(row_all, start, local_rows, axis=1)
     hidden, flat_grad, _ = lax.optimization_barrier((hidden, flat_grad, stacked))
     shares = lax.psum_scatter(stacked, "tensor", scatter_dimension=0, tiled=True).astype(

time: 219 us -> 215 us (0.982)
  blocking collectives: 56.5 us -> 50.8 us
    psum x2 -> x0, blocking collectives: 23.9 us -> none  [the longest x1 12.8 us: per_device(): reduced = lax.psum(jnp.concatenate([gain_part, row_all]), 'tensor')]
    all_gather x0 -> x2, blocking collectives: none -> 18.3 us  [the longest x1 9.16 us: per_device(): lax.all_gather(reduced[local_feat:], 'dp', axis=0)]
  transfers between devices with their start and end apart: 3 -> 3, of which waited for: 2 -> 3; matrix products, arithmetic and copies ran while one was open for 10% -> 10% of each run, Pallas kernels for 0% -> 0%
where the time goes in v14:
time: 215 us
  waiting for transfers between devices  100 us (47%)
  blocking collectives  50.8 us (24%)
  matrix products  34.4 us (16%)
  between operations  14 us (7%)
  Pallas kernels  6.05 us (3%)
  local copies, waits for them, and re-layouts  5.36 us (2%)
  other arithmetic  4.1 us (2%)
    psum x1, waiting for transfers between devices, per_device(): gate_sum, up_sum = lax.psum(parts, 'dp')  79.2 us
    psum x1, waiting for transfers between devices, per_device(): back_first = lax.psum(back_part, 'dp')  18.9 us
    psum x1, blocking collectives, per_device(): square_sum = lax.psum(jnp.sum(inputs_all * inputs_all, axis=2), 'dp')  12.5 us
    all_gather x1, blocking collectives, per_device(): grad_all = lax.all_gather(d_output, 'tensor', axis=1, tiled=True)  10.8 us
    all_gather x1, blocking collectives, per_device(): lax.all_gather(inputs_all, 'tensor', axis=1, tiled=True).astype(jnp.float32)  9.28 us
    all_gather x1, blocking collectives, per_device(): lax.all_gather(reduced[local_feat:], 'dp', axis=0)  9.16 us
    all_gather x1, blocking collectives, per_device(): lax.all_gather(jnp.concatenate([gain_part, row_all]), 'tensor', axis=0)  9.09 us
    dot_general x1, matrix products, per_device(): lax.dot_general(flat_normed, gate_grad, contract_rows, preferred_element_...  6.6 us
  transfers between devices with their start and end apart: 3, of which 3 were waited for; matrix products, arithmetic and copies ran while one was open for 10% of the time, Pallas kernels for 0%

profile of v14, /device:TPU:0, one launch (start us, length us, event | category | flops | bytes accessed | tf_op | source)
XLA Modules:
  0.0 215.1 jit_solution(10015569889450625651)
XLA Ops:
  7.2 0.8 copy.26
  8.0 10.8 %all_gather.18 = bf16[4,32,1024]{2,0,1:T(4,128)(2,1)S(1)} all-gather(bf16[4,4,1024]{2,0,1:T(4,128)(2,1)S(1)} %copy.26), channel_id=1, replica_groups=mesh['dp'=4,'tensor'=8] {'tensor'}, dimensions={1}, use_global_device_ids=true | all-gather | bytes 294912 | tf_op jit(solution)/shard_map/all_gather | solution.py:55
  18.8 0.8 copy.27
  19.6 6.1 %shard_map.126 = bf16[128,3584]{1,0:T(8,128)(2,1)} custom-call(bf16[128,1024]{1,0:T(8,128)(2,1)} %bitcast.69, bf16[3584,1024]{1,0:T(8,128)(2,1)} %weight_ref.1), custom_call_target="tpu_custom_call" | custom-call | flops 939524096 | bytes 8519680 | tf_op jit(solution)/shard_map/pallas_call | solution.py:32
  25.8 9.3 %all_gather.19 = bf16[4,32,1024]{2,0,1:T(4,128)(2,1)S(1)} all-gather(bf16[4,4,1024]{2,0,1:T(4,128)(2,1)S(1)} %copy.28), channel_id=1, replica_groups=mesh['dp'=4,'tensor'=8] {'tensor'}, dimensions={1}, use_global_device_ids=true | all-gather | bytes 294912 | tf_op jit(solution)/shard_map/all_gather | solution.py:62
  35.2 12.5 %psum.28 = f32[4,32]{1,0:T(4,128)S(1)} all-reduce(f32[4,32]{1,0:T(4,128)S(1)} %multiply_reduce_fusion), channel_id=1, replica_groups=mesh['dp'=4,'tensor'=8] {'dp'}, use_global_device_ids=true, to_apply=%region_1.0 | all-reduce | flops 128 | bytes 1024 | tf_op jit(solution)/shard_map/psum | solution.py:63
  47.9 5.3 %convolution_convert_fusion.4 = bf16[128,3584]{1,0:T(8,128)(2,1)} fusion(bf16[128,1024]{1,0:T(8,128)(2,1)S(1)} %bitcast.65, bf16[1024,3584]{1,0:T(8,128)(2,1)} %param.9), kind=kOutput, calls=%fused_computation.4 | convolution fusion | flops 939982848 | bytes 8519680 | tf_op jit(solution)/shard_map/dot_general | solution.py:82
  53.2 2.1 convolution_convert_fusion.3
  55.3 18.9 %all-reduce.4.cloned.1.call-done = bf16[128,3584]{1,0:T(8,128)(2,1)} async-done(((bf16[128,3584]{1,0:T(8,128)(2,1)}), bf16[128,3584]{1,0:T(8,128)(2,1)}) %all-reduce.4.cloned.1.call-update) | async-done | bytes 917520 | tf_op jit(solution)/shard_map/psum | solution.py:60
  74.7 79.2 %all-reduce.6.cloned.1.call-done = (bf16[128,3584]{1,0:T(8,128)(2,1)}, bf16[128,3584]{1,0:T(8,128)(2,1)}) async-done(((bf16[128,3584]{1,0:T(8,128)(2,1)}, bf16[128,3584]{1,0:T(8,128)(2,1)}), (bf16[128,3584]{1,0:T(8,128)(2,1)}, bf16[128,3584]{1,0:T(8,128)(2,1)})) %all-reduce.6.cloned.1.call-update) | async-done | bytes 1835024 | tf_op jit(solution)/shard_map/psum | solution.py:86
  154.0 2.2 %fusion.1 = bf16[128,3584]{1,0:T(8,128)(2,1)S(1)} fusion(bf16[128,3584]{1,0:T(8,128)(2,1)} %get-tuple-element.21, f32[128]{0:T(128)S(1)} %mul.126, bf16[128,3584]{1,0:T(8,128)(2,1)} %get-tuple-element.22), kind=kLoop, calls=%fused_computation.12 | loop fusion | flops 4128768 | bytes 2753024 | tf_op jit(solution)/shard_map/convert_element_type | solution.py:16
  156.2 6.0 %fusion.27 = f32[128,1024]{1,0:T(8,128)S(1)} fusion(bf16[1024,3584]{1,0:T(8,128)(2,1)} %param.9, bf16[128,3584]{1,0:T(8,128)(2,1)S(1)} %copy-done.1, bf16[128,3584]{1,0:T(8,128)(2,1)} %all-reduce.4.cloned.1.call-done, bf16[128,3584]{1,0:T(8,128)(2,1)S(1)} %copy-done.2, f32[128]{0:T(128)S(1)} %mul.126), kind=kOutput, calls=%fused_computation.56 | convolution fusion | flops 945946624 | bytes 10617344 | tf_op jit(solution)/shard_map/dot_general | solution.py:97
  162.3 5.4 %convolution_convert_fusion.1 = bf16[1024,3584]{1,0:T(8,128)(2,1)} fusion(bf16[128,1024]{1,0:T(8,128)(2,1)S(1)} %bitcast.67, bf16[128,3584]{1,0:T(8,128)(2,1)S(1)} %copy-done.7, f32[128]{0:T(128)S(1)} %mul.126, bf16[128,3584]{1,0:T(8,128)(2,1)S(1)} %copy-done.2), kind=kOutput, calls=%fused_computation.1 | convolution fusion | flops 947322880 | bytes 9437696 | tf_op jit(solution)/shard_map/dot_general | solution.py:136
  167.7 1.2 convolution_convert_fusion.5
  169.6 2.6 %fusion.14 = (f32[1024]{0:T(1024)S(1)}, f32[128]{0:T(128)S(1)}, bf16[128,1024]{1,0:T(8,128)(2,1)S(1)}) fusion(f32[4,32,1024]{2,1,0:T(8,128)S(1)} %get-tuple-element.27, f32[4,32,1024]{2,1,0:T(8,128)S(1)} %copy_convert_fusion, f32[1024]{0:T(1024)S(1)} %copy-done.6, f32[128,1024]{1,0:T(8,128)S(1)} %fusion.27, bf16[1024,3584]{1,0:T(8,128)(2,1)S(1)} %bitcast.64, ...), kind=kOutput, calls=%fused_computation.30 | convolution fusion | flops 944569216 | bytes 11019264 | tf_op jit(solution)/shard_map/dot_general | solution.py:99
  172.7 0.9 reshape.50
  173.7 9.1 %all-gather.2 = f32[8,1,1152]{2,1,0:T(1,128)S(1)} all-gather(f32[1,1,1152]{2,1,0:T(1,128)S(1)} %reshape.60), channel_id=2, replica_groups=mesh['dp'=4,'tensor'=8] {'tensor'}, dimensions={0}, use_global_device_ids=true | all-gather | bytes 41472 | tf_op jit(solution)/shard_map/all_gather | solution.py:116
  183.4 5.1 %convolution_convert_fusion = bf16[3584,1024]{1,0:T(8,128)(2,1)} fusion(bf16[128,3584]{1,0:T(8,128)(2,1)S(1)} %fusion.1, bf16[128,1024]{1,0:T(8,128)(2,1)S(1)} %bitcast.70), kind=kOutput, calls=%fused_computation | convolution fusion | flops 943194112 | bytes 8519680 | tf_op jit(solution)/shard_map/dot_general | solution.py:130
  188.6 9.2 %all-gather.3 = f32[4,1,128]{2,1,0:T(1,128)S(1)} all-gather(f32[1,1,128]{2,1,0:T(1,128)S(1)} %slice_bitcast_fusion.2), channel_id=3, replica_groups=mesh['dp'=4,'tensor'=8] {'dp'}, dimensions={0}, use_global_device_ids=true | all-gather | bytes 2560 | tf_op jit(solution)/shard_map/all_gather | solution.py:119
  197.8 0.7 fusion.23
  198.5 6.6 %convolution_convert_fusion.2 = bf16[1024,3584]{1,0:T(8,128)(2,1)} fusion(bf16[128,1024]{1,0:T(8,128)(2,1)S(1)} %bitcast.68, bf16[128,3584]{1,0:T(8,128)(2,1)S(1)} %copy-done.1, bf16[128,3584]{1,0:T(8,128)(2,1)} %all-reduce.4.cloned.1.call-done, bf16[128,3584]{1,0:T(8,128)(2,1)S(1)} %copy-done.3, f32[128]{0:T(128)S(1)} %mul.126), kind=kOutput, calls=%fused_computation.2 | convolution fusion | flops 949616640 | bytes 10355200 | tf_op jit(solution)/shard_map/dot_general | solution.py:133
  205.1 1.8 reduce-scatter.2.cloned.1.call-done
  206.9 0.9 copy.31
  207.8 0.7 fusion.17
  (56 shorter events, 2.8 us)
Async XLA Ops:
  7.2 67.0 %all-reduce.4.cloned.1.call-start = ((), (), s32[]{:S(2)}) async-start(), calls=%async_computation.1 | async-start | bytes 1835008 | tf_op jit(solution)/shard_map/psum | solution.py:60
  19.6 6.1 %copy-start.4 = (bf16[4,4,1024]{2,1,0:T(4,128)(2,1)S(1)}, bf16[4,4,1024]{2,1,0:T(4,128)(2,1)}, u32[]{:S(2)}) copy-start(bf16[4,4,1024]{2,1,0:T(4,128)(2,1)} %param.7) | copy-start | bytes 98308
  19.6 28.1 %copy-start.6 = (f32[1024]{0:T(1024)S(1)}, f32[1024]{0:T(1024)}, u32[]{:S(2)}) copy-start(f32[1024]{0:T(1024)} %param.8) | copy-start | bytes 12292
  25.7 128.3 %all-reduce.6.cloned.1.call-start = ((), (), s32[]{:S(2)}) async-start(), calls=%async_computation.3 | async-start | bytes 3670016 | tf_op jit(solution)/shard_map/psum | solution.py:86
  47.7 5.5 %slice-start.2 = ((s8[7340032]{0:T(1024)(128)(4,1)}), s8[4194304]{0:T(1024)(128)(4,1)S(1)}, s32[]{:S(2)}) async-start(s8[7340032]{0:T(1024)(128)(4,1)} %bitcast.61), calls=%async_computation.6 | async-start | bytes 8388608
  47.8 5.4 %slice-start.3 = ((s8[7340032]{0:T(1024)(128)(4,1)}), s8[3145728]{0:T(1024)(128)(4,1)S(1)}, s32[]{:S(2)}) async-start(s8[7340032]{0:T(1024)(128)(4,1)} %bitcast.61), calls=%async_computation.7 | async-start | bytes 6291456
  55.3 19.2 %copy-start.8 = (s32[4]{0:T(128)S(1)}, s32[4]{0:T(128)}, u32[]{:S(2)}) copy-start(s32[4]{0:T(128)} %param.13) | copy-start | bytes 52
  74.2 132.7 %reduce-scatter.2.cloned.1.call-start = ((), (), s32[]{:S(2)}) async-start(), calls=%async_computation.2 | async-start | bytes 589824 | tf_op jit(solution)/shard_map/reduce_scatter | solution.py:123
  154.0 2.3 %copy-start.1 = (bf16[128,3584]{1,0:T(8,128)(2,1)S(1)}, bf16[128,3584]{1,0:T(8,128)(2,1)}, u32[]{:S(2)}) copy-start(bf16[128,3584]{1,0:T(8,128)(2,1)} %get-tuple-element.21) | copy-start | bytes 2752516
  154.0 2.3 %copy-start.2 = (bf16[128,3584]{1,0:T(8,128)(2,1)S(1)}, bf16[128,3584]{1,0:T(8,128)(2,1)}, u32[]{:S(2)}) copy-start(bf16[128,3584]{1,0:T(8,128)(2,1)} %get-tuple-element.22) | copy-start | bytes 2752516
  154.0 13.7 %slice-start = ((s8[7340032]{0:T(1024)(128)(4,1)}), s8[4194304]{0:T(1024)(128)(4,1)S(1)}, s32[]{:S(2)}) async-start(s8[7340032]{0:T(1024)(128)(4,1)} %bitcast.59), calls=%async_computation.4 | async-start | bytes 8388608
  156.2 6.1 %copy-start.7 = (bf16[128,3584]{1,0:T(8,128)(2,1)S(1)}, bf16[128,3584]{1,0:T(8,128)(2,1)}, u32[]{:S(2)}) copy-start(bf16[128,3584]{1,0:T(8,128)(2,1)} %all-reduce.4.cloned.1.call-done) | copy-start | bytes 2752516
  156.2 11.5 %slice-start.1 = ((s8[7340032]{0:T(1024)(128)(4,1)}), s8[3145728]{0:T(1024)(128)(4,1)S(1)}, s32[]{:S(2)}) async-start(s8[7340032]{0:T(1024)(128)(4,1)} %bitcast.59), calls=%async_computation.5 | async-start | bytes 6291456
  162.3 6.7 %slice-start.4 = ((s8[7340032]{0:T(1024)(128)(4,1)}), s8[4194304]{0:T(1024)(128)(4,1)S(1)}, s32[]{:S(2)}) async-start(s8[7340032]{0:T(1024)(128)(4,1)} %bitcast.63), calls=%async_computation.8 | async-start | bytes 8388608
  167.7 1.9 slice-start.5
  172.2 11.2 %copy-start = (bf16[4,32,1024]{2,1,0:T(8,128)(2,1)S(1)}, bf16[4,32,1024]{2,1,0:T(8,128)(2,1)}, u32[]{:S(2)}) copy-start(bf16[4,32,1024]{2,1,0:T(8,128)(2,1)} %copy.27) | copy-start | bytes 786436
  183.4 15.1 %copy-start.3 = (bf16[128,3584]{1,0:T(8,128)(2,1)S(1)}, bf16[128,3584]{1,0:T(8,128)(2,1)}, u32[]{:S(2)}) copy-start(bf16[128,3584]{1,0:T(8,128)(2,1)} %get-tuple-element.22) | copy-start | bytes 2752516
  198.5 9.3 %copy-start.5 = (bf16[4,4,1024]{2,1,0:T(4,128)(2,1)S(1)}, bf16[4,4,1024]{2,1,0:T(4,128)(2,1)}, u32[]{:S(2)}) copy-start(bf16[4,4,1024]{2,1,0:T(4,128)(2,1)} %param.12) | copy-start | bytes 98308
Sparse Core Ops, SparseCore 0:
  25.8 48.3 all-reduce.3
  77.2 76.7 all-reduce.5
  173.8 33.1 reduce-scatter.1

commit v15 on v14

--- a/solution.py
+++ b/solution.py
@@ -60,7 +60,9 @@
     back_first = lax.psum(back_part, "dp")
     inputs_all, _ = lax.optimization_barrier((inputs, back_part))
     inputs_all = lax.all_gather(inputs_all, "tensor", axis=1, tiled=True).astype(jnp.float32)
-    square_sum = lax.psum(jnp.sum(inputs_all * inputs_all, axis=2), "dp")
+    square_sum = jnp.sum(
+        lax.all_gather(jnp.sum(inputs_all * inputs_all, axis=2), "dp", axis=0), axis=0
+    )
     row_scale_all = lax.rsqrt(square_sum / full_width + epsilon)
     normed_all = (inputs_all * row_scale_all[:, :, None] * norm_gain).astype(jnp.bfloat16)
     row_scale = lax.dynamic_slice_in_dim(row_scale_all, start, local_rows, axis=1)

time: 215 us -> 215 us (level)
    all_gather x0 -> x1, blocking collectives: none -> 12.5 us  [per_device(): lax.all_gather(jnp.sum(inputs_all * inputs_all, axis=2), 'dp', axis=0)]
    psum x1 -> x0, blocking collectives: 12.5 us -> none  [per_device(): square_sum = lax.psum(jnp.sum(inputs_all * inputs_all, axis=2), 'dp')]
where the time goes in v15:
time: 215 us
  waiting for transfers between devices  99.8 us (46%)
  blocking collectives  50.9 us (24%)
  matrix products  34.4 us (16%)
  between operations  14 us (7%)
  Pallas kernels  6.05 us (3%)
  local copies, waits for them, and re-layouts  5.36 us (2%)
  other arithmetic  4.11 us (2%)
    psum x1, waiting for transfers between devices, per_device(): gate_sum, up_sum = lax.psum(parts, 'dp')  79.2 us
    psum x1, waiting for transfers between devices, per_device(): back_first = lax.psum(back_part, 'dp')  18.7 us
    all_gather x1, blocking collectives, per_device(): lax.all_gather(jnp.sum(inputs_all * inputs_all, axis=2), 'dp', axis=0)  12.5 us
    all_gather x1, blocking collectives, per_device(): grad_all = lax.all_gather(d_output, 'tensor', axis=1, tiled=True)  10.8 us
    all_gather x1, blocking collectives, per_device(): lax.all_gather(inputs_all, 'tensor', axis=1, tiled=True).astype(jnp.float32)  9.28 us
    all_gather x1, blocking collectives, per_device(): lax.all_gather(reduced[local_feat:], 'dp', axis=0)  9.16 us
    all_gather x1, blocking collectives, per_device(): lax.all_gather(jnp.concatenate([gain_part, row_all]), 'tensor', axis=0)  9.11 us
    dot_general x1, matrix products, per_device(): lax.dot_general(flat_normed, gate_grad, contract_rows, preferred_element_...  6.6 us
  transfers between devices with their start and end apart: 3, of which 3 were waited for; matrix products, arithmetic and copies ran while one was open for 10% of the time, Pallas kernels for 0%

profile of v15, /device:TPU:0, one launch (start us, length us, event | category | flops | bytes accessed | tf_op | source)
XLA Modules:
  0.0 214.9 jit_solution(8759722348690637792)
XLA Ops:
  7.2 0.8 copy.26
  8.0 10.8 %all_gather.24 = bf16[4,32,1024]{2,0,1:T(4,128)(2,1)S(1)} all-gather(bf16[4,4,1024]{2,0,1:T(4,128)(2,1)S(1)} %copy.26), channel_id=1, replica_groups=mesh['dp'=4,'tensor'=8] {'tensor'}, dimensions={1}, use_global_device_ids=true | all-gather | bytes 294912 | tf_op jit(solution)/shard_map/all_gather | solution.py:55
  18.8 0.8 copy.27
  19.6 6.1 %shard_map.126 = bf16[128,3584]{1,0:T(8,128)(2,1)} custom-call(bf16[128,1024]{1,0:T(8,128)(2,1)} %bitcast.70, bf16[3584,1024]{1,0:T(8,128)(2,1)} %weight_ref.1), custom_call_target="tpu_custom_call" | custom-call | flops 939524096 | bytes 8519680 | tf_op jit(solution)/shard_map/pallas_call | solution.py:32
  25.8 9.3 %all_gather.25 = bf16[4,32,1024]{2,0,1:T(4,128)(2,1)S(1)} all-gather(bf16[4,4,1024]{2,0,1:T(4,128)(2,1)S(1)} %copy.28), channel_id=1, replica_groups=mesh['dp'=4,'tensor'=8] {'tensor'}, dimensions={1}, use_global_device_ids=true | all-gather | bytes 294912 | tf_op jit(solution)/shard_map/all_gather | solution.py:62
  35.2 12.5 %all-gather.3 = f32[4,4,32]{2,1,0:T(4,128)S(1)} all-gather(f32[1,4,32]{2,1,0:T(4,128)S(1)} %bitcast.75), channel_id=2, replica_groups=mesh['dp'=4,'tensor'=8] {'dp'}, dimensions={0}, use_global_device_ids=true | all-gather | bytes 2560 | tf_op jit(solution)/shard_map/all_gather | solution.py:64
  47.9 5.3 %convolution_convert_fusion.4 = bf16[128,3584]{1,0:T(8,128)(2,1)} fusion(bf16[128,1024]{1,0:T(8,128)(2,1)S(1)} %bitcast.66, bf16[1024,3584]{1,0:T(8,128)(2,1)} %param.9), kind=kOutput, calls=%fused_computation.4 | convolution fusion | flops 939982848 | bytes 8519680 | tf_op jit(solution)/shard_map/dot_general | solution.py:84
  53.3 2.1 convolution_convert_fusion.3
  55.3 18.7 %all-reduce.4.cloned.1.call-done = bf16[128,3584]{1,0:T(8,128)(2,1)} async-done(((bf16[128,3584]{1,0:T(8,128)(2,1)}), bf16[128,3584]{1,0:T(8,128)(2,1)}) %all-reduce.4.cloned.1.call-update) | async-done | bytes 917520 | tf_op jit(solution)/shard_map/psum | solution.py:60
  74.6 79.2 %all-reduce.6.cloned.1.call-done = (bf16[128,3584]{1,0:T(8,128)(2,1)}, bf16[128,3584]{1,0:T(8,128)(2,1)}) async-done(((bf16[128,3584]{1,0:T(8,128)(2,1)}, bf16[128,3584]{1,0:T(8,128)(2,1)}), (bf16[128,3584]{1,0:T(8,128)(2,1)}, bf16[128,3584]{1,0:T(8,128)(2,1)})) %all-reduce.6.cloned.1.call-update) | async-done | bytes 1835024 | tf_op jit(solution)/shard_map/psum | solution.py:88
  153.8 2.2 %fusion.1 = bf16[128,3584]{1,0:T(8,128)(2,1)S(1)} fusion(bf16[128,3584]{1,0:T(8,128)(2,1)} %get-tuple-element.21, f32[128]{0:T(128)S(1)} %mul.126, bf16[128,3584]{1,0:T(8,128)(2,1)} %get-tuple-element.22), kind=kLoop, calls=%fused_computation.12 | loop fusion | flops 4128768 | bytes 2753024 | tf_op jit(solution)/shard_map/convert_element_type | solution.py:16
  156.1 6.0 %fusion.27 = f32[128,1024]{1,0:T(8,128)S(1)} fusion(bf16[1024,3584]{1,0:T(8,128)(2,1)} %param.9, bf16[128,3584]{1,0:T(8,128)(2,1)S(1)} %copy-done.1, bf16[128,3584]{1,0:T(8,128)(2,1)} %all-reduce.4.cloned.1.call-done, bf16[128,3584]{1,0:T(8,128)(2,1)S(1)} %copy-done.2, f32[128]{0:T(128)S(1)} %mul.126), kind=kOutput, calls=%fused_computation.56 | convolution fusion | flops 945946624 | bytes 10617344 | tf_op jit(solution)/shard_map/dot_general | solution.py:99
  162.2 5.4 %convolution_convert_fusion.1 = bf16[1024,3584]{1,0:T(8,128)(2,1)} fusion(bf16[128,1024]{1,0:T(8,128)(2,1)S(1)} %bitcast.68, bf16[128,3584]{1,0:T(8,128)(2,1)S(1)} %copy-done.7, f32[128]{0:T(128)S(1)} %mul.126, bf16[128,3584]{1,0:T(8,128)(2,1)S(1)} %copy-done.2), kind=kOutput, calls=%fused_computation.1 | convolution fusion | flops 947322880 | bytes 9437696 | tf_op jit(solution)/shard_map/dot_general | solution.py:138
  167.6 1.2 convolution_convert_fusion.5
  169.5 2.6 %fusion.14 = (f32[1024]{0:T(1024)S(1)}, f32[128]{0:T(128)S(1)}, bf16[128,1024]{1,0:T(8,128)(2,1)S(1)}) fusion(f32[4,32,1024]{2,1,0:T(8,128)S(1)} %get-tuple-element.27, f32[4,32,1024]{2,1,0:T(8,128)S(1)} %copy_convert_fusion, f32[1024]{0:T(1024)S(1)} %copy-done.6, f32[128,1024]{1,0:T(8,128)S(1)} %fusion.27, bf16[1024,3584]{1,0:T(8,128)(2,1)S(1)} %bitcast.65, ...), kind=kOutput, calls=%fused_computation.30 | convolution fusion | flops 944569216 | bytes 11019264 | tf_op jit(solution)/shard_map/dot_general | solution.py:101
  172.6 0.9 reshape.54
  173.5 9.1 %all-gather.4 = f32[8,1,1152]{2,1,0:T(1,128)S(1)} all-gather(f32[1,1,1152]{2,1,0:T(1,128)S(1)} %reshape.67), channel_id=3, replica_groups=mesh['dp'=4,'tensor'=8] {'tensor'}, dimensions={0}, use_global_device_ids=true | all-gather | bytes 41472 | tf_op jit(solution)/shard_map/all_gather | solution.py:118
  183.3 5.1 %convolution_convert_fusion = bf16[3584,1024]{1,0:T(8,128)(2,1)} fusion(bf16[128,3584]{1,0:T(8,128)(2,1)S(1)} %fusion.1, bf16[128,1024]{1,0:T(8,128)(2,1)S(1)} %bitcast.71), kind=kOutput, calls=%fused_computation | convolution fusion | flops 943194112 | bytes 8519680 | tf_op jit(solution)/shard_map/dot_general | solution.py:132
  188.4 9.2 %all-gather.5 = f32[4,1,128]{2,1,0:T(1,128)S(1)} all-gather(f32[1,1,128]{2,1,0:T(1,128)S(1)} %slice_bitcast_fusion.2), channel_id=4, replica_groups=mesh['dp'=4,'tensor'=8] {'dp'}, dimensions={0}, use_global_device_ids=true | all-gather | bytes 2560 | tf_op jit(solution)/shard_map/all_gather | solution.py:121
  197.7 0.7 fusion.23
  198.4 6.6 %convolution_convert_fusion.2 = bf16[1024,3584]{1,0:T(8,128)(2,1)} fusion(bf16[128,1024]{1,0:T(8,128)(2,1)S(1)} %bitcast.69, bf16[128,3584]{1,0:T(8,128)(2,1)S(1)} %copy-done.1, bf16[128,3584]{1,0:T(8,128)(2,1)} %all-reduce.4.cloned.1.call-done, bf16[128,3584]{1,0:T(8,128)(2,1)S(1)} %copy-done.3, f32[128]{0:T(128)S(1)} %mul.126), kind=kOutput, calls=%fused_computation.2 | convolution fusion | flops 949616640 | bytes 10355200 | tf_op jit(solution)/shard_map/dot_general | solution.py:135
  205.0 1.8 reduce-scatter.2.cloned.1.call-done
  206.8 0.9 copy.31
  207.7 0.7 fusion.17
  (57 shorter events, 2.8 us)
Async XLA Ops:
  7.2 66.9 %all-reduce.4.cloned.1.call-start = ((), (), s32[]{:S(2)}) async-start(), calls=%async_computation.1 | async-start | bytes 1835008 | tf_op jit(solution)/shard_map/psum | solution.py:60
  19.6 6.1 %copy-start.4 = (bf16[4,4,1024]{2,1,0:T(4,128)(2,1)S(1)}, bf16[4,4,1024]{2,1,0:T(4,128)(2,1)}, u32[]{:S(2)}) copy-start(bf16[4,4,1024]{2,1,0:T(4,128)(2,1)} %param.7) | copy-start | bytes 98308
  19.6 28.2 %copy-start.6 = (f32[1024]{0:T(1024)S(1)}, f32[1024]{0:T(1024)}, u32[]{:S(2)}) copy-start(f32[1024]{0:T(1024)} %param.8) | copy-start | bytes 12292
  25.7 128.1 %all-reduce.6.cloned.1.call-start = ((), (), s32[]{:S(2)}) async-start(), calls=%async_computation.3 | async-start | bytes 3670016 | tf_op jit(solution)/shard_map/psum | solution.py:88
  47.8 5.5 %slice-start.2 = ((s8[7340032]{0:T(1024)(128)(4,1)}), s8[4194304]{0:T(1024)(128)(4,1)S(1)}, s32[]{:S(2)}) async-start(s8[7340032]{0:T(1024)(128)(4,1)} %bitcast.62), calls=%async_computation.6 | async-start | bytes 8388608
  47.9 5.4 %slice-start.3 = ((s8[7340032]{0:T(1024)(128)(4,1)}), s8[3145728]{0:T(1024)(128)(4,1)S(1)}, s32[]{:S(2)}) async-start(s8[7340032]{0:T(1024)(128)(4,1)} %bitcast.62), calls=%async_computation.7 | async-start | bytes 6291456
  55.3 19.0 %copy-start.8 = (s32[4]{0:T(128)S(1)}, s32[4]{0:T(128)}, u32[]{:S(2)}) copy-start(s32[4]{0:T(128)} %param.13) | copy-start | bytes 52
  74.1 132.7 %reduce-scatter.2.cloned.1.call-start = ((), (), s32[]{:S(2)}) async-start(), calls=%async_computation.2 | async-start | bytes 589824 | tf_op jit(solution)/shard_map/reduce_scatter | solution.py:125
  153.8 2.3 %copy-start.1 = (bf16[128,3584]{1,0:T(8,128)(2,1)S(1)}, bf16[128,3584]{1,0:T(8,128)(2,1)}, u32[]{:S(2)}) copy-start(bf16[128,3584]{1,0:T(8,128)(2,1)} %get-tuple-element.21) | copy-start | bytes 2752516
  153.8 2.3 %copy-start.2 = (bf16[128,3584]{1,0:T(8,128)(2,1)S(1)}, bf16[128,3584]{1,0:T(8,128)(2,1)}, u32[]{:S(2)}) copy-start(bf16[128,3584]{1,0:T(8,128)(2,1)} %get-tuple-element.22) | copy-start | bytes 2752516
  153.8 13.7 %slice-start = ((s8[7340032]{0:T(1024)(128)(4,1)}), s8[4194304]{0:T(1024)(128)(4,1)S(1)}, s32[]{:S(2)}) async-start(s8[7340032]{0:T(1024)(128)(4,1)} %bitcast.60), calls=%async_computation.4 | async-start | bytes 8388608
  156.1 6.1 %copy-start.7 = (bf16[128,3584]{1,0:T(8,128)(2,1)S(1)}, bf16[128,3584]{1,0:T(8,128)(2,1)}, u32[]{:S(2)}) copy-start(bf16[128,3584]{1,0:T(8,128)(2,1)} %all-reduce.4.cloned.1.call-done) | copy-start | bytes 2752516
  156.1 11.5 %slice-start.1 = ((s8[7340032]{0:T(1024)(128)(4,1)}), s8[3145728]{0:T(1024)(128)(4,1)S(1)}, s32[]{:S(2)}) async-start(s8[7340032]{0:T(1024)(128)(4,1)} %bitcast.60), calls=%async_computation.5 | async-start | bytes 6291456
  162.2 6.7 %slice-start.4 = ((s8[7340032]{0:T(1024)(128)(4,1)}), s8[4194304]{0:T(1024)(128)(4,1)S(1)}, s32[]{:S(2)}) async-start(s8[7340032]{0:T(1024)(128)(4,1)} %bitcast.64), calls=%async_computation.8 | async-start | bytes 8388608
  167.6 1.9 slice-start.5
  172.1 11.2 %copy-start = (bf16[4,32,1024]{2,1,0:T(8,128)(2,1)S(1)}, bf16[4,32,1024]{2,1,0:T(8,128)(2,1)}, u32[]{:S(2)}) copy-start(bf16[4,32,1024]{2,1,0:T(8,128)(2,1)} %copy.27) | copy-start | bytes 786436
  183.3 15.1 %copy-start.3 = (bf16[128,3584]{1,0:T(8,128)(2,1)S(1)}, bf16[128,3584]{1,0:T(8,128)(2,1)}, u32[]{:S(2)}) copy-start(bf16[128,3584]{1,0:T(8,128)(2,1)} %get-tuple-element.22) | copy-start | bytes 2752516
  198.4 9.3 %copy-start.5 = (bf16[4,4,1024]{2,1,0:T(4,128)(2,1)S(1)}, bf16[4,4,1024]{2,1,0:T(4,128)(2,1)}, u32[]{:S(2)}) copy-start(bf16[4,4,1024]{2,1,0:T(4,128)(2,1)} %param.12) | copy-start | bytes 98308
Sparse Core Ops, SparseCore 0:
  25.8 48.2 all-reduce.3
  77.0 76.7 all-reduce.5
  173.6 33.1 reduce-scatter.1

commit v16 on v15

--- a/solution.py
+++ b/solution.py
@@ -114,12 +114,12 @@
     row_all = jnp.sum(
         normed_part * (norm_gain * inputs_all.reshape(rows * batches, local_feat)), axis=1
     )
-    reduced = jnp.sum(
-        lax.all_gather(jnp.concatenate([gain_part, row_all]), "tensor", axis=0), axis=0
-    )
-    d_gain = reduced[:local_feat]
-    row_all = jnp.sum(lax.all_gather(reduced[local_feat:], "dp", axis=0), axis=0)
-    row_all = row_all.reshape(batches, rows)
+    gathered = lax.all_gather(
+        jnp.concatenate([gain_part, row_all]), ("dp", "tensor"), axis=0
+    ).reshape(lax.axis_size("dp"), groups, -1)
+    own = lax.dynamic_index_in_dim(gathered, lax.axis_index("dp"), 0, keepdims=False)
+    d_gain = jnp.sum(own[:, :local_feat], axis=0)
+    row_all = jnp.sum(gathered[:, :, local_feat:], axis=(0, 1)).reshape(batches, rows)
     row_product = lax.dynamic_slice_in_dim(row_all, start, local_rows, axis=1)
     hidden, flat_grad, _ = lax.optimization_barrier((hidden, flat_grad, stacked))
     shares = lax.psum_scatter(stacked, "tensor", scatter_dimension=0, tiled=True).astype(

time: 215 us -> 235 us (1.093)
  blocking collectives: 50.9 us -> 72.8 us
    all_gather x2 -> x1, blocking collectives: 18.3 us -> 40.2 us  [per_device(): lax.all_gather(jnp.concatenate([gain_part, row_all]), ('dp', 'tensor'), a...]
  transfers between devices with their start and end apart: 3 -> 3, of which waited for: 3 -> 2; matrix products, arithmetic and copies ran while one was open for 10% -> 9% of each run, Pallas kernels for 0% -> 0%
where the time goes in v16:
time: 235 us
  waiting for transfers between devices  98 us (42%)
  blocking collectives  72.8 us (31%)
  matrix products  34.4 us (15%)
  between operations  14 us (6%)
  Pallas kernels  6.05 us (3%)
  local copies, waits for them, and re-layouts  4.8 us (2%)
  other arithmetic  4.68 us (2%)
    psum x1, waiting for transfers between devices, per_device(): gate_sum, up_sum = lax.psum(parts, 'dp')  79.2 us
    all_gather x1, blocking collectives, per_device(): lax.all_gather(jnp.concatenate([gain_part, row_all]), ('dp', 'tensor'), a...  40.2 us
    psum x1, waiting for transfers between devices, per_device(): back_first = lax.psum(back_part, 'dp')  18.7 us
    all_gather x1, blocking collectives, per_device(): lax.all_gather(jnp.sum(inputs_all * inputs_all, axis=2), 'dp', axis=0)  12.5 us
    all_gather x1, blocking collectives, per_device(): grad_all = lax.all_gather(d_output, 'tensor', axis=1, tiled=True)  10.8 us
    all_gather x1, blocking collectives, per_device(): lax.all_gather(inputs_all, 'tensor', axis=1, tiled=True).astype(jnp.float32)  9.28 us
    dot_general x1, matrix products, per_device(): lax.dot_general(flat_normed, gate_grad, contract_rows, preferred_element_...  6.6 us
    pallas_call x1, Pallas kernels, back_project(): pl.pallas_call(back_kernel, grid=(n // tile,), in_specs=[pl.BlockSpec((m,...  6.05 us
  transfers between devices with their start and end apart: 3, of which 2 were waited for; matrix products, arithmetic and copies ran while one was open for 9% of the time, Pallas kernels for 0%

profile of v16, /device:TPU:0, one launch (start us, length us, event | category | flops | bytes accessed | tf_op | source)
XLA Modules:
  0.0 235.1 jit_solution(763100153104466454)
XLA Ops:
  7.2 0.8 copy.26
  8.0 10.8 %all_gather.18 = bf16[4,32,1024]{2,0,1:T(4,128)(2,1)S(1)} all-gather(bf16[4,4,1024]{2,0,1:T(4,128)(2,1)S(1)} %copy.26), channel_id=1, replica_groups=mesh['dp'=4,'tensor'=8] {'tensor'}, dimensions={1}, use_global_device_ids=true | all-gather | bytes 294912 | tf_op jit(solution)/shard_map/all_gather | solution.py:55
  18.8 0.8 copy.27
  19.6 6.1 %shard_map.126 = bf16[128,3584]{1,0:T(8,128)(2,1)} custom-call(bf16[128,1024]{1,0:T(8,128)(2,1)} %bitcast.73, bf16[3584,1024]{1,0:T(8,128)(2,1)} %weight_ref.1), custom_call_target="tpu_custom_call" | custom-call | flops 939524096 | bytes 8519680 | tf_op jit(solution)/shard_map/pallas_call | solution.py:32
  25.8 9.3 %all_gather.19 = bf16[4,32,1024]{2,0,1:T(4,128)(2,1)S(1)} all-gather(bf16[4,4,1024]{2,0,1:T(4,128)(2,1)S(1)} %copy.28), channel_id=1, replica_groups=mesh['dp'=4,'tensor'=8] {'tensor'}, dimensions={1}, use_global_device_ids=true | all-gather | bytes 294912 | tf_op jit(solution)/shard_map/all_gather | solution.py:62
  35.2 12.5 %all-gather.2 = f32[4,4,32]{2,1,0:T(4,128)S(1)} all-gather(f32[1,4,32]{2,1,0:T(4,128)S(1)} %bitcast.80), channel_id=2, replica_groups=mesh['dp'=4,'tensor'=8] {'dp'}, dimensions={0}, use_global_device_ids=true | all-gather | bytes 2560 | tf_op jit(solution)/shard_map/all_gather | solution.py:64
  47.9 5.3 %convolution_convert_fusion.4 = bf16[128,3584]{1,0:T(8,128)(2,1)} fusion(bf16[128,1024]{1,0:T(8,128)(2,1)S(1)} %bitcast.69, bf16[1024,3584]{1,0:T(8,128)(2,1)} %param.9), kind=kOutput, calls=%fused_computation.4 | convolution fusion | flops 939982848 | bytes 8519680 | tf_op jit(solution)/shard_map/dot_general | solution.py:84
  53.3 2.1 convolution_convert_fusion.3
  55.3 18.7 %all-reduce.4.cloned.1.call-done = bf16[128,3584]{1,0:T(8,128)(2,1)} async-done(((bf16[128,3584]{1,0:T(8,128)(2,1)}), bf16[128,3584]{1,0:T(8,128)(2,1)}) %all-reduce.4.cloned.1.call-update) | async-done | bytes 917520 | tf_op jit(solution)/shard_map/psum | solution.py:60
  74.6 79.2 %all-reduce.6.cloned.1.call-done = (bf16[128,3584]{1,0:T(8,128)(2,1)}, bf16[128,3584]{1,0:T(8,128)(2,1)}) async-done(((bf16[128,3584]{1,0:T(8,128)(2,1)}, bf16[128,3584]{1,0:T(8,128)(2,1)}), (bf16[128,3584]{1,0:T(8,128)(2,1)}, bf16[128,3584]{1,0:T(8,128)(2,1)})) %all-reduce.6.cloned.1.call-update) | async-done | bytes 1835024 | tf_op jit(solution)/shard_map/psum | solution.py:88
  153.8 2.2 fusion.1
  156.1 6.0 %fusion.27 = f32[128,1024]{1,0:T(8,128)S(1)} fusion(bf16[1024,3584]{1,0:T(8,128)(2,1)} %param.9, bf16[128,3584]{1,0:T(8,128)(2,1)S(1)} %copy-done.1, bf16[128,3584]{1,0:T(8,128)(2,1)} %all-reduce.4.cloned.1.call-done, bf16[128,3584]{1,0:T(8,128)(2,1)S(1)} %copy-done.2, f32[128]{0:T(128)S(1)} %mul.126), kind=kOutput, calls=%fused_computation.59 | convolution fusion | flops 945946624 | bytes 10617344 | tf_op jit(solution)/shard_map/dot_general | solution.py:99
  162.2 5.4 %convolution_convert_fusion.1 = bf16[1024,3584]{1,0:T(8,128)(2,1)} fusion(bf16[128,1024]{1,0:T(8,128)(2,1)S(1)} %bitcast.71, bf16[128,3584]{1,0:T(8,128)(2,1)S(1)} %copy-done.7, f32[128]{0:T(128)S(1)} %mul.126, bf16[128,3584]{1,0:T(8,128)(2,1)S(1)} %copy-done.2), kind=kOutput, calls=%fused_computation.1 | convolution fusion | flops 947322880 | bytes 9437696 | tf_op jit(solution)/shard_map/dot_general | solution.py:138
  167.6 1.2 convolution_convert_fusion.5
  168.8 0.6 slice-done.5
  169.4 2.6 %fusion.14 = (f32[1024]{0:T(1024)S(1)}, f32[128]{0:T(128)S(1)}, bf16[128,1024]{1,0:T(8,128)(2,1)S(1)}) fusion(f32[4,32,1024]{2,1,0:T(8,128)S(1)} %get-tuple-element.27, f32[4,32,1024]{2,1,0:T(8,128)S(1)} %copy_convert_fusion, f32[1024]{0:T(1024)S(1)} %copy-done.6, f32[128,1024]{1,0:T(8,128)S(1)} %fusion.27, bf16[1024,3584]{1,0:T(8,128)(2,1)S(1)} %bitcast.68, ...), kind=kOutput, calls=%fused_computation.30 | convolution fusion | flops 944569216 | bytes 11019264 | tf_op jit(solution)/shard_map/dot_general | solution.py:101
  172.6 0.9 reshape.57
  173.5 40.2 %all-gather.3 = f32[32,1,1152]{2,1,0:T(1,128)S(1)} all-gather(f32[1,1,1152]{2,1,0:T(1,128)S(1)} %reshape.71), channel_id=3, replica_groups=mesh['dp'=4,'tensor'=8] {'dp','tensor'}, dimensions={0}, use_global_device_ids=true | all-gather | bytes 152064 | tf_op jit(solution)/shard_map/all_gather | solution.py:117
  213.8 5.1 %convolution_convert_fusion = bf16[3584,1024]{1,0:T(8,128)(2,1)} fusion(bf16[128,3584]{1,0:T(8,128)(2,1)S(1)} %fusion.1, bf16[128,1024]{1,0:T(8,128)(2,1)S(1)} %bitcast.74), kind=kOutput, calls=%fused_computation | convolution fusion | flops 943194112 | bytes 8519680 | tf_op jit(solution)/shard_map/dot_general | solution.py:132
  219.1 0.7 fusion.23
  219.7 0.6 slice_reduce_fusion
  220.3 6.6 %convolution_convert_fusion.2 = bf16[1024,3584]{1,0:T(8,128)(2,1)} fusion(bf16[128,1024]{1,0:T(8,128)(2,1)S(1)} %bitcast.72, bf16[128,3584]{1,0:T(8,128)(2,1)S(1)} %copy-done.1, bf16[128,3584]{1,0:T(8,128)(2,1)} %all-reduce.4.cloned.1.call-done, bf16[128,3584]{1,0:T(8,128)(2,1)S(1)} %copy-done.3, f32[128]{0:T(128)S(1)} %mul.126), kind=kOutput, calls=%fused_computation.2 | convolution fusion | flops 949616640 | bytes 10355200 | tf_op jit(solution)/shard_map/dot_general | solution.py:135
  226.9 0.9 copy.31
  227.8 0.7 fusion.17
  (56 shorter events, 1.6 us)
Async XLA Ops:
  7.2 66.9 %all-reduce.4.cloned.1.call-start = ((), (), s32[]{:S(2)}) async-start(), calls=%async_computation.1 | async-start | bytes 1835008 | tf_op jit(solution)/shard_map/psum | solution.py:60
  19.6 6.1 %copy-start.4 = (bf16[4,4,1024]{2,1,0:T(4,128)(2,1)S(1)}, bf16[4,4,1024]{2,1,0:T(4,128)(2,1)}, u32[]{:S(2)}) copy-start(bf16[4,4,1024]{2,1,0:T(4,128)(2,1)} %param.7) | copy-start | bytes 98308
  19.6 28.2 %copy-start.6 = (f32[1024]{0:T(1024)S(1)}, f32[1024]{0:T(1024)}, u32[]{:S(2)}) copy-start(f32[1024]{0:T(1024)} %param.8) | copy-start | bytes 12292
  25.7 128.1 %all-reduce.6.cloned.1.call-start = ((), (), s32[]{:S(2)}) async-start(), calls=%async_computation.3 | async-start | bytes 3670016 | tf_op jit(solution)/shard_map/psum | solution.py:88
  47.8 5.5 %slice-start.2 = ((s8[7340032]{0:T(1024)(128)(4,1)}), s8[4194304]{0:T(1024)(128)(4,1)S(1)}, s32[]{:S(2)}) async-start(s8[7340032]{0:T(1024)(128)(4,1)} %bitcast.65), calls=%async_computation.6 | async-start | bytes 8388608
  47.9 5.4 %slice-start.3 = ((s8[7340032]{0:T(1024)(128)(4,1)}), s8[3145728]{0:T(1024)(128)(4,1)S(1)}, s32[]{:S(2)}) async-start(s8[7340032]{0:T(1024)(128)(4,1)} %bitcast.65), calls=%async_computation.7 | async-start | bytes 6291456
  55.3 19.0 %copy-start.8 = (s32[4]{0:T(128)S(1)}, s32[4]{0:T(128)}, u32[]{:S(2)}) copy-start(s32[4]{0:T(128)} %param.13) | copy-start | bytes 52
  74.1 152.8 %reduce-scatter.2.cloned.1.call-start = ((), (), s32[]{:S(2)}) async-start(), calls=%async_computation.2 | async-start | bytes 589824 | tf_op jit(solution)/shard_map/reduce_scatter | solution.py:125
  153.8 2.3 copy-start.1
  153.8 2.3 copy-start.2
  153.8 13.7 %slice-start = ((s8[7340032]{0:T(1024)(128)(4,1)}), s8[4194304]{0:T(1024)(128)(4,1)S(1)}, s32[]{:S(2)}) async-start(s8[7340032]{0:T(1024)(128)(4,1)} %bitcast.63), calls=%async_computation.4 | async-start | bytes 8388608
  156.1 6.1 %copy-start.7 = (bf16[128,3584]{1,0:T(8,128)(2,1)S(1)}, bf16[128,3584]{1,0:T(8,128)(2,1)}, u32[]{:S(2)}) copy-start(bf16[128,3584]{1,0:T(8,128)(2,1)} %all-reduce.4.cloned.1.call-done) | copy-start | bytes 2752516
  156.1 11.5 %slice-start.1 = ((s8[7340032]{0:T(1024)(128)(4,1)}), s8[3145728]{0:T(1024)(128)(4,1)S(1)}, s32[]{:S(2)}) async-start(s8[7340032]{0:T(1024)(128)(4,1)} %bitcast.63), calls=%async_computation.5 | async-start | bytes 6291456
  162.2 6.7 %slice-start.4 = ((s8[7340032]{0:T(1024)(128)(4,1)}), s8[4194304]{0:T(1024)(128)(4,1)S(1)}, s32[]{:S(2)}) async-start(s8[7340032]{0:T(1024)(128)(4,1)} %bitcast.67), calls=%async_computation.8 | async-start | bytes 8388608
  167.6 1.9 slice-start.5
  172.1 41.7 %copy-start = (bf16[4,32,1024]{2,1,0:T(8,128)(2,1)S(1)}, bf16[4,32,1024]{2,1,0:T(8,128)(2,1)}, u32[]{:S(2)}) copy-start(bf16[4,32,1024]{2,1,0:T(8,128)(2,1)} %copy.27) | copy-start | bytes 786436
  213.8 6.5 %copy-start.3 = (bf16[128,3584]{1,0:T(8,128)(2,1)S(1)}, bf16[128,3584]{1,0:T(8,128)(2,1)}, u32[]{:S(2)}) copy-start(bf16[128,3584]{1,0:T(8,128)(2,1)} %get-tuple-element.22) | copy-start | bytes 2752516
  220.3 7.5 %copy-start.5 = (bf16[4,4,1024]{2,1,0:T(4,128)(2,1)S(1)}, bf16[4,4,1024]{2,1,0:T(4,128)(2,1)}, u32[]{:S(2)}) copy-start(bf16[4,4,1024]{2,1,0:T(4,128)(2,1)} %param.12) | copy-start | bytes 98308
Sparse Core Ops, SparseCore 0:
  25.8 48.2 all-reduce.3
  77.0 76.7 all-reduce.5
  173.6 33.2 reduce-scatter.1

commit v17 on v15

--- a/solution.py
+++ b/solution.py
@@ -121,7 +121,6 @@
     row_all = jnp.sum(lax.all_gather(reduced[local_feat:], "dp", axis=0), axis=0)
     row_all = row_all.reshape(batches, rows)
     row_product = lax.dynamic_slice_in_dim(row_all, start, local_rows, axis=1)
-    hidden, flat_grad, _ = lax.optimization_barrier((hidden, flat_grad, stacked))
     shares = lax.psum_scatter(stacked, "tensor", scatter_dimension=0, tiled=True).astype(
         jnp.float32
     )

time: 215 us -> 227 us (1.056)
  waiting for transfers between devices: 99.8 us -> 114 us
    reduce_scatter x1, waiting for transfers between devices: 1.83 us -> 15.5 us  [per_device(): lax.psum_scatter(stacked, 'tensor', scatter_dimension=0, tiled=True)]
    dot_general x1, matrix products: 1.24 us -> 5.22 us  [per_device(): down_term = jnp.dot(hidden, down_w, preferred_element_type=jnp.float32)]
    dot_general x1, matrix products: 6.03 us -> 2.57 us  [per_device(): lax.dot_general(gate_grad, gate_w, contract_cols, preferred_element_type=...]
    dot_general x1, matrix products: 2.07 us -> 5.34 us  [per_device(): up_part = jnp.dot(flat_normed, up_w, preferred_element_type=jnp.float32)]
    dot_general x1, matrix products: 5.34 us -> 2.07 us  [per_device(): gate_part = jnp.dot(flat_normed, gate_w, preferred_element_type=jnp.float32)]
  transfers between devices with their start and end apart: 3 -> 3, of which waited for: 3 -> 3; matrix products, arithmetic and copies ran while one was open for 10% -> 7% of each run, Pallas kernels for 0% -> 0%
where the time goes in v17:
time: 227 us
  waiting for transfers between devices  114 us (50%)
  blocking collectives  50.9 us (22%)
  matrix products  35.5 us (16%)
  between operations  14 us (6%)
  Pallas kernels  6.05 us (3%)
  local copies, waits for them, and re-layouts  4.75 us (2%)
    psum x1, waiting for transfers between devices, per_device(): gate_sum, up_sum = lax.psum(parts, 'dp')  79.2 us
    psum x1, waiting for transfers between devices, per_device(): back_first = lax.psum(back_part, 'dp')  18.7 us
    reduce_scatter x1, waiting for transfers between devices, per_device(): lax.psum_scatter(stacked, 'tensor', scatter_dimension=0, tiled=True)  15.5 us
    all_gather x1, blocking collectives, per_device(): lax.all_gather(jnp.sum(inputs_all * inputs_all, axis=2), 'dp', axis=0)  12.5 us
    all_gather x1, blocking collectives, per_device(): grad_all = lax.all_gather(d_output, 'tensor', axis=1, tiled=True)  10.8 us
    all_gather x1, blocking collectives, per_device(): lax.all_gather(inputs_all, 'tensor', axis=1, tiled=True).astype(jnp.float32)  9.29 us
    all_gather x1, blocking collectives, per_device(): lax.all_gather(reduced[local_feat:], 'dp', axis=0)  9.19 us
    all_gather x1, blocking collectives, per_device(): lax.all_gather(jnp.concatenate([gain_part, row_all]), 'tensor', axis=0)  9.1 us
  transfers between devices with their start and end apart: 3, of which 3 were waited for; matrix products, arithmetic and copies ran while one was open for 7% of the time, Pallas kernels for 0%

profile of v17, /device:TPU:0, one launch (start us, length us, event | category | flops | bytes accessed | tf_op | source)
XLA Modules:
  0.0 226.9 jit_solution(4523615879249227943)
XLA Ops:
  7.2 0.8 copy.26
  8.0 10.8 %all_gather.24 = bf16[4,32,1024]{2,0,1:T(4,128)(2,1)S(1)} all-gather(bf16[4,4,1024]{2,0,1:T(4,128)(2,1)S(1)} %copy.26), channel_id=1, replica_groups=mesh['dp'=4,'tensor'=8] {'tensor'}, dimensions={1}, use_global_device_ids=true | all-gather | bytes 294912 | tf_op jit(solution)/shard_map/all_gather | solution.py:55
  18.8 0.8 copy.27
  19.6 6.0 %shard_map.126 = bf16[128,3584]{1,0:T(8,128)(2,1)} custom-call(bf16[128,1024]{1,0:T(8,128)(2,1)} %bitcast.70, bf16[3584,1024]{1,0:T(8,128)(2,1)} %weight_ref.1), custom_call_target="tpu_custom_call" | custom-call | flops 939524096 | bytes 8519680 | tf_op jit(solution)/shard_map/pallas_call | solution.py:32
  25.8 9.3 %all_gather.25 = bf16[4,32,1024]{2,0,1:T(4,128)(2,1)S(1)} all-gather(bf16[4,4,1024]{2,0,1:T(4,128)(2,1)S(1)} %copy.28), channel_id=1, replica_groups=mesh['dp'=4,'tensor'=8] {'tensor'}, dimensions={1}, use_global_device_ids=true | all-gather | bytes 294912 | tf_op jit(solution)/shard_map/all_gather | solution.py:62
  35.2 12.5 %all-gather.3 = f32[4,4,32]{2,1,0:T(4,128)S(1)} all-gather(f32[1,4,32]{2,1,0:T(4,128)S(1)} %bitcast.73), channel_id=2, replica_groups=mesh['dp'=4,'tensor'=8] {'dp'}, dimensions={0}, use_global_device_ids=true | all-gather | bytes 2560 | tf_op jit(solution)/shard_map/all_gather | solution.py:64
  47.9 5.3 %convolution_convert_fusion.3 = bf16[128,3584]{1,0:T(8,128)(2,1)} fusion(bf16[128,1024]{1,0:T(8,128)(2,1)S(1)} %bitcast.64, bf16[1024,3584]{1,0:T(8,128)(2,1)} %param.10), kind=kOutput, calls=%fused_computation.3 | convolution fusion | flops 939982848 | bytes 8519680 | tf_op jit(solution)/shard_map/dot_general | solution.py:85
  53.3 2.1 convolution_convert_fusion.4
  55.4 18.7 %all-reduce.4.cloned.1.call-done = bf16[128,3584]{1,0:T(8,128)(2,1)} async-done(((bf16[128,3584]{1,0:T(8,128)(2,1)}), bf16[128,3584]{1,0:T(8,128)(2,1)}) %all-reduce.4.cloned.1.call-update) | async-done | bytes 917520 | tf_op jit(solution)/shard_map/psum | solution.py:60
  74.6 79.2 %all-reduce.6.cloned.1.call-done = (bf16[128,3584]{1,0:T(8,128)(2,1)}, bf16[128,3584]{1,0:T(8,128)(2,1)}) async-done(((bf16[128,3584]{1,0:T(8,128)(2,1)}, bf16[128,3584]{1,0:T(8,128)(2,1)}), (bf16[128,3584]{1,0:T(8,128)(2,1)}, bf16[128,3584]{1,0:T(8,128)(2,1)})) %all-reduce.6.cloned.1.call-update) | async-done | bytes 1835024 | tf_op jit(solution)/shard_map/psum | solution.py:88
  153.8 5.2 %convolution_convert_fusion.5 = bf16[128,1024]{1,0:T(8,128)(2,1)S(1)} fusion(bf16[3584,1024]{1,0:T(8,128)(2,1)} %weight_ref.1, bf16[128,3584]{1,0:T(8,128)(2,1)} %get-tuple-element.17, f32[128]{0:T(128)S(1)} %mul.126, bf16[128,3584]{1,0:T(8,128)(2,1)} %get-tuple-element.18), kind=kOutput, calls=%fused_computation.24 | convolution fusion | flops 943783936 | bytes 9437696 | tf_op jit(solution)/shard_map/dot_general | solution.py:98
  159.1 5.4 %convolution_convert_fusion = bf16[3584,1024]{1,0:T(8,128)(2,1)} fusion(bf16[128,1024]{1,0:T(8,128)(2,1)S(1)} %bitcast.71, bf16[128,3584]{1,0:T(8,128)(2,1)S(1)} %copy-done.5, f32[128]{0:T(128)S(1)} %mul.126, bf16[128,3584]{1,0:T(8,128)(2,1)S(1)} %copy-done.6), kind=kOutput, calls=%fused_computation | convolution fusion | flops 947322880 | bytes 9437696 | tf_op jit(solution)/shard_map/dot_general | solution.py:131
  164.6 2.6 %fusion.29 = f32[128,1024]{1,0:T(8,128)S(1)} fusion(bf16[1024,3584]{1,0:T(8,128)(2,1)S(1)} %bitcast.61, bf16[128,3584]{1,0:T(8,128)(2,1)S(1)} %copy-done.5, bf16[128,3584]{1,0:T(8,128)(2,1)S(1)} %copy-done.4, bf16[128,3584]{1,0:T(8,128)(2,1)S(1)} %copy-done.6, f32[128]{0:T(128)S(1)} %mul.126), kind=kOutput, calls=%fused_computation.56 | convolution fusion | flops 945946624 | bytes 10617344 | tf_op jit(solution)/shard_map/dot_general | solution.py:99
  167.1 5.4 %convolution_convert_fusion.1 = bf16[1024,3584]{1,0:T(8,128)(2,1)} fusion(bf16[128,1024]{1,0:T(8,128)(2,1)S(1)} %bitcast.66, bf16[128,3584]{1,0:T(8,128)(2,1)S(1)} %copy-done.4, f32[128]{0:T(128)S(1)} %mul.126, bf16[128,3584]{1,0:T(8,128)(2,1)S(1)} %copy-done.6), kind=kOutput, calls=%fused_computation.1 | convolution fusion | flops 947322880 | bytes 9437696 | tf_op jit(solution)/shard_map/dot_general | solution.py:137
  172.5 2.6 %fusion.14 = (f32[1024]{0:T(1024)S(1)}, f32[128]{0:T(128)S(1)}, bf16[128,1024]{1,0:T(8,128)(2,1)S(1)}) fusion(f32[4,32,1024]{2,1,0:T(8,128)S(1)} %get-tuple-element.23, f32[4,32,1024]{2,1,0:T(8,128)S(1)} %copy_convert_fusion, f32[1024]{0:T(1024)S(1)} %copy-done.3, f32[128,1024]{1,0:T(8,128)S(1)} %fusion.29, bf16[1024,3584]{1,0:T(8,128)(2,1)S(1)} %bitcast.63, ...), kind=kOutput, calls=%fused_computation.30 | convolution fusion | flops 944569216 | bytes 11019264 | tf_op jit(solution)/shard_map/dot_general | solution.py:101
  175.2 9.1 %all-gather.4 = f32[8,1,1152]{2,1,0:T(1,128)S(1)} all-gather(f32[1,1,1152]{2,1,0:T(1,128)S(1)} %reshape.67), channel_id=3, replica_groups=mesh['dp'=4,'tensor'=8] {'tensor'}, dimensions={0}, use_global_device_ids=true | all-gather | bytes 41472 | tf_op jit(solution)/shard_map/all_gather | solution.py:118
  184.3 0.6 slice.19
  185.4 0.9 reshape.54
  186.4 9.2 %all-gather.5 = f32[4,1,128]{2,1,0:T(1,128)S(1)} all-gather(f32[1,1,128]{2,1,0:T(1,128)S(1)} %slice_bitcast_fusion.2), channel_id=4, replica_groups=mesh['dp'=4,'tensor'=8] {'dp'}, dimensions={0}, use_global_device_ids=true | all-gather | bytes 2560 | tf_op jit(solution)/shard_map/all_gather | solution.py:121
  195.6 0.7 fusion.23
  196.3 6.9 %convolution_convert_fusion.2 = bf16[1024,3584]{1,0:T(8,128)(2,1)} fusion(bf16[128,1024]{1,0:T(8,128)(2,1)S(1)} %bitcast.67, bf16[128,3584]{1,0:T(8,128)(2,1)} %get-tuple-element.17, bf16[128,3584]{1,0:T(8,128)(2,1)S(1)} %copy-done.4, bf16[128,3584]{1,0:T(8,128)(2,1)} %get-tuple-element.18, f32[128]{0:T(128)S(1)} %mul.126), kind=kOutput, calls=%fused_computation.2 | convolution fusion | flops 949616640 | bytes 10355200 | tf_op jit(solution)/shard_map/dot_general | solution.py:134
  203.2 15.5 %reduce-scatter.2.cloned.1.call-done = bf16[4,8,1024]{2,1,0:T(8,128)(2,1)} async-done(((bf16[32,8,1024]{2,1,0:T(8,128)(2,1)}), bf16[4,8,1024]{2,1,0:T(8,128)(2,1)}) %reduce-scatter.2.cloned.1.call-update) | async-done | bytes 65552 | tf_op jit(solution)/shard_map/reduce_scatter | solution.py:124
  218.7 0.9 copy.31
  219.6 0.7 fusion.17
  (54 shorter events, 1.6 us)
Async XLA Ops:
  7.2 66.9 %all-reduce.4.cloned.1.call-start = ((), (), s32[]{:S(2)}) async-start(), calls=%async_computation.1 | async-start | bytes 1835008 | tf_op jit(solution)/shard_map/psum | solution.py:60
  19.6 6.1 %copy-start.1 = (bf16[4,4,1024]{2,1,0:T(4,128)(2,1)S(1)}, bf16[4,4,1024]{2,1,0:T(4,128)(2,1)}, u32[]{:S(2)}) copy-start(bf16[4,4,1024]{2,1,0:T(4,128)(2,1)} %param.7) | copy-start | bytes 98308
  19.6 28.2 %copy-start.3 = (f32[1024]{0:T(1024)S(1)}, f32[1024]{0:T(1024)}, u32[]{:S(2)}) copy-start(f32[1024]{0:T(1024)} %param.8) | copy-start | bytes 12292
  25.7 128.2 %all-reduce.6.cloned.1.call-start = ((), (), s32[]{:S(2)}) async-start(), calls=%async_computation.3 | async-start | bytes 3670016 | tf_op jit(solution)/shard_map/psum | solution.py:88
  47.8 5.5 %slice-start = ((s8[7340032]{0:T(1024)(128)(4,1)}), s8[4194304]{0:T(1024)(128)(4,1)S(1)}, s32[]{:S(2)}) async-start(s8[7340032]{0:T(1024)(128)(4,1)} %bitcast.58), calls=%async_computation.4 | async-start | bytes 8388608
  47.9 5.4 %slice-start.1 = ((s8[7340032]{0:T(1024)(128)(4,1)}), s8[3145728]{0:T(1024)(128)(4,1)S(1)}, s32[]{:S(2)}) async-start(s8[7340032]{0:T(1024)(128)(4,1)} %bitcast.58), calls=%async_computation.5 | async-start | bytes 6291456
  55.4 19.0 %copy-start.7 = (s32[4]{0:T(128)S(1)}, s32[4]{0:T(128)}, u32[]{:S(2)}) copy-start(s32[4]{0:T(128)} %param.13) | copy-start | bytes 52
  74.1 144.6 %reduce-scatter.2.cloned.1.call-start = ((), (), s32[]{:S(2)}) async-start(), calls=%async_computation.2 | async-start | bytes 589824 | tf_op jit(solution)/shard_map/reduce_scatter | solution.py:124
  153.8 5.2 %copy-start = (bf16[4,32,1024]{2,1,0:T(8,128)(2,1)S(1)}, bf16[4,32,1024]{2,1,0:T(8,128)(2,1)}, u32[]{:S(2)}) copy-start(bf16[4,32,1024]{2,1,0:T(8,128)(2,1)} %copy.27) | copy-start | bytes 786436
  153.8 5.2 %copy-start.5 = (bf16[128,3584]{1,0:T(8,128)(2,1)S(1)}, bf16[128,3584]{1,0:T(8,128)(2,1)}, u32[]{:S(2)}) copy-start(bf16[128,3584]{1,0:T(8,128)(2,1)} %get-tuple-element.17) | copy-start | bytes 2752516
  153.8 5.3 %copy-start.6 = (bf16[128,3584]{1,0:T(8,128)(2,1)S(1)}, bf16[128,3584]{1,0:T(8,128)(2,1)}, u32[]{:S(2)}) copy-start(bf16[128,3584]{1,0:T(8,128)(2,1)} %get-tuple-element.18) | copy-start | bytes 2752516
  153.8 10.7 %slice-start.2 = ((s8[7340032]{0:T(1024)(128)(4,1)}), s8[4194304]{0:T(1024)(128)(4,1)S(1)}, s32[]{:S(2)}) async-start(s8[7340032]{0:T(1024)(128)(4,1)} %bitcast.60), calls=%async_computation.6 | async-start | bytes 8388608
  159.1 5.5 %slice-start.3 = ((s8[7340032]{0:T(1024)(128)(4,1)}), s8[3145728]{0:T(1024)(128)(4,1)S(1)}, s32[]{:S(2)}) async-start(s8[7340032]{0:T(1024)(128)(4,1)} %bitcast.60), calls=%async_computation.7 | async-start | bytes 6291456
  159.1 5.4 %copy-start.4 = (bf16[128,3584]{1,0:T(8,128)(2,1)S(1)}, bf16[128,3584]{1,0:T(8,128)(2,1)}, u32[]{:S(2)}) copy-start(bf16[128,3584]{1,0:T(8,128)(2,1)} %all-reduce.4.cloned.1.call-done) | copy-start | bytes 2752516
  159.1 13.4 %slice-start.4 = ((s8[7340032]{0:T(1024)(128)(4,1)}), s8[4194304]{0:T(1024)(128)(4,1)S(1)}, s32[]{:S(2)}) async-start(s8[7340032]{0:T(1024)(128)(4,1)} %bitcast.62), calls=%async_computation.8 | async-start | bytes 8388608
  164.6 8.0 %slice-start.5 = ((s8[7340032]{0:T(1024)(128)(4,1)}), s8[3145728]{0:T(1024)(128)(4,1)S(1)}, s32[]{:S(2)}) async-start(s8[7340032]{0:T(1024)(128)(4,1)} %bitcast.62), calls=%async_computation.9 | async-start | bytes 6291456
  196.3 23.3 %copy-start.2 = (bf16[4,4,1024]{2,1,0:T(4,128)(2,1)S(1)}, bf16[4,4,1024]{2,1,0:T(4,128)(2,1)}, u32[]{:S(2)}) copy-start(bf16[4,4,1024]{2,1,0:T(4,128)(2,1)} %param.12) | copy-start | bytes 98308
Sparse Core Ops, SparseCore 0:
  25.8 48.2 all-reduce.3
  77.0 76.7 all-reduce.5
  186.5 32.2 reduce-scatter.1
